TPU v7x, 32 devices: a whole 2x2x4 slice. The times are simulated.
32 devices in a mesh: group: 8 (over z, x), blk: 4 (over y, core).
Axes of the slice: x: 2, y: 2, z: 4, core: 2. Of those that a mesh axis runs over, the one named last changes fastest.
Arguments:
- sources: bfloat16 [32768, 512], P(('group', 'blk')), may hold values from -20 to 20
- targets: bfloat16 [256, 512], P(('group', 'blk')), may hold values from -20 to 20
- target_potential: bfloat16 [256], P(('group', 'blk')), may hold values from -1.5 to 1.5
- log_source_mass: float32 [32768], P(('group', 'blk')), may hold values from -3 to 0
- log_target_mass: float32 [256], P(('group', 'blk')), may hold values from -3 to 0
Outputs:
- source_potential: float32 [32768], P(('group', 'blk'))
- target_update: float32 [256], P(('group', 'blk'))
All inputs are finite; a program needn't handle non-finite values.
Results may differ from a plain program's by a relative error of at most 0.0003.
Values may be sent and summed in bfloat16 or wider, within the bound.
No kernel may reach another device: no remote copies, remote signals or barrier semaphores. Data moves between devices by JAX's collectives and lax.ppermute only.
A program may use at most 64 MiB of HBM per device.

v0:
```python
import jax
import jax.numpy as jnp
from jax import lax
from jax.sharding import PartitionSpec as P

epsilon = 0.05


def passed_along(block, axis, distance):
    devices = range(lax.axis_size(axis))
    route = [((i - distance) % len(devices), i) for i in devices]
    return lax.ppermute(block, axis, route)


def merged(x, axis, combine):
    everything = jax.tree.map(lambda part: lax.all_gather(part, axis), x)
    first = jax.tree.map(lambda part: part[0], everything)

    def hop(k, so_far):
        return combine(so_far, jax.tree.map(lambda part: part[k], everything))

    return lax.fori_loop(1, lax.axis_size(axis), hop, first)


def scores(source_rows, target_rows, target_pots):
    features = source_rows.shape[1]
    offset = target_pots.astype(jnp.float32) / epsilon - jnp.sum(
        jnp.square(target_rows.astype(jnp.float32)), 1
    ) / (features * epsilon)
    products = lax.dot_general(
        source_rows, target_rows, (((1,), (1,)), ((), ())), preferred_element_type=jnp.float32
    )
    return products * (2.0 / (features * epsilon)) + offset[None, :]


def split_blocks(target_rows, target_pots):
    row_count = target_rows.shape[0]
    block_width = 512 if row_count % 512 == 0 else row_count
    return (
        target_rows.reshape(row_count // block_width, block_width, target_rows.shape[1]),
        target_pots.reshape(row_count // block_width, block_width),
    )


def row_fold(running, source_rows, target_rows, target_pots):

    def advance(state, pieces):
        logits = scores(source_rows, pieces[0], pieces[1])
        run_max, run_sum = state
        new_max = jnp.maximum(run_max, jnp.max(logits, 1))
        new_sum = run_sum * jnp.exp(run_max - new_max) + jnp.sum(
            jnp.exp(logits - new_max[:, None]), 1
        )
        return ((new_max, new_sum), None)

    return lax.scan(advance, running, split_blocks(target_rows, target_pots))[0]


def column_parts(source_rows, source_dual, target_rows, target_pots):

    def single(pieces):
        logits = scores(source_rows, pieces[0], pieces[1])
        logits = logits - pieces[1].astype(jnp.float32)[None, :] / epsilon + source_dual[:, None]
        col_max = jnp.max(logits, 0)
        return (col_max, jnp.sum(jnp.exp(logits - col_max[None, :]), 0))

    col_max, col_sum = lax.map(single, split_blocks(target_rows, target_pots))
    return (col_max.reshape(-1), col_sum.reshape(-1))


def combine(first, second):
    new_max = jnp.maximum(first[0], second[0])
    return (
        new_max,
        first[1] * jnp.exp(first[0] - new_max) + second[1] * jnp.exp(second[0] - new_max),
    )


def per_device(sources, targets, target_potential, log_source_mass, log_target_mass):
    source_count = sources.shape[0]
    target_count = targets.shape[0]
    group_count = lax.axis_size("group")
    cycle_size = lax.axis_size("blk")
    initial = (
        jnp.full((source_count,), -1e30, jnp.float32),
        jnp.zeros((source_count,), jnp.float32),
    )
    gathered = (
        lax.all_gather(targets, "group", axis=0, tiled=True),
        lax.all_gather(target_potential, "group", axis=0, tiled=True),
    )
    own_block = lax.axis_index("blk")
    held = [(own_block, gathered)]
    forward_set = gathered
    backward_set = gathered
    for distance in range(1, cycle_size // 2 + 1):
        forward_set = passed_along((forward_set[0], forward_set[1]), "blk", 1)
        held.append(((own_block - distance) % cycle_size, forward_set))
        if distance <= (cycle_size - 1) // 2:
            backward_set = passed_along((backward_set[0], backward_set[1]), "blk", -1)
            held.append(((own_block + distance) % cycle_size, backward_set))
    running = initial
    for position, pieces in held:
        running = row_fold(running, sources, pieces[0], pieces[1])
    source_dual = log_source_mass - (running[0] + jnp.log(running[1]))
    grid_max = jnp.zeros((group_count, cycle_size, target_count), jnp.float32)
    grid_sum = jnp.zeros((group_count, cycle_size, target_count), jnp.float32)
    for position, pieces in held:
        part_max, part_sum = column_parts(sources, source_dual, pieces[0], pieces[1])
        where_put = (0, position, 0)
        grid_max = lax.dynamic_update_slice(
            grid_max, part_max.reshape(group_count, 1, target_count), where_put
        )
        grid_sum = lax.dynamic_update_slice(
            grid_sum, part_sum.reshape(group_count, 1, target_count), where_put
        )
    col_max = grid_max.reshape(-1)
    col_sum = grid_sum.reshape(-1)
    first_owned = (lax.axis_index("group") * cycle_size + lax.axis_index("blk")) * target_count
    total_max, total_sum = merged((col_max, col_sum), ("group", "blk"), combine)
    owned_max = lax.dynamic_slice_in_dim(total_max, first_owned, target_count)
    owned_sum = lax.dynamic_slice_in_dim(total_sum, first_owned, target_count)
    features = sources.shape[1]
    source_potential = (
        epsilon * source_dual + jnp.sum(jnp.square(sources.astype(jnp.float32)), 1) / features
    )
    target_update = epsilon * (log_target_mass - (owned_max + jnp.log(owned_sum)))
    return (source_potential, target_update)


def solution(mesh):
    return jax.shard_map(
        per_device,
        mesh=mesh,
        in_specs=(
            P(("group", "blk"), None),
            P(("group", "blk"), None),
            P(("group", "blk")),
            P(("group", "blk")),
            P(("group", "blk")),
        ),
        out_specs=(P(("group", "blk")), P(("group", "blk"))),
        check_vma=False,
    )
```

profile of v0, /device:TPU:0, one launch (start us, length us, event | category | flops | bytes accessed | tf_op | source)
XLA Modules:
  0.0 147.5 jit_solution(8099603570743714564)
XLA Ops:
  0.6 0.0 copy-start
  0.6 32.6 %all_gather.12 = bf16[64,512]{1,0:T(8,128)(2,1)S(1)} all-gather(bf16[8,512]{1,0:T(8,128)(2,1)} %param.8), channel_id=1, replica_groups=mesh['group'=8,'blk'=4] {'group'}, dimensions={0}, use_global_device_ids=true | all-gather | bytes 73728 | tf_op jit(solution)/shard_map/all_gather | solution.py:89
  33.3 1.7 %collective-permute-start.2 = (bf16[64,512]{1,0:T(8,128)(2,1)S(1)}, bf16[64,512]{1,0:T(8,128)(2,1)S(1)}, u32[]{:S(2)}, u32[]{:S(2)}) collective-permute-start(bf16[64,512]{1,0:T(8,128)(2,1)S(1)} %all_gather.12), channel_id=1, source_target_pairs={{1,0},{2,1},{3,2},{0,3},{5,4},{6,5},{7,6},{4,7},{9,8},{10,9},{11,1... | collective-permute-start | bytes 196616 | tf_op jit(solution)/shard_map/ppermute | solution.py:12
  35.0 1.2 dynamic-slice.8
  36.9 0.9 dynamic-update-slice
  37.8 21.3 %all-reduce = bf16[64]{0:T(256)(128)(2,1)S(1)} all-reduce(bf16[64]{0:T(256)(128)(2,1)S(1)} %dynamic-update-slice), channel_id=1, replica_groups=mesh['group'=8,'blk'=4] {'group'}, use_global_device_ids=true, to_apply=%add | all-reduce | flops 64 | bytes 256
  59.1 0.0 collective-permute-start.1
  59.1 1.7 %collective-permute-start.3 = (bf16[64]{0:T(256)(128)(2,1)S(1)}, bf16[64]{0:T(256)(128)(2,1)S(1)}, u32[]{:S(2)}, u32[]{:S(2)}) collective-permute-start(bf16[64]{0:T(256)(128)(2,1)S(1)} %all-reduce), channel_id=1, source_target_pairs={{1,0},{2,1},{3,2},{0,3},{5,4},{6,5},{7,6},{4,7},{9,8},{10,9},{11,1... | collective-permute-start | bytes 392 | tf_op jit(solution)/shard_map/ppermute | solution.py:12
  60.9 0.1 multiply_reduce_fusion.4
  61.0 1.7 %fusion.14 = (f32[1024]{0:T(1024)S(1)}, f32[1024,64]{0,1:T(8,128)S(1)}) fusion(f32[64]{0:T(128)S(1)} %get-tuple-element.326, bf16[1024,512]{1,0:T(8,128)(2,1)} %param.7, bf16[64,512]{1,0:T(8,128)(2,1)S(1)} %all_gather.12), kind=kOutput, calls=%fused_computation.51 | convolution fusion | flops 67304448 | bytes 1380608 | tf_op jit(solution)/shard_map/while/body/eval_jaxpr/dot_general | solution.py:30
  62.7 0.3 multiply_reduce_fusion
  63.0 0.0 collective-permute-done.1
  63.0 0.1 collective-permute-start.5
  63.1 1.6 %collective-permute-start.4 = (bf16[64,512]{1,0:T(8,128)(2,1)S(1)}, bf16[64,512]{1,0:T(8,128)(2,1)S(1)}, u32[]{:S(2)}, u32[]{:S(2)}) collective-permute-start(bf16[64,512]{1,0:T(8,128)(2,1)S(1)} %collective-permute-done), channel_id=1, source_target_pairs={{3,0},{0,1},{1,2},{2,3},{7,4},{4,5},{5,6},{6,7},{11,8},{8,9},{9,10... | collective-permute-start | bytes 196616 | tf_op jit(solution)/shard_map/ppermute | solution.py:12
  64.7 0.1 multiply_reduce_fusion.3
  64.8 0.5 fusion.13
  65.3 0.1 multiply_reduce_fusion.2
  65.4 0.0 collective-permute-done.3
  65.5 0.5 fusion.12
  65.9 0.9 collective-permute-done.4
  66.9 0.1 multiply_reduce_fusion.1
  67.0 0.0 collective-permute-done.5
  67.0 0.0 copy-start.1
  67.0 0.5 fusion.11
  67.5 0.1 exponential_reduce_fusion.4
  67.6 0.1 exponential_reduce_fusion.6
  67.7 0.0 copy-done.1
  67.7 0.6 multiply_add_fusion.1
  68.3 0.2 fusion.7
  68.5 0.0 copy-start.2
  68.5 0.3 exponential_reduce_fusion
  68.9 0.3 exponential_reduce_fusion.1
  69.1 0.1 reshape_reshape.29
  69.2 0.1 reshape_reshape.28
  69.3 0.1 reshape_reshape.30
  69.4 0.1 reshape_reshape.31
  69.5 0.1 dynamic_update_slice.45
  69.7 0.1 reshape.118
  69.7 37.9 %all-gather.1 = f32[32,1,256]{2,1,0:T(1,128)S(1)} all-gather(f32[1,1,256]{2,1,0:T(1,128)S(1)} %reshape.118), channel_id=1, replica_groups=mesh['group'=8,'blk'=4] {'group','blk'}, dimensions={0}, use_global_device_ids=true | all-gather | bytes 33792 | tf_op jit(solution)/shard_map/all_gather | solution.py:16
  107.6 0.1 reshape_reshape.25
  107.7 0.1 reshape_reshape.24
  107.8 0.1 reshape_reshape.26
  107.8 0.1 reshape_reshape.27
  107.9 0.1 dynamic_update_slice.41
  108.1 0.1 reshape.116
  108.2 36.8 %all-gather = f32[32,1,256]{2,1,0:T(1,128)S(1)} all-gather(f32[1,1,256]{2,1,0:T(1,128)S(1)} %reshape.116), channel_id=1, replica_groups=mesh['group'=8,'blk'=4] {'group','blk'}, dimensions={0}, use_global_device_ids=true | all-gather | bytes 33792 | tf_op jit(solution)/shard_map/all_gather | solution.py:16
  145.1 1.8 %while.11 = (s32[]{:T(128)}, f32[256]{0:T(256)S(1)}, f32[256]{0:T(256)S(1)}, f32[32,256]{1,0:T(8,128)S(1)}, f32[32,256]{1,0:T(8,128)S(1)}, /*index=5*/s32[]{:T(128)}, s32[]{:T(128)}, s32[]{:T(128)}) while((s32[]{:T(128)}, f32[256]{0:T(256)S(1)}, f32[256]{0:T(256)S(1)}, f32[32,256]{1,0:T(8,128)S(1)}, f32[32,256]{1,0:T(8,128)S(1)}, ...), condition=%wide.region_22.23_spmd, body=%wide.region_21.22_spmd.sunk | while | flops 1541 | bytes 10371 | solution.py:22
  146.9 0.6 subtract_multiply_fusion
  (85 shorter events, 1.3 us)
Async XLA Ops:
  0.6 62.0 %copy-start = (bf16[1024,512]{1,0:T(8,128)(2,1)S(1)}, bf16[1024,512]{1,0:T(8,128)(2,1)}, u32[]{:S(2)}) copy-start(bf16[1024,512]{1,0:T(8,128)(2,1)} %param.7) | copy-start | bytes 3145732
  33.3 29.8 %collective-permute-start = (bf16[64,512]{1,0:T(8,128)(2,1)S(1)}, bf16[64,512]{1,0:T(8,128)(2,1)S(1)}, u32[]{:S(2)}, u32[]{:S(2)}) collective-permute-start(bf16[64,512]{1,0:T(8,128)(2,1)S(1)} %all_gather.12), channel_id=1, source_target_pairs={{3,0},{0,1},{1,2},{2,3},{7,4},{4,5},{5,6},{6,7},{11,8},{8,9},{9,10... | collective-permute-start | bytes 196616 | tf_op jit(solution)/shard_map/ppermute | solution.py:12
  33.3 32.0 %collective-permute-start.2 = (bf16[64,512]{1,0:T(8,128)(2,1)S(1)}, bf16[64,512]{1,0:T(8,128)(2,1)S(1)}, u32[]{:S(2)}, u32[]{:S(2)}) collective-permute-start(bf16[64,512]{1,0:T(8,128)(2,1)S(1)} %all_gather.12), channel_id=1, source_target_pairs={{1,0},{2,1},{3,2},{0,3},{5,4},{6,5},{7,6},{4,7},{9,8},{10,9},{11,1... | collective-permute-start | bytes 196616 | tf_op jit(solution)/shard_map/ppermute | solution.py:12
  59.1 3.9 %collective-permute-start.1 = (bf16[64]{0:T(256)(128)(2,1)S(1)}, bf16[64]{0:T(256)(128)(2,1)S(1)}, u32[]{:S(2)}, u32[]{:S(2)}) collective-permute-start(bf16[64]{0:T(256)(128)(2,1)S(1)} %all-reduce), channel_id=1, source_target_pairs={{3,0},{0,1},{1,2},{2,3},{7,4},{4,5},{5,6},{6,7},{11,8},{8,9},{9,10... | collective-permute-start | bytes 392 | tf_op jit(solution)/shard_map/ppermute | solution.py:12
  59.1 6.3 %collective-permute-start.3 = (bf16[64]{0:T(256)(128)(2,1)S(1)}, bf16[64]{0:T(256)(128)(2,1)S(1)}, u32[]{:S(2)}, u32[]{:S(2)}) collective-permute-start(bf16[64]{0:T(256)(128)(2,1)S(1)} %all-reduce), channel_id=1, source_target_pairs={{1,0},{2,1},{3,2},{0,3},{5,4},{6,5},{7,6},{4,7},{9,8},{10,9},{11,1... | collective-permute-start | bytes 392 | tf_op jit(solution)/shard_map/ppermute | solution.py:12
  63.0 3.9 %collective-permute-start.5 = (bf16[64]{0:T(256)(128)(2,1)S(1)}, bf16[64]{0:T(256)(128)(2,1)S(1)}, u32[]{:S(2)}, u32[]{:S(2)}) collective-permute-start(bf16[64]{0:T(256)(128)(2,1)S(1)} %collective-permute-done.1), channel_id=1, source_target_pairs={{3,0},{0,1},{1,2},{2,3},{7,4},{4,5},{5,6},{6,7},{11,8},{8,9},{9,10... | collective-permute-start | bytes 392 | tf_op jit(solution)/shard_map/ppermute | solution.py:12
  63.1 3.7 %collective-permute-start.4 = (bf16[64,512]{1,0:T(8,128)(2,1)S(1)}, bf16[64,512]{1,0:T(8,128)(2,1)S(1)}, u32[]{:S(2)}, u32[]{:S(2)}) collective-permute-start(bf16[64,512]{1,0:T(8,128)(2,1)S(1)} %collective-permute-done), channel_id=1, source_target_pairs={{3,0},{0,1},{1,2},{2,3},{7,4},{4,5},{5,6},{6,7},{11,8},{8,9},{9,10... | collective-permute-start | bytes 196616 | tf_op jit(solution)/shard_map/ppermute | solution.py:12
  67.0 0.7 copy-start.1
  68.5 78.3 %copy-start.2 = (f32[8]{0:T(128)S(1)}, f32[8]{0:T(128)}, u32[]{:S(2)}) copy-start(f32[8]{0:T(128)} %param.11) | copy-start | bytes 100
where the time goes:
time: 148 us; the launch traced here: 147 us
  blocking collectives  129 us (87%)
  starting transfers between devices  5.19 us (4%)
  local copies, waits for them, and re-layouts  3.66 us (2%)
  other arithmetic  3.62 us (2%)
  matrix products  3.04 us (2%)
  between operations  1.56 us (1%)
    all_gather x2, blocking collectives, merged(): everything = jax.tree.map(lambda part: lax.all_gather(part, axis), x)  74.7 us
    all_gather x1, blocking collectives, per_device(): lax.all_gather(targets, 'group', axis=0, tiled=True)  32.6 us
    unnamed x1, blocking collectives  21.3 us
    ppermute x6, starting transfers between devices, passed_along(): return lax.ppermute(block, axis, route)  5.19 us
    dot_general x4, matrix products, scores(): lax.dot_general(source_rows, target_rows, (((1,), (1,)), ((), ())), prefe...  3.04 us
  transfers between devices with their start and end apart: 6, of which 1 were waited for; matrix products, arithmetic and copies ran while one was open for 4% of the time, Pallas kernels for 0%

commit v1 on v0

v1 whole, which is shorter than its diff:
```python
import jax
import jax.numpy as jnp
from jax import lax
from jax.sharding import PartitionSpec as P

epsilon = 0.05
AXES = ("group", "blk")


def exchange(x, bit, count):
    route = [(i, i ^ (1 << bit)) for i in range(count)]
    return lax.ppermute(x, AXES, route)


def combine(first, second):
    new_max = jnp.maximum(first[0], second[0])
    new_sum = first[1] * jnp.exp(first[0] - new_max) + second[1] * jnp.exp(second[0] - new_max)
    return jnp.stack([new_max, new_sum])


def per_device(sources, targets, target_potential, log_source_mass, log_target_mass):
    count = lax.axis_size("group") * lax.axis_size("blk")
    levels = count.bit_length() - 1
    if (1 << levels) != count:
        raise ValueError("count not pow2")
    order = list(reversed(range(levels)))
    features = sources.shape[1]
    factor = 2.0 / (features * epsilon)

    held_rows, held_pots = targets, target_potential
    for bit in order:
        other_rows, other_pots = exchange((held_rows, held_pots), bit, count)
        held_rows = jnp.concatenate([held_rows, other_rows], 0)
        held_pots = jnp.concatenate([held_pots, other_pots], 0)

    pot_f32 = held_pots.astype(jnp.float32)
    offset = pot_f32 / epsilon - jnp.sum(jnp.square(held_rows.astype(jnp.float32)), 1) / (
        features * epsilon
    )
    products = lax.dot_general(
        sources, held_rows, (((1,), (1,)), ((), ())), preferred_element_type=jnp.float32
    )
    logits = products * factor + offset[None, :]
    row_max = jnp.max(logits, 1)
    row_lse = row_max + jnp.log(jnp.sum(jnp.exp(logits - row_max[:, None]), 1))
    source_dual = log_source_mass - row_lse
    columns = logits - pot_f32[None, :] / epsilon + source_dual[:, None]
    col_max = jnp.max(columns, 0)
    col_sum = jnp.sum(jnp.exp(columns - col_max[None, :]), 0)

    part = jnp.stack([col_max, col_sum])
    for bit in reversed(order):
        half = part.shape[1] // 2
        arrived = exchange(part[:, half:], bit, count)
        part = combine(part[:, :half], arrived)

    source_potential = epsilon * source_dual + jnp.sum(
        jnp.square(sources.astype(jnp.float32)), 1
    ) / features
    target_update = epsilon * (log_target_mass - (part[0] + jnp.log(part[1])))
    return (source_potential, target_update)


def solution(mesh):
    return jax.shard_map(
        per_device,
        mesh=mesh,
        in_specs=(
            P(AXES, None),
            P(AXES, None),
            P(AXES),
            P(AXES),
            P(AXES),
        ),
        out_specs=(P(AXES), P(AXES)),
        check_vma=False,
    )
```

time: 148 us -> 57.2 us (0.39)
  blocking collectives: 129 us -> 0 us
  waiting for transfers between devices: 0.95 us -> 22.4 us
  starting transfers between devices: 5.19 us -> 22.7 us
  other arithmetic: 3.62 us -> 8 us
  matrix products: 3.04 us -> 0.48 us
    all_gather x3 -> x0, blocking collectives: 107 us -> none  [the longest x2 74.7 us: merged(): everything = jax.tree.map(lambda part: lax.all_gather(part, axis), x)]
    ppermute x6 -> x15, waiting for transfers between devices: 0.95 us -> 22.4 us  [exchange(): return lax.ppermute(x, AXES, route)]
    unnamed x1 -> x0, blocking collectives: 21.3 us -> none
    ppermute x6 -> x15, starting transfers between devices: 5.19 us -> 22.7 us  [exchange(): return lax.ppermute(x, AXES, route)]
    concatenate x0 -> x6, other arithmetic: none -> 4.3 us  [the longest x3 2.19 us: per_device(): held_pots = jnp.concatenate([held_pots, other_pots], 0)]
    dot_general x4 -> x1, matrix products: 3.04 us -> 0.48 us  [per_device(): lax.dot_general(sources, held_rows, (((1,), (1,)), ((), ())), preferred_e...]
  transfers between devices with their start and end apart: 6 -> 15, of which waited for: 1 -> 11; matrix products, arithmetic and copies ran while one was open for 4% -> 10% of each run, Pallas kernels for 0% -> 0%
where the time goes in v1:
time: 57.2 us; the launch traced here: 56.8 us
  starting transfers between devices  22.7 us (40%)
  waiting for transfers between devices  22.4 us (39%)
  other arithmetic  8 us (14%)
  local copies, waits for them, and re-layouts  2.4 us (4%)
  between operations  0.77 us (1%)
    ppermute x15, starting transfers between devices, exchange(): return lax.ppermute(x, AXES, route)  22.7 us
    ppermute x15, waiting for transfers between devices, exchange(): return lax.ppermute(x, AXES, route)  22.4 us
    concatenate x3, other arithmetic, per_device(): held_pots = jnp.concatenate([held_pots, other_pots], 0)  2.19 us
    concatenate x3, other arithmetic, per_device(): held_rows = jnp.concatenate([held_rows, other_rows], 0)  2.1 us
    reduce_sum x1, other arithmetic, per_device(): jnp.sum(jnp.square(sources.astype(jnp.float32)), 1) / features  1.5 us
    unnamed x12, local copies, waits for them, and re-layouts  1.23 us
  transfers between devices with their start and end apart: 15, of which 11 were waited for; matrix products, arithmetic and copies ran while one was open for 10% of the time, Pallas kernels for 0%

profile of v1, /device:TPU:0, one launch (start us, length us, event | category | flops | bytes accessed | tf_op | source)
XLA Modules:
  0.0 56.8 jit_solution(664141412395459808)
XLA Ops:
  0.6 0.0 copy-start.1
  0.6 4.1 %collective-permute-start.5 = (bf16[8]{0:T(256)(128)(2,1)}, bf16[8]{0:T(256)(128)(2,1)S(1)}, u32[]{:S(2)}, u32[]{:S(2)}) collective-permute-start(bf16[8]{0:T(256)(128)(2,1)} %param.7), channel_id=1, source_target_pairs={{0,16},{1,17},{2,18},{3,19},{4,20},{5,21},{6,22},{7,23},{8,24},{9,... | collective-permute-start | bytes 56 | tf_op jit(solution)/shard_map/ppermute | solution.py:12
  4.7 1.7 %collective-permute-done.5 = bf16[8]{0:T(256)(128)(2,1)S(1)} collective-permute-done((bf16[8]{0:T(256)(128)(2,1)}, bf16[8]{0:T(256)(128)(2,1)S(1)}, u32[]{:S(2)}, u32[]{:S(2)}) %collective-permute-start.5) | collective-permute-done | bytes 48 | tf_op jit(solution)/shard_map/ppermute | solution.py:12
  6.4 0.7 %pad_maximum_fusion.8 = bf16[16]{0:T(256)(128)(2,1)S(1)} fusion(bf16[8]{0:T(256)(128)(2,1)S(1)} %collective-permute-done.5, bf16[8]{0:T(256)(128)(2,1)} %param.7), kind=kLoop, calls=%fused_computation.33 | loop fusion | flops 64 | bytes 64 | tf_op jit(solution)/shard_map/concatenate | solution.py:34
  7.1 1.9 %collective-permute-start.6 = (bf16[16]{0:T(256)(128)(2,1)S(1)}, bf16[16]{0:T(256)(128)(2,1)S(1)}, u32[]{:S(2)}, u32[]{:S(2)}) collective-permute-start(bf16[16]{0:T(256)(128)(2,1)S(1)} %pad_maximum_fusion.8), channel_id=1, source_target_pairs={{0,8},{1,9},{2,10},{3,11},{4,12},{5,13},{6,14},{7,15},{8,0},{9,1},... | collective-permute-start | bytes 104 | tf_op jit(solution)/shard_map/ppermute | solution.py:12
  9.0 1.6 %collective-permute-done.6 = bf16[16]{0:T(256)(128)(2,1)S(1)} collective-permute-done((bf16[16]{0:T(256)(128)(2,1)S(1)}, bf16[16]{0:T(256)(128)(2,1)S(1)}, u32[]{:S(2)}, u32[]{:S(2)}) %collective-permute-start.6) | collective-permute-done | bytes 64 | tf_op jit(solution)/shard_map/ppermute | solution.py:12
  10.7 0.7 %pad_maximum_fusion.9 = bf16[32]{0:T(256)(128)(2,1)S(1)} fusion(bf16[16]{0:T(256)(128)(2,1)S(1)} %collective-permute-done.6, bf16[8]{0:T(256)(128)(2,1)S(1)} %collective-permute-done.5, bf16[8]{0:T(256)(128)(2,1)} %param.7), kind=kLoop, calls=%fused_computation.34 | loop fusion | flops 192 | bytes 128 | tf_op jit(solution)/shard_map/concatenate | solution.py:34
  11.4 1.8 %collective-permute-start.7 = (bf16[32]{0:T(256)(128)(2,1)S(1)}, bf16[32]{0:T(256)(128)(2,1)S(1)}, u32[]{:S(2)}, u32[]{:S(2)}) collective-permute-start(bf16[32]{0:T(256)(128)(2,1)S(1)} %pad_maximum_fusion.9), channel_id=1, source_target_pairs={{0,4},{1,5},{2,6},{3,7},{4,0},{5,1},{6,2},{7,3},{8,12},{9,13},{10,... | collective-permute-start | bytes 200 | tf_op jit(solution)/shard_map/ppermute | solution.py:12
  13.2 2.6 %collective-permute-start = (bf16[8,512]{1,0:T(8,128)(2,1)}, bf16[8,512]{1,0:T(8,128)(2,1)S(1)}, u32[]{:S(2)}, u32[]{:S(2)}) collective-permute-start(bf16[8,512]{1,0:T(8,128)(2,1)} %param.6), channel_id=1, source_target_pairs={{0,16},{1,17},{2,18},{3,19},{4,20},{5,21},{6,22},{7,23},{8,24},{9,... | collective-permute-start | bytes 24584 | tf_op jit(solution)/shard_map/ppermute | solution.py:12
  15.8 0.7 %pad_maximum_fusion.10 = bf16[64]{0:T(256)(128)(2,1)S(1)} fusion(bf16[32]{0:T(256)(128)(2,1)S(1)} %collective-permute-done.7, bf16[16]{0:T(256)(128)(2,1)S(1)} %collective-permute-done.6, bf16[8]{0:T(256)(128)(2,1)S(1)} %collective-permute-done.5, bf16[8]{0:T(256)(128)(2,1)} %param.7), kind=kLoop, calls=%fused_computation.35 | loop fusion | flops 512 | bytes 256 | tf_op jit(solution)/shard_map/concatenate | solution.py:34
  16.5 1.5 %collective-permute-start.8 = (bf16[64]{0:T(256)(128)(2,1)S(1)}, bf16[64]{0:T(256)(128)(2,1)S(1)}, u32[]{:S(2)}, u32[]{:S(2)}) collective-permute-start(bf16[64]{0:T(256)(128)(2,1)S(1)} %pad_maximum_fusion.10), channel_id=1, source_target_pairs={{0,2},{1,3},{2,0},{3,1},{4,6},{5,7},{6,4},{7,5},{8,10},{9,11},{10,... | collective-permute-start | bytes 392 | tf_op jit(solution)/shard_map/ppermute | solution.py:12
  18.1 0.7 %constant_dynamic-update-slice_fusion.4 = (bf16[128,512]{1,0:T(8,128)(2,1)S(1)}, bf16[256,512]{1,0:T(8,128)(2,1)S(1)}) fusion(bf16[8,512]{1,0:T(8,128)(2,1)} %param.6), kind=kLoop, calls=%fused_computation.14 | loop fusion | bytes 24576
  18.8 1.3 %collective-permute-done.8 = bf16[64]{0:T(256)(128)(2,1)S(1)} collective-permute-done((bf16[64]{0:T(256)(128)(2,1)S(1)}, bf16[64]{0:T(256)(128)(2,1)S(1)}, u32[]{:S(2)}, u32[]{:S(2)}) %collective-permute-start.8) | collective-permute-done | bytes 160 | tf_op jit(solution)/shard_map/ppermute | solution.py:12
  20.1 0.8 %concatenate.53 = bf16[128]{0:T(256)(128)(2,1)S(1)} concatenate(bf16[8]{0:T(256)(128)(2,1)} %param.7, bf16[8]{0:T(256)(128)(2,1)S(1)} %collective-permute-done.5, bf16[16]{0:T(256)(128)(2,1)S(1)} %collective-permute-done.6, bf16[32]{0:T(256)(128)(2,1)S(1)} %collective-permute-done.7, bf16[64]{0:T(256)(128)(2,1)S(1)} %collective-permute-done.8), dimensions={0} | concatenate | bytes 512 | tf_op jit(solution)/shard_map/concatenate | solution.py:34
  20.9 0.7 %pad_maximum_fusion.2 = bf16[16,512]{1,0:T(8,128)(2,1)S(1)} fusion(bf16[8,512]{1,0:T(8,128)(2,1)S(1)} %collective-permute-done, bf16[8,512]{1,0:T(8,128)(2,1)} %param.6), kind=kLoop, calls=%fused_computation.21 | loop fusion | flops 32768 | bytes 32768 | tf_op jit(solution)/shard_map/concatenate | solution.py:33
  21.6 1.6 %collective-permute-start.1 = (bf16[16,512]{1,0:T(8,128)(2,1)S(1)}, bf16[16,512]{1,0:T(8,128)(2,1)S(1)}, u32[]{:S(2)}, u32[]{:S(2)}) collective-permute-start(bf16[16,512]{1,0:T(8,128)(2,1)S(1)} %pad_maximum_fusion.2), channel_id=1, source_target_pairs={{0,8},{1,9},{2,10},{3,11},{4,12},{5,13},{6,14},{7,15},{8,0},{9,1},... | collective-permute-start | bytes 49160 | tf_op jit(solution)/shard_map/ppermute | solution.py:12
  23.1 2.2 %collective-permute-done.1 = bf16[16,512]{1,0:T(8,128)(2,1)S(1)} collective-permute-done((bf16[16,512]{1,0:T(8,128)(2,1)S(1)}, bf16[16,512]{1,0:T(8,128)(2,1)S(1)}, u32[]{:S(2)}, u32[]{:S(2)}) %collective-permute-start.1) | collective-permute-done | bytes 16416 | tf_op jit(solution)/shard_map/ppermute | solution.py:12
  25.3 0.7 %pad_maximum_fusion.1 = bf16[32,512]{1,0:T(8,128)(2,1)S(1)} fusion(bf16[16,512]{1,0:T(8,128)(2,1)S(1)} %collective-permute-done.1, bf16[8,512]{1,0:T(8,128)(2,1)S(1)} %collective-permute-done, bf16[8,512]{1,0:T(8,128)(2,1)} %param.6), kind=kLoop, calls=%fused_computation.9 | loop fusion | flops 98304 | bytes 65536 | tf_op jit(solution)/shard_map/concatenate | solution.py:33
  26.0 0.9 %collective-permute-start.2 = (bf16[32,512]{1,0:T(8,128)(2,1)S(1)}, bf16[32,512]{1,0:T(8,128)(2,1)S(1)}, u32[]{:S(2)}, u32[]{:S(2)}) collective-permute-start(bf16[32,512]{1,0:T(8,128)(2,1)S(1)} %pad_maximum_fusion.1), channel_id=1, source_target_pairs={{0,4},{1,5},{2,6},{3,7},{4,0},{5,1},{6,2},{7,3},{8,12},{9,13},{10,... | collective-permute-start | bytes 98312 | tf_op jit(solution)/shard_map/ppermute | solution.py:12
  27.0 3.0 %collective-permute-done.2 = bf16[32,512]{1,0:T(8,128)(2,1)S(1)} collective-permute-done((bf16[32,512]{1,0:T(8,128)(2,1)S(1)}, bf16[32,512]{1,0:T(8,128)(2,1)S(1)}, u32[]{:S(2)}, u32[]{:S(2)}) %collective-permute-start.2) | collective-permute-done | bytes 32800 | tf_op jit(solution)/shard_map/ppermute | solution.py:12
  29.9 0.7 %pad_maximum_fusion = bf16[64,512]{1,0:T(8,128)(2,1)S(1)} fusion(bf16[32,512]{1,0:T(8,128)(2,1)S(1)} %collective-permute-done.2, bf16[16,512]{1,0:T(8,128)(2,1)S(1)} %collective-permute-done.1, bf16[8,512]{1,0:T(8,128)(2,1)S(1)} %collective-permute-done, bf16[8,512]{1,0:T(8,128)(2,1)} %param.6), kind=kLoop, calls=%fused_computation.8 | loop fusion | flops 262144 | bytes 131072 | tf_op jit(solution)/shard_map/concatenate | solution.py:33
  30.6 1.5 %collective-permute-start.3 = (bf16[64,512]{1,0:T(8,128)(2,1)S(1)}, bf16[64,512]{1,0:T(8,128)(2,1)S(1)}, u32[]{:S(2)}, u32[]{:S(2)}) collective-permute-start(bf16[64,512]{1,0:T(8,128)(2,1)S(1)} %pad_maximum_fusion), channel_id=1, source_target_pairs={{0,2},{1,3},{2,0},{3,1},{4,6},{5,7},{6,4},{7,5},{8,10},{9,11},{10,... | collective-permute-start | bytes 196616 | tf_op jit(solution)/shard_map/ppermute | solution.py:12
  32.2 2.7 %collective-permute-done.3 = bf16[64,512]{1,0:T(8,128)(2,1)S(1)} collective-permute-done((bf16[64,512]{1,0:T(8,128)(2,1)S(1)}, bf16[64,512]{1,0:T(8,128)(2,1)S(1)}, u32[]{:S(2)}, u32[]{:S(2)}) %collective-permute-start.3) | collective-permute-done | bytes 65568 | tf_op jit(solution)/shard_map/ppermute | solution.py:12
  34.9 0.1 collective-permute-start.4
  35.0 1.5 %multiply_reduce_fusion = f32[1024]{0:T(1024)S(1)} fusion(bf16[1024,512]{1,0:T(8,128)(2,1)} %param.5), kind=kLoop, calls=%fused_computation | loop fusion | flops 1571840 | bytes 1052672 | tf_op jit(solution)/shard_map/reduce_sum | solution.py:57
  36.5 0.1 concatenate.54
  36.6 0.1 multiply_reduce_fusion.1
  36.8 0.5 fusion.9
  37.3 0.2 exponential_reduce_fusion.1
  37.5 0.5 copy-done.2
  38.0 0.6 %multiply_add_fusion = (f32[1024]{0:T(1024)}, f32[1024]{0:T(1024)S(1)}) fusion(f32[1024]{0:T(1024)S(1)} %multiply_reduce_fusion, f32[1024]{0:T(1024)S(1)} %copy-done.2, f32[1024]{0:T(1024)S(1)} %get-tuple-element.24, f32[1024]{0:T(1024)S(1)} %exponential_reduce_fusion.1), kind=kLoop, calls=%fused_computation.22 | loop fusion | flops 5120 | bytes 24576 | tf_op jit(solution)/shard_map/add | solution.py:57
  38.6 0.3 fusion.1
  38.8 0.4 exponential_reduce_fusion
  39.2 0.6 collective-permute-start.10
  39.8 0.8 %collective-permute-done.10 = f32[2,128]{1,0:T(2,128)S(1)} collective-permute-done((f32[2,128]{1,0:T(2,128)S(1)}, f32[2,128]{1,0:T(2,128)S(1)}, u32[]{:S(2)}, u32[]{:S(2)}) %collective-permute-start.10) | collective-permute-done | bytes 1056 | tf_op jit(solution)/shard_map/ppermute | solution.py:12
  40.6 0.1 slice.116
  40.7 1.5 %collective-permute-start.11 = (f32[2,64]{1,0:T(2,128)S(1)}, f32[2,64]{1,0:T(2,128)S(1)}, u32[]{:S(2)}, u32[]{:S(2)}) collective-permute-start(f32[2,64]{1,0:T(2,128)S(1)} %slice.116), channel_id=1, source_target_pairs={{0,2},{1,3},{2,0},{3,1},{4,6},{5,7},{6,4},{7,5},{8,10},{9,11},{10,... | collective-permute-start | bytes 1544 | tf_op jit(solution)/shard_map/ppermute | solution.py:12
  42.2 2.0 %collective-permute-done.11 = f32[2,64]{1,0:T(2,128)S(1)} collective-permute-done((f32[2,64]{1,0:T(2,128)S(1)}, f32[2,64]{1,0:T(2,128)S(1)}, u32[]{:S(2)}, u32[]{:S(2)}) %collective-permute-start.11) | collective-permute-done | bytes 544 | tf_op jit(solution)/shard_map/ppermute | solution.py:12
  44.3 0.1 slice.121
  44.4 1.0 %collective-permute-start.12 = (f32[2,32]{1,0:T(2,128)S(1)}, f32[2,32]{1,0:T(2,128)S(1)}, u32[]{:S(2)}, u32[]{:S(2)}) collective-permute-start(f32[2,32]{1,0:T(2,128)S(1)} %slice.121), channel_id=1, source_target_pairs={{0,4},{1,5},{2,6},{3,7},{4,0},{5,1},{6,2},{7,3},{8,12},{9,13},{10,... | collective-permute-start | bytes 776 | tf_op jit(solution)/shard_map/ppermute | solution.py:12
  45.4 2.6 %collective-permute-done.12 = f32[2,32]{1,0:T(2,128)S(1)} collective-permute-done((f32[2,32]{1,0:T(2,128)S(1)}, f32[2,32]{1,0:T(2,128)S(1)}, u32[]{:S(2)}, u32[]{:S(2)}) %collective-permute-start.12) | collective-permute-done | bytes 288 | tf_op jit(solution)/shard_map/ppermute | solution.py:12
  48.0 0.1 slice.126
  48.1 1.6 %collective-permute-start.13 = (f32[2,16]{1,0:T(2,128)S(1)}, f32[2,16]{1,0:T(2,128)S(1)}, u32[]{:S(2)}, u32[]{:S(2)}) collective-permute-start(f32[2,16]{1,0:T(2,128)S(1)} %slice.126), channel_id=1, source_target_pairs={{0,8},{1,9},{2,10},{3,11},{4,12},{5,13},{6,14},{7,15},{8,0},{9,1},... | collective-permute-start | bytes 392 | tf_op jit(solution)/shard_map/ppermute | solution.py:12
  49.7 2.0 %collective-permute-done.13 = f32[2,16]{1,0:T(2,128)S(1)} collective-permute-done((f32[2,16]{1,0:T(2,128)S(1)}, f32[2,16]{1,0:T(2,128)S(1)}, u32[]{:S(2)}, u32[]{:S(2)}) %collective-permute-start.13) | collective-permute-done | bytes 160 | tf_op jit(solution)/shard_map/ppermute | solution.py:12
  51.7 0.1 slice.131
  51.7 2.1 %collective-permute-start.14 = (f32[2,8]{1,0:T(2,128)S(1)}, f32[2,8]{1,0:T(2,128)S(1)}, u32[]{:S(2)}, u32[]{:S(2)}) collective-permute-start(f32[2,8]{1,0:T(2,128)S(1)} %slice.131), channel_id=1, source_target_pairs={{0,16},{1,17},{2,18},{3,19},{4,20},{5,21},{6,22},{7,23},{8,24},{9,... | collective-permute-start | bytes 200 | tf_op jit(solution)/shard_map/ppermute | solution.py:12
  53.8 2.4 %collective-permute-done.14 = f32[2,8]{1,0:T(2,128)S(1)} collective-permute-done((f32[2,8]{1,0:T(2,128)S(1)}, f32[2,8]{1,0:T(2,128)S(1)}, u32[]{:S(2)}, u32[]{:S(2)}) %collective-permute-start.14) | collective-permute-done | bytes 96 | tf_op jit(solution)/shard_map/ppermute | solution.py:12
  56.2 0.5 subtract_multiply_fusion
  (26 shorter events, 0.2 us)
Async XLA Ops:
  0.6 35.9 %copy-start.1 = (bf16[8]{0:T(256)(128)(2,1)S(1)}, bf16[8]{0:T(256)(128)(2,1)}, u32[]{:S(2)}) copy-start(bf16[8]{0:T(256)(128)(2,1)} %param.7) | copy-start | bytes 52
  0.6 5.8 %collective-permute-start.5 = (bf16[8]{0:T(256)(128)(2,1)}, bf16[8]{0:T(256)(128)(2,1)S(1)}, u32[]{:S(2)}, u32[]{:S(2)}) collective-permute-start(bf16[8]{0:T(256)(128)(2,1)} %param.7), channel_id=1, source_target_pairs={{0,16},{1,17},{2,18},{3,19},{4,20},{5,21},{6,22},{7,23},{8,24},{9,... | collective-permute-start | bytes 56 | tf_op jit(solution)/shard_map/ppermute | solution.py:12
  7.1 3.5 %collective-permute-start.6 = (bf16[16]{0:T(256)(128)(2,1)S(1)}, bf16[16]{0:T(256)(128)(2,1)S(1)}, u32[]{:S(2)}, u32[]{:S(2)}) collective-permute-start(bf16[16]{0:T(256)(128)(2,1)S(1)} %pad_maximum_fusion.8), channel_id=1, source_target_pairs={{0,8},{1,9},{2,10},{3,11},{4,12},{5,13},{6,14},{7,15},{8,0},{9,1},... | collective-permute-start | bytes 104 | tf_op jit(solution)/shard_map/ppermute | solution.py:12
  11.4 4.4 %collective-permute-start.7 = (bf16[32]{0:T(256)(128)(2,1)S(1)}, bf16[32]{0:T(256)(128)(2,1)S(1)}, u32[]{:S(2)}, u32[]{:S(2)}) collective-permute-start(bf16[32]{0:T(256)(128)(2,1)S(1)} %pad_maximum_fusion.9), channel_id=1, source_target_pairs={{0,4},{1,5},{2,6},{3,7},{4,0},{5,1},{6,2},{7,3},{8,12},{9,13},{10,... | collective-permute-start | bytes 200 | tf_op jit(solution)/shard_map/ppermute | solution.py:12
  13.2 7.6 %collective-permute-start = (bf16[8,512]{1,0:T(8,128)(2,1)}, bf16[8,512]{1,0:T(8,128)(2,1)S(1)}, u32[]{:S(2)}, u32[]{:S(2)}) collective-permute-start(bf16[8,512]{1,0:T(8,128)(2,1)} %param.6), channel_id=1, source_target_pairs={{0,16},{1,17},{2,18},{3,19},{4,20},{5,21},{6,22},{7,23},{8,24},{9,... | collective-permute-start | bytes 24584 | tf_op jit(solution)/shard_map/ppermute | solution.py:12
  16.5 3.5 %collective-permute-start.8 = (bf16[64]{0:T(256)(128)(2,1)S(1)}, bf16[64]{0:T(256)(128)(2,1)S(1)}, u32[]{:S(2)}, u32[]{:S(2)}) collective-permute-start(bf16[64]{0:T(256)(128)(2,1)S(1)} %pad_maximum_fusion.10), channel_id=1, source_target_pairs={{0,2},{1,3},{2,0},{3,1},{4,6},{5,7},{6,4},{7,5},{8,10},{9,11},{10,... | collective-permute-start | bytes 392 | tf_op jit(solution)/shard_map/ppermute | solution.py:12
  20.9 15.6 %collective-permute-start.9 = (bf16[128]{0:T(256)(128)(2,1)S(1)}, bf16[128]{0:T(256)(128)(2,1)S(1)}, u32[]{:S(2)}, u32[]{:S(2)}) collective-permute-start(bf16[128]{0:T(256)(128)(2,1)S(1)} %concatenate.53), channel_id=1, source_target_pairs={{0,1},{1,0},{2,3},{3,2},{4,5},{5,4},{6,7},{7,6},{8,9},{9,8},{10,11... | collective-permute-start | bytes 776 | tf_op jit(solution)/shard_map/ppermute | solution.py:12
  21.6 3.7 %collective-permute-start.1 = (bf16[16,512]{1,0:T(8,128)(2,1)S(1)}, bf16[16,512]{1,0:T(8,128)(2,1)S(1)}, u32[]{:S(2)}, u32[]{:S(2)}) collective-permute-start(bf16[16,512]{1,0:T(8,128)(2,1)S(1)} %pad_maximum_fusion.2), channel_id=1, source_target_pairs={{0,8},{1,9},{2,10},{3,11},{4,12},{5,13},{6,14},{7,15},{8,0},{9,1},... | collective-permute-start | bytes 49160 | tf_op jit(solution)/shard_map/ppermute | solution.py:12
  26.0 10.8 %copy-start = (bf16[1024,512]{1,0:T(8,128)(2,1)S(1)}, bf16[1024,512]{1,0:T(8,128)(2,1)}, u32[]{:S(2)}) copy-start(bf16[1024,512]{1,0:T(8,128)(2,1)} %param.5) | copy-start | bytes 3145732
  26.0 3.9 %collective-permute-start.2 = (bf16[32,512]{1,0:T(8,128)(2,1)S(1)}, bf16[32,512]{1,0:T(8,128)(2,1)S(1)}, u32[]{:S(2)}, u32[]{:S(2)}) collective-permute-start(bf16[32,512]{1,0:T(8,128)(2,1)S(1)} %pad_maximum_fusion.1), channel_id=1, source_target_pairs={{0,4},{1,5},{2,6},{3,7},{4,0},{5,1},{6,2},{7,3},{8,12},{9,13},{10,... | collective-permute-start | bytes 98312 | tf_op jit(solution)/shard_map/ppermute | solution.py:12
  30.6 4.3 %collective-permute-start.3 = (bf16[64,512]{1,0:T(8,128)(2,1)S(1)}, bf16[64,512]{1,0:T(8,128)(2,1)S(1)}, u32[]{:S(2)}, u32[]{:S(2)}) collective-permute-start(bf16[64,512]{1,0:T(8,128)(2,1)S(1)} %pad_maximum_fusion), channel_id=1, source_target_pairs={{0,2},{1,3},{2,0},{3,1},{4,6},{5,7},{6,4},{7,5},{8,10},{9,11},{10,... | collective-permute-start | bytes 196616 | tf_op jit(solution)/shard_map/ppermute | solution.py:12
  34.9 1.7 %collective-permute-start.4 = (bf16[128,512]{1,0:T(8,128)(2,1)S(1)}, bf16[128,512]{1,0:T(8,128)(2,1)S(1)}, u32[]{:S(2)}, u32[]{:S(2)}) collective-permute-start(bf16[128,512]{1,0:T(8,128)(2,1)S(1)} %get-tuple-element.12), channel_id=1, source_target_pairs={{0,1},{1,0},{2,3},{3,2},{4,5},{5,4},{6,7},{7,6},{8,9},{9,8},{10,11... | collective-permute-start | bytes 393224 | tf_op jit(solution)/shard_map/ppermute | solution.py:12
  37.3 0.7 %copy-start.2 = (f32[1024]{0:T(1024)S(1)}, f32[1024]{0:T(1024)}, u32[]{:S(2)}) copy-start(f32[1024]{0:T(1024)} %param.8) | copy-start | bytes 12292
  38.6 17.7 %copy-start.3 = (f32[8]{0:T(128)S(1)}, f32[8]{0:T(128)}, u32[]{:S(2)}) copy-start(f32[8]{0:T(128)} %param.9) | copy-start | bytes 100
  39.2 1.4 %collective-permute-start.10 = (f32[2,128]{1,0:T(2,128)S(1)}, f32[2,128]{1,0:T(2,128)S(1)}, u32[]{:S(2)}, u32[]{:S(2)}) collective-permute-start(f32[2,128]{1,0:T(2,128)S(1)} %pad_maximum_fusion.3), channel_id=1, source_target_pairs={{0,1},{1,0},{2,3},{3,2},{4,5},{5,4},{6,7},{7,6},{8,9},{9,8},{10,11... | collective-permute-start | bytes 3080 | tf_op jit(solution)/shard_map/ppermute | solution.py:12
  40.7 3.6 %collective-permute-start.11 = (f32[2,64]{1,0:T(2,128)S(1)}, f32[2,64]{1,0:T(2,128)S(1)}, u32[]{:S(2)}, u32[]{:S(2)}) collective-permute-start(f32[2,64]{1,0:T(2,128)S(1)} %slice.116), channel_id=1, source_target_pairs={{0,2},{1,3},{2,0},{3,1},{4,6},{5,7},{6,4},{7,5},{8,10},{9,11},{10,... | collective-permute-start | bytes 1544 | tf_op jit(solution)/shard_map/ppermute | solution.py:12
  44.4 3.6 %collective-permute-start.12 = (f32[2,32]{1,0:T(2,128)S(1)}, f32[2,32]{1,0:T(2,128)S(1)}, u32[]{:S(2)}, u32[]{:S(2)}) collective-permute-start(f32[2,32]{1,0:T(2,128)S(1)} %slice.121), channel_id=1, source_target_pairs={{0,4},{1,5},{2,6},{3,7},{4,0},{5,1},{6,2},{7,3},{8,12},{9,13},{10,... | collective-permute-start | bytes 776 | tf_op jit(solution)/shard_map/ppermute | solution.py:12
  48.1 3.6 %collective-permute-start.13 = (f32[2,16]{1,0:T(2,128)S(1)}, f32[2,16]{1,0:T(2,128)S(1)}, u32[]{:S(2)}, u32[]{:S(2)}) collective-permute-start(f32[2,16]{1,0:T(2,128)S(1)} %slice.126), channel_id=1, source_target_pairs={{0,8},{1,9},{2,10},{3,11},{4,12},{5,13},{6,14},{7,15},{8,0},{9,1},... | collective-permute-start | bytes 392 | tf_op jit(solution)/shard_map/ppermute | solution.py:12
  51.7 4.5 %collective-permute-start.14 = (f32[2,8]{1,0:T(2,128)S(1)}, f32[2,8]{1,0:T(2,128)S(1)}, u32[]{:S(2)}, u32[]{:S(2)}) collective-permute-start(f32[2,8]{1,0:T(2,128)S(1)} %slice.131), channel_id=1, source_target_pairs={{0,16},{1,17},{2,18},{3,19},{4,20},{5,21},{6,22},{7,23},{8,24},{9,... | collective-permute-start | bytes 200 | tf_op jit(solution)/shard_map/ppermute | solution.py:12

commit v2 on v1

--- a/solution.py
+++ b/solution.py
@@ -27,11 +27,12 @@
     features = sources.shape[1]
     factor = 2.0 / (features * epsilon)
 
-    held_rows, held_pots = targets, target_potential
+    held = jnp.concatenate(
+        [targets, jnp.broadcast_to(target_potential[:, None], (targets.shape[0], 128))], 1
+    )
     for bit in order:
-        other_rows, other_pots = exchange((held_rows, held_pots), bit, count)
-        held_rows = jnp.concatenate([held_rows, other_rows], 0)
-        held_pots = jnp.concatenate([held_pots, other_pots], 0)
+        held = jnp.concatenate([held, exchange(held, bit, count)], 0)
+    held_rows, held_pots = held[:, :features], held[:, features]
 
     pot_f32 = held_pots.astype(jnp.float32)
     offset = pot_f32 / epsilon - jnp.sum(jnp.square(held_rows.astype(jnp.float32)), 1) / (

time: 57.2 us -> 44.5 us (0.78)
  waiting for transfers between devices: 22.4 us -> 15.7 us
  starting transfers between devices: 22.7 us -> 18.9 us
  other arithmetic: 8 us -> 6.62 us
  local copies, waits for them, and re-layouts: 2.4 us -> 1.61 us
    ppermute x15 -> x10, waiting for transfers between devices: 22.4 us -> 15.7 us  [exchange(): return lax.ppermute(x, AXES, route)]
    ppermute x15 -> x10, starting transfers between devices: 22.7 us -> 18.9 us  [exchange(): return lax.ppermute(x, AXES, route)]
    concatenate x6 -> x3, other arithmetic: 4.3 us -> 2.11 us  [per_device(): held = jnp.concatenate([held, exchange(held, bit, count)], 0)]
    concatenate x4 -> x2, local copies, waits for them, and re-layouts: 0.88 us -> 0.05 us  [per_device(): held = jnp.concatenate([held, exchange(held, bit, count)], 0)]
    broadcast_in_dim x0 -> x1, local copies, waits for them, and re-layouts: none -> 0.73 us  [per_device(): jnp.broadcast_to(target_potential[:, None], (targets.shape[0], 128))]
    unnamed x0 -> x1, other arithmetic: none -> 0.7 us
    unnamed x12 -> x9, local copies, waits for them, and re-layouts: 1.23 us -> 0.55 us
  transfers between devices with their start and end apart: 15 -> 10, of which waited for: 11 -> 9; matrix products, arithmetic and copies ran while one was open for 10% -> 3% of each run, Pallas kernels for 0% -> 0%
where the time goes in v2:
time: 44.5 us; the launch traced here: 44.1 us
  starting transfers between devices  18.9 us (42%)
  waiting for transfers between devices  15.7 us (35%)
  other arithmetic  6.62 us (15%)
  local copies, waits for them, and re-layouts  1.61 us (4%)
  between operations  0.74 us (2%)
  matrix products  0.48 us (1%)
    ppermute x10, starting transfers between devices, exchange(): return lax.ppermute(x, AXES, route)  18.9 us
    ppermute x10, waiting for transfers between devices, exchange(): return lax.ppermute(x, AXES, route)  15.7 us
    concatenate x3, other arithmetic, per_device(): held = jnp.concatenate([held, exchange(held, bit, count)], 0)  2.11 us
    reduce_sum x1, other arithmetic, per_device(): jnp.sum(jnp.square(sources.astype(jnp.float32)), 1) / features  1.5 us
  transfers between devices with their start and end apart: 10, of which 9 were waited for; matrix products, arithmetic and copies ran while one was open for 3% of the time, Pallas kernels for 0%

profile of v2, /device:TPU:0, one launch (start us, length us, event | category | flops | bytes accessed | tf_op | source)
XLA Modules:
  0.0 44.1 jit_solution(922833046506422929)
XLA Ops:
  0.6 0.7 %broadcast_in_dim.2 = bf16[8,128]{1,0:T(8,128)(2,1)S(1)} broadcast(bf16[8]{0:T(256)(128)(2,1)} %param.7), dimensions={0} | broadcast | bytes 2064 | tf_op jit(solution)/shard_map/broadcast_in_dim | solution.py:31
  1.4 0.7 %constant_dynamic-update-slice_fusion.4 = (bf16[128,640]{1,0:T(8,128)(2,1)S(1)}, bf16[256,640]{1,0:T(8,128)(2,1)S(1)}, bf16[8,640]{1,0:T(8,128)(2,1)S(1)}) fusion(bf16[8,128]{1,0:T(8,128)(2,1)S(1)} %broadcast_in_dim.2, bf16[8,512]{1,0:T(8,128)(2,1)} %param.6), kind=kLoop, calls=%fused_computation.16 | loop fusion | flops 20478 | bytes 40960
  2.1 4.0 %collective-permute-start = (bf16[8,640]{1,0:T(8,128)(2,1)S(1)}, bf16[8,640]{1,0:T(8,128)(2,1)S(1)}, u32[]{:S(2)}, u32[]{:S(2)}) collective-permute-start(bf16[8,640]{1,0:T(8,128)(2,1)S(1)} %get-tuple-element.22), channel_id=1, source_target_pairs={{0,16},{1,17},{2,18},{3,19},{4,20},{5,21},{6,22},{7,23},{8,24},{9,... | collective-permute-start | bytes 30728 | tf_op jit(solution)/shard_map/ppermute | solution.py:12
  6.1 1.6 %collective-permute-done = bf16[8,640]{1,0:T(8,128)(2,1)S(1)} collective-permute-done((bf16[8,640]{1,0:T(8,128)(2,1)S(1)}, bf16[8,640]{1,0:T(8,128)(2,1)S(1)}, u32[]{:S(2)}, u32[]{:S(2)}) %collective-permute-start) | collective-permute-done | bytes 10272 | tf_op jit(solution)/shard_map/ppermute | solution.py:12
  7.7 0.7 %pad_maximum_fusion.2 = bf16[16,640]{1,0:T(8,128)(2,1)S(1)} fusion(bf16[8,640]{1,0:T(8,128)(2,1)S(1)} %collective-permute-done, bf16[8,128]{1,0:T(8,128)(2,1)S(1)} %broadcast_in_dim.2, bf16[8,512]{1,0:T(8,128)(2,1)} %param.6), kind=kLoop, calls=%fused_computation.23 | loop fusion | flops 61440 | bytes 40960 | tf_op jit(solution)/shard_map/concatenate | solution.py:34
  8.4 1.9 %collective-permute-start.1 = (bf16[16,640]{1,0:T(8,128)(2,1)S(1)}, bf16[16,640]{1,0:T(8,128)(2,1)S(1)}, u32[]{:S(2)}, u32[]{:S(2)}) collective-permute-start(bf16[16,640]{1,0:T(8,128)(2,1)S(1)} %pad_maximum_fusion.2), channel_id=1, source_target_pairs={{0,8},{1,9},{2,10},{3,11},{4,12},{5,13},{6,14},{7,15},{8,0},{9,1},... | collective-permute-start | bytes 61448 | tf_op jit(solution)/shard_map/ppermute | solution.py:12
  10.4 1.9 %collective-permute-done.1 = bf16[16,640]{1,0:T(8,128)(2,1)S(1)} collective-permute-done((bf16[16,640]{1,0:T(8,128)(2,1)S(1)}, bf16[16,640]{1,0:T(8,128)(2,1)S(1)}, u32[]{:S(2)}, u32[]{:S(2)}) %collective-permute-start.1) | collective-permute-done | bytes 20512 | tf_op jit(solution)/shard_map/ppermute | solution.py:12
  12.2 0.7 %pad_maximum_fusion.1 = bf16[32,640]{1,0:T(8,128)(2,1)S(1)} fusion(bf16[16,640]{1,0:T(8,128)(2,1)S(1)} %collective-permute-done.1, bf16[8,640]{1,0:T(8,128)(2,1)S(1)} %collective-permute-done, bf16[8,128]{1,0:T(8,128)(2,1)S(1)} %broadcast_in_dim.2, bf16[8,512]{1,0:T(8,128)(2,1)} %param.6), kind=kLoop, calls=%fused_computation.11 | loop fusion | flops 163840 | bytes 81920 | tf_op jit(solution)/shard_map/concatenate | solution.py:34
  12.9 1.8 %collective-permute-start.2 = (bf16[32,640]{1,0:T(8,128)(2,1)S(1)}, bf16[32,640]{1,0:T(8,128)(2,1)S(1)}, u32[]{:S(2)}, u32[]{:S(2)}) collective-permute-start(bf16[32,640]{1,0:T(8,128)(2,1)S(1)} %pad_maximum_fusion.1), channel_id=1, source_target_pairs={{0,4},{1,5},{2,6},{3,7},{4,0},{5,1},{6,2},{7,3},{8,12},{9,13},{10,... | collective-permute-start | bytes 122888 | tf_op jit(solution)/shard_map/ppermute | solution.py:12
  14.8 2.2 %collective-permute-done.2 = bf16[32,640]{1,0:T(8,128)(2,1)S(1)} collective-permute-done((bf16[32,640]{1,0:T(8,128)(2,1)S(1)}, bf16[32,640]{1,0:T(8,128)(2,1)S(1)}, u32[]{:S(2)}, u32[]{:S(2)}) %collective-permute-start.2) | collective-permute-done | bytes 40992 | tf_op jit(solution)/shard_map/ppermute | solution.py:12
  16.9 0.7 %pad_maximum_fusion = bf16[64,640]{1,0:T(8,128)(2,1)S(1)} fusion(bf16[32,640]{1,0:T(8,128)(2,1)S(1)} %collective-permute-done.2, bf16[16,640]{1,0:T(8,128)(2,1)S(1)} %collective-permute-done.1, bf16[8,640]{1,0:T(8,128)(2,1)S(1)} %collective-permute-done, bf16[8,128]{1,0:T(8,128)(2,1)S(1)} %broadcast_in_dim.2, bf16[8,512]{1,0:T(8,128)(2,1)} %param.6), kind=kLoop, calls=%fused_computation.10 | loop fusion | flops 409600 | bytes 163840 | tf_op jit(solution)/shard_map/concatenate | solution.py:34
  17.6 0.0 copy-start
  17.6 1.9 %collective-permute-start.3 = (bf16[64,640]{1,0:T(8,128)(2,1)S(1)}, bf16[64,640]{1,0:T(8,128)(2,1)S(1)}, u32[]{:S(2)}, u32[]{:S(2)}) collective-permute-start(bf16[64,640]{1,0:T(8,128)(2,1)S(1)} %pad_maximum_fusion), channel_id=1, source_target_pairs={{0,2},{1,3},{2,0},{3,1},{4,6},{5,7},{6,4},{7,5},{8,10},{9,11},{10,... | collective-permute-start | bytes 245768 | tf_op jit(solution)/shard_map/ppermute | solution.py:12
  19.6 2.6 %collective-permute-done.3 = bf16[64,640]{1,0:T(8,128)(2,1)S(1)} collective-permute-done((bf16[64,640]{1,0:T(8,128)(2,1)S(1)}, bf16[64,640]{1,0:T(8,128)(2,1)S(1)}, u32[]{:S(2)}, u32[]{:S(2)}) %collective-permute-start.3) | collective-permute-done | bytes 81952 | tf_op jit(solution)/shard_map/ppermute | solution.py:12
  22.2 0.1 collective-permute-start.4
  22.2 1.5 %multiply_reduce_fusion = f32[1024]{0:T(1024)S(1)} fusion(bf16[1024,512]{1,0:T(8,128)(2,1)} %param.5), kind=kLoop, calls=%fused_computation | loop fusion | flops 1571840 | bytes 1052672 | tf_op jit(solution)/shard_map/reduce_sum | solution.py:58
  23.8 0.0 collective-permute-done.4
  23.8 0.1 multiply_reduce_fusion.1
  23.9 0.1 multiply_reduce_fusion.2
  24.1 0.0 copy-done
  24.1 0.5 %fusion.10 = (f32[1024]{0:T(1024)S(1)}, f32[256,1024]{1,0:T(8,128)S(1)}) fusion(f32[256]{0:T(256)S(1)} %multiply_subtract_fusion, bf16[1024,512]{1,0:T(8,128)(2,1)S(1)} %copy-done, bf16[256,640]{1,0:T(8,128)(2,1)S(1)} %constant_dynamic-update-slice_fusion.5), kind=kOutput, calls=%fused_computation.53 | convolution fusion | flops 269220864 | bytes 2364416 | tf_op jit(solution)/shard_map/dot_general | solution.py:41
  24.6 0.0 copy-start.1
  24.6 0.2 exponential_reduce_fusion.1
  24.7 0.5 %copy-done.1 = f32[1024]{0:T(1024)S(1)} copy-done((f32[1024]{0:T(1024)S(1)}, f32[1024]{0:T(1024)}, u32[]{:S(2)}) %copy-start.1) | copy-done | bytes 4120
  25.2 0.6 %multiply_add_fusion = (f32[1024]{0:T(1024)}, f32[1024]{0:T(1024)S(1)}) fusion(f32[1024]{0:T(1024)S(1)} %multiply_reduce_fusion, f32[1024]{0:T(1024)S(1)} %copy-done.1, f32[1024]{0:T(1024)S(1)} %get-tuple-element.23, f32[1024]{0:T(1024)S(1)} %exponential_reduce_fusion.1), kind=kLoop, calls=%fused_computation.25 | loop fusion | flops 5120 | bytes 24576 | tf_op jit(solution)/shard_map/add | solution.py:58
  25.8 0.0 copy-start.2
  25.9 0.3 fusion.1
  26.1 0.4 exponential_reduce_fusion
  26.5 0.6 %collective-permute-start.5 = (f32[2,128]{1,0:T(2,128)S(1)}, f32[2,128]{1,0:T(2,128)S(1)}, u32[]{:S(2)}, u32[]{:S(2)}) collective-permute-start(f32[2,128]{1,0:T(2,128)S(1)} %pad_maximum_fusion.4), channel_id=1, source_target_pairs={{0,1},{1,0},{2,3},{3,2},{4,5},{5,4},{6,7},{7,6},{8,9},{9,8},{10,11... | collective-permute-start | bytes 3080 | tf_op jit(solution)/shard_map/ppermute | solution.py:12
  27.1 0.8 %collective-permute-done.5 = f32[2,128]{1,0:T(2,128)S(1)} collective-permute-done((f32[2,128]{1,0:T(2,128)S(1)}, f32[2,128]{1,0:T(2,128)S(1)}, u32[]{:S(2)}, u32[]{:S(2)}) %collective-permute-start.5) | collective-permute-done | bytes 1056 | tf_op jit(solution)/shard_map/ppermute | solution.py:12
  27.9 0.1 slice.124
  28.0 1.9 %collective-permute-start.6 = (f32[2,64]{1,0:T(2,128)S(1)}, f32[2,64]{1,0:T(2,128)S(1)}, u32[]{:S(2)}, u32[]{:S(2)}) collective-permute-start(f32[2,64]{1,0:T(2,128)S(1)} %slice.124), channel_id=1, source_target_pairs={{0,2},{1,3},{2,0},{3,1},{4,6},{5,7},{6,4},{7,5},{8,10},{9,11},{10,... | collective-permute-start | bytes 1544 | tf_op jit(solution)/shard_map/ppermute | solution.py:12
  29.9 1.7 %collective-permute-done.6 = f32[2,64]{1,0:T(2,128)S(1)} collective-permute-done((f32[2,64]{1,0:T(2,128)S(1)}, f32[2,64]{1,0:T(2,128)S(1)}, u32[]{:S(2)}, u32[]{:S(2)}) %collective-permute-start.6) | collective-permute-done | bytes 544 | tf_op jit(solution)/shard_map/ppermute | solution.py:12
  31.6 0.1 slice.129
  31.7 1.8 %collective-permute-start.7 = (f32[2,32]{1,0:T(2,128)S(1)}, f32[2,32]{1,0:T(2,128)S(1)}, u32[]{:S(2)}, u32[]{:S(2)}) collective-permute-start(f32[2,32]{1,0:T(2,128)S(1)} %slice.129), channel_id=1, source_target_pairs={{0,4},{1,5},{2,6},{3,7},{4,0},{5,1},{6,2},{7,3},{8,12},{9,13},{10,... | collective-permute-start | bytes 776 | tf_op jit(solution)/shard_map/ppermute | solution.py:12
  33.5 1.7 %collective-permute-done.7 = f32[2,32]{1,0:T(2,128)S(1)} collective-permute-done((f32[2,32]{1,0:T(2,128)S(1)}, f32[2,32]{1,0:T(2,128)S(1)}, u32[]{:S(2)}, u32[]{:S(2)}) %collective-permute-start.7) | collective-permute-done | bytes 288 | tf_op jit(solution)/shard_map/ppermute | solution.py:12
  35.3 0.1 slice.134
  35.4 1.9 %collective-permute-start.8 = (f32[2,16]{1,0:T(2,128)S(1)}, f32[2,16]{1,0:T(2,128)S(1)}, u32[]{:S(2)}, u32[]{:S(2)}) collective-permute-start(f32[2,16]{1,0:T(2,128)S(1)} %slice.134), channel_id=1, source_target_pairs={{0,8},{1,9},{2,10},{3,11},{4,12},{5,13},{6,14},{7,15},{8,0},{9,1},... | collective-permute-start | bytes 392 | tf_op jit(solution)/shard_map/ppermute | solution.py:12
  37.3 1.7 %collective-permute-done.8 = f32[2,16]{1,0:T(2,128)S(1)} collective-permute-done((f32[2,16]{1,0:T(2,128)S(1)}, f32[2,16]{1,0:T(2,128)S(1)}, u32[]{:S(2)}, u32[]{:S(2)}) %collective-permute-start.8) | collective-permute-done | bytes 160 | tf_op jit(solution)/shard_map/ppermute | solution.py:12
  39.0 0.1 slice.139
  39.0 2.9 %collective-permute-start.9 = (f32[2,8]{1,0:T(2,128)S(1)}, f32[2,8]{1,0:T(2,128)S(1)}, u32[]{:S(2)}, u32[]{:S(2)}) collective-permute-start(f32[2,8]{1,0:T(2,128)S(1)} %slice.139), channel_id=1, source_target_pairs={{0,16},{1,17},{2,18},{3,19},{4,20},{5,21},{6,22},{7,23},{8,24},{9,... | collective-permute-start | bytes 200 | tf_op jit(solution)/shard_map/ppermute | solution.py:12
  42.0 1.5 %collective-permute-done.9 = f32[2,8]{1,0:T(2,128)S(1)} collective-permute-done((f32[2,8]{1,0:T(2,128)S(1)}, f32[2,8]{1,0:T(2,128)S(1)}, u32[]{:S(2)}, u32[]{:S(2)}) %collective-permute-start.9) | collective-permute-done | bytes 96 | tf_op jit(solution)/shard_map/ppermute | solution.py:12
  43.5 0.0 copy-done.2
  43.5 0.5 %subtract_multiply_fusion = f32[8]{0:T(128)} fusion(f32[8]{0:T(128)S(1)} %copy-done.2, f32[2,8]{1,0:T(2,128)S(1)} %collective-permute-done.9, f32[1,16]{1,0:T(1,128)S(1)} %get-tuple-element.2, f32[1,16]{1,0:T(1,128)S(1)} %get-tuple-element.3), kind=kLoop, calls=%fused_computation.45 | loop fusion | flops 72 | bytes 192 | tf_op jit(solution)/shard_map/mul | solution.py:61
  (15 shorter events, 0.2 us)
Async XLA Ops:
  2.1 5.7 %collective-permute-start = (bf16[8,640]{1,0:T(8,128)(2,1)S(1)}, bf16[8,640]{1,0:T(8,128)(2,1)S(1)}, u32[]{:S(2)}, u32[]{:S(2)}) collective-permute-start(bf16[8,640]{1,0:T(8,128)(2,1)S(1)} %get-tuple-element.22), channel_id=1, source_target_pairs={{0,16},{1,17},{2,18},{3,19},{4,20},{5,21},{6,22},{7,23},{8,24},{9,... | collective-permute-start | bytes 30728 | tf_op jit(solution)/shard_map/ppermute | solution.py:12
  8.4 3.8 %collective-permute-start.1 = (bf16[16,640]{1,0:T(8,128)(2,1)S(1)}, bf16[16,640]{1,0:T(8,128)(2,1)S(1)}, u32[]{:S(2)}, u32[]{:S(2)}) collective-permute-start(bf16[16,640]{1,0:T(8,128)(2,1)S(1)} %pad_maximum_fusion.2), channel_id=1, source_target_pairs={{0,8},{1,9},{2,10},{3,11},{4,12},{5,13},{6,14},{7,15},{8,0},{9,1},... | collective-permute-start | bytes 61448 | tf_op jit(solution)/shard_map/ppermute | solution.py:12
  12.9 4.0 %collective-permute-start.2 = (bf16[32,640]{1,0:T(8,128)(2,1)S(1)}, bf16[32,640]{1,0:T(8,128)(2,1)S(1)}, u32[]{:S(2)}, u32[]{:S(2)}) collective-permute-start(bf16[32,640]{1,0:T(8,128)(2,1)S(1)} %pad_maximum_fusion.1), channel_id=1, source_target_pairs={{0,4},{1,5},{2,6},{3,7},{4,0},{5,1},{6,2},{7,3},{8,12},{9,13},{10,... | collective-permute-start | bytes 122888 | tf_op jit(solution)/shard_map/ppermute | solution.py:12
  17.6 6.4 %copy-start = (bf16[1024,512]{1,0:T(8,128)(2,1)S(1)}, bf16[1024,512]{1,0:T(8,128)(2,1)}, u32[]{:S(2)}) copy-start(bf16[1024,512]{1,0:T(8,128)(2,1)} %param.5) | copy-start | bytes 3145732
  17.6 4.5 %collective-permute-start.3 = (bf16[64,640]{1,0:T(8,128)(2,1)S(1)}, bf16[64,640]{1,0:T(8,128)(2,1)S(1)}, u32[]{:S(2)}, u32[]{:S(2)}) collective-permute-start(bf16[64,640]{1,0:T(8,128)(2,1)S(1)} %pad_maximum_fusion), channel_id=1, source_target_pairs={{0,2},{1,3},{2,0},{3,1},{4,6},{5,7},{6,4},{7,5},{8,10},{9,11},{10,... | collective-permute-start | bytes 245768 | tf_op jit(solution)/shard_map/ppermute | solution.py:12
  22.2 1.6 %collective-permute-start.4 = (bf16[128,640]{1,0:T(8,128)(2,1)S(1)}, bf16[128,640]{1,0:T(8,128)(2,1)S(1)}, u32[]{:S(2)}, u32[]{:S(2)}) collective-permute-start(bf16[128,640]{1,0:T(8,128)(2,1)S(1)} %get-tuple-element.12), channel_id=1, source_target_pairs={{0,1},{1,0},{2,3},{3,2},{4,5},{5,4},{6,7},{7,6},{8,9},{9,8},{10,11... | collective-permute-start | bytes 491528 | tf_op jit(solution)/shard_map/ppermute | solution.py:12
  24.6 0.7 %copy-start.1 = (f32[1024]{0:T(1024)S(1)}, f32[1024]{0:T(1024)}, u32[]{:S(2)}) copy-start(f32[1024]{0:T(1024)} %param.8) | copy-start | bytes 12292
  25.8 17.7 %copy-start.2 = (f32[8]{0:T(128)S(1)}, f32[8]{0:T(128)}, u32[]{:S(2)}) copy-start(f32[8]{0:T(128)} %param.9) | copy-start | bytes 100
  26.5 1.4 %collective-permute-start.5 = (f32[2,128]{1,0:T(2,128)S(1)}, f32[2,128]{1,0:T(2,128)S(1)}, u32[]{:S(2)}, u32[]{:S(2)}) collective-permute-start(f32[2,128]{1,0:T(2,128)S(1)} %pad_maximum_fusion.4), channel_id=1, source_target_pairs={{0,1},{1,0},{2,3},{3,2},{4,5},{5,4},{6,7},{7,6},{8,9},{9,8},{10,11... | collective-permute-start | bytes 3080 | tf_op jit(solution)/shard_map/ppermute | solution.py:12
  28.0 3.6 %collective-permute-start.6 = (f32[2,64]{1,0:T(2,128)S(1)}, f32[2,64]{1,0:T(2,128)S(1)}, u32[]{:S(2)}, u32[]{:S(2)}) collective-permute-start(f32[2,64]{1,0:T(2,128)S(1)} %slice.124), channel_id=1, source_target_pairs={{0,2},{1,3},{2,0},{3,1},{4,6},{5,7},{6,4},{7,5},{8,10},{9,11},{10,... | collective-permute-start | bytes 1544 | tf_op jit(solution)/shard_map/ppermute | solution.py:12
  31.7 3.6 %collective-permute-start.7 = (f32[2,32]{1,0:T(2,128)S(1)}, f32[2,32]{1,0:T(2,128)S(1)}, u32[]{:S(2)}, u32[]{:S(2)}) collective-permute-start(f32[2,32]{1,0:T(2,128)S(1)} %slice.129), channel_id=1, source_target_pairs={{0,4},{1,5},{2,6},{3,7},{4,0},{5,1},{6,2},{7,3},{8,12},{9,13},{10,... | collective-permute-start | bytes 776 | tf_op jit(solution)/shard_map/ppermute | solution.py:12
  35.4 3.6 %collective-permute-start.8 = (f32[2,16]{1,0:T(2,128)S(1)}, f32[2,16]{1,0:T(2,128)S(1)}, u32[]{:S(2)}, u32[]{:S(2)}) collective-permute-start(f32[2,16]{1,0:T(2,128)S(1)} %slice.134), channel_id=1, source_target_pairs={{0,8},{1,9},{2,10},{3,11},{4,12},{5,13},{6,14},{7,15},{8,0},{9,1},... | collective-permute-start | bytes 392 | tf_op jit(solution)/shard_map/ppermute | solution.py:12
  39.0 4.5 %collective-permute-start.9 = (f32[2,8]{1,0:T(2,128)S(1)}, f32[2,8]{1,0:T(2,128)S(1)}, u32[]{:S(2)}, u32[]{:S(2)}) collective-permute-start(f32[2,8]{1,0:T(2,128)S(1)} %slice.139), channel_id=1, source_target_pairs={{0,16},{1,17},{2,18},{3,19},{4,20},{5,21},{6,22},{7,23},{8,24},{9,... | collective-permute-start | bytes 200 | tf_op jit(solution)/shard_map/ppermute | solution.py:12

commit v3 on v2

--- a/solution.py
+++ b/solution.py
@@ -12,12 +12,6 @@
     return lax.ppermute(x, AXES, route)
 
 
-def combine(first, second):
-    new_max = jnp.maximum(first[0], second[0])
-    new_sum = first[1] * jnp.exp(first[0] - new_max) + second[1] * jnp.exp(second[0] - new_max)
-    return jnp.stack([new_max, new_sum])
-
-
 def per_device(sources, targets, target_potential, log_source_mass, log_target_mass):
     count = lax.axis_size("group") * lax.axis_size("blk")
     levels = count.bit_length() - 1
@@ -27,8 +21,10 @@
     features = sources.shape[1]
     factor = 2.0 / (features * epsilon)
 
-    held = jnp.concatenate(
-        [targets, jnp.broadcast_to(target_potential[:, None], (targets.shape[0], 128))], 1
+    held = lax.optimization_barrier(
+        jnp.concatenate(
+            [targets, jnp.broadcast_to(target_potential[:, None], (targets.shape[0], 128))], 1
+        )
     )
     for bit in order:
         held = jnp.concatenate([held, exchange(held, bit, count)], 0)
@@ -49,11 +45,15 @@
     col_max = jnp.max(columns, 0)
     col_sum = jnp.sum(jnp.exp(columns - col_max[None, :]), 0)
 
-    part = jnp.stack([col_max, col_sum])
-    for bit in reversed(order):
-        half = part.shape[1] // 2
-        arrived = exchange(part[:, half:], bit, count)
-        part = combine(part[:, :half], arrived)
+    me = lax.axis_index(AXES)
+    apart = me ^ jnp.arange(count)
+    where = sum(((apart >> bit) & 1) << step for step, bit in enumerate(order))
+    part = jnp.stack([col_max, col_sum]).reshape(2, count, -1)
+    part = jnp.take(part, where, axis=1)
+    part = lax.all_to_all(part, AXES, 1, 1, tiled=True)
+    owned_max = jnp.max(part[0], 0)
+    owned_sum = jnp.sum(part[1] * jnp.exp(part[0] - owned_max[None, :]), 0)
+    part = (owned_max, owned_sum)
 
     source_potential = epsilon * source_dual + jnp.sum(
         jnp.square(sources.astype(jnp.float32)), 1

time: 44.5 us -> 39.6 us (0.89)
  blocking collectives: 0 us -> 13.3 us
  starting transfers between devices: 18.9 us -> 9.76 us
  waiting for transfers between devices: 15.7 us -> 8.21 us
  other arithmetic: 6.62 us -> 4.67 us
  local copies, waits for them, and re-layouts: 1.61 us -> 2.12 us
    all_to_all x0 -> x1, blocking collectives: none -> 13.3 us  [per_device(): part = lax.all_to_all(part, AXES, 1, 1, tiled=True)]
    ppermute x10 -> x5, starting transfers between devices: 18.9 us -> 9.76 us  [exchange(): return lax.ppermute(x, AXES, route)]
    ppermute x10 -> x5, waiting for transfers between devices: 15.7 us -> 8.21 us  [exchange(): return lax.ppermute(x, AXES, route)]
    concatenate x3, other arithmetic: 2.11 us -> 0.02 us  [per_device(): held = jnp.concatenate([held, exchange(held, bit, count)], 0)]
    unnamed x1 -> x0, other arithmetic: 0.7 us -> none
    concatenate x0 -> x1, other arithmetic: none -> 0.7 us  [per_device(): jnp.concatenate([targets, jnp.broadcast_to(target_potential[:, None], (ta...]
    gather x0 -> x1, local copies, waits for them, and re-layouts: none -> 0.61 us  [per_device(): part = jnp.take(part, where, axis=1)]
  transfers between devices with their start and end apart: 10 -> 5, of which waited for: 9 -> 4; matrix products, arithmetic and copies ran while one was open for 3% -> 4% of each run, Pallas kernels for 0% -> 0%
where the time goes in v3:
time: 39.6 us; the launch traced here: 39.3 us
  blocking collectives  13.3 us (34%)
  starting transfers between devices  9.76 us (25%)
  waiting for transfers between devices  8.21 us (21%)
  other arithmetic  4.67 us (12%)
  local copies, waits for them, and re-layouts  2.12 us (5%)
  between operations  0.75 us (2%)
  matrix products  0.48 us (1%)
    all_to_all x1, blocking collectives, per_device(): part = lax.all_to_all(part, AXES, 1, 1, tiled=True)  13.3 us
    ppermute x5, starting transfers between devices, exchange(): return lax.ppermute(x, AXES, route)  9.76 us
    ppermute x5, waiting for transfers between devices, exchange(): return lax.ppermute(x, AXES, route)  8.21 us
    reduce_sum x1, other arithmetic, per_device(): jnp.sum(jnp.square(sources.astype(jnp.float32)), 1) / features  1.5 us
  transfers between devices with their start and end apart: 5, of which 4 were waited for; matrix products, arithmetic and copies ran while one was open for 4% of the time, Pallas kernels for 0%

profile of v3, /device:TPU:0, one launch (start us, length us, event | category | flops | bytes accessed | tf_op | source)
XLA Modules:
  0.0 39.3 jit_solution(10335273213500936371)
XLA Ops:
  0.6 0.7 %broadcast_in_dim.9 = bf16[8,128]{1,0:T(8,128)(2,1)S(1)} broadcast(bf16[8]{0:T(256)(128)(2,1)} %param.7), dimensions={0} | broadcast | bytes 2064 | tf_op jit(solution)/shard_map/broadcast_in_dim | solution.py:26
  1.4 0.7 %pad_maximum_fusion.4 = bf16[8,640]{1,0:T(8,128)(2,1)S(1)} fusion(bf16[8,128]{1,0:T(8,128)(2,1)S(1)} %broadcast_in_dim.9, bf16[8,512]{1,0:T(8,128)(2,1)} %param.6), kind=kLoop, calls=%fused_computation.28 | loop fusion | flops 20480 | bytes 20480 | tf_op jit(solution)/shard_map/concatenate | solution.py:25
  2.1 4.0 %collective-permute-start = (bf16[8,640]{1,0:T(8,128)(2,1)S(1)}, bf16[8,640]{1,0:T(8,128)(2,1)S(1)}, u32[]{:S(2)}, u32[]{:S(2)}) collective-permute-start(bf16[8,640]{1,0:T(8,128)(2,1)S(1)} %pad_maximum_fusion.4), channel_id=1, source_target_pairs={{0,16},{1,17},{2,18},{3,19},{4,20},{5,21},{6,22},{7,23},{8,24},{9,... | collective-permute-start | bytes 30728 | tf_op jit(solution)/shard_map/ppermute | solution.py:12
  6.1 1.6 %collective-permute-done = bf16[8,640]{1,0:T(8,128)(2,1)S(1)} collective-permute-done((bf16[8,640]{1,0:T(8,128)(2,1)S(1)}, bf16[8,640]{1,0:T(8,128)(2,1)S(1)}, u32[]{:S(2)}, u32[]{:S(2)}) %collective-permute-start) | collective-permute-done | bytes 10272 | tf_op jit(solution)/shard_map/ppermute | solution.py:12
  7.7 1.9 %collective-permute-start.1 = (bf16[16,640]{1,0:T(8,128)(2,1)S(1)}, bf16[16,640]{1,0:T(8,128)(2,1)S(1)}, u32[]{:S(2)}, u32[]{:S(2)}) collective-permute-start(bf16[16,640]{1,0:T(8,128)(2,1)S(1)} %pad_maximum_fusion.3), channel_id=1, source_target_pairs={{0,8},{1,9},{2,10},{3,11},{4,12},{5,13},{6,14},{7,15},{8,0},{9,1},... | collective-permute-start | bytes 61448 | tf_op jit(solution)/shard_map/ppermute | solution.py:12
  9.7 1.9 %collective-permute-done.1 = bf16[16,640]{1,0:T(8,128)(2,1)S(1)} collective-permute-done((bf16[16,640]{1,0:T(8,128)(2,1)S(1)}, bf16[16,640]{1,0:T(8,128)(2,1)S(1)}, u32[]{:S(2)}, u32[]{:S(2)}) %collective-permute-start.1) | collective-permute-done | bytes 20512 | tf_op jit(solution)/shard_map/ppermute | solution.py:12
  11.5 1.8 %collective-permute-start.2 = (bf16[32,640]{1,0:T(8,128)(2,1)S(1)}, bf16[32,640]{1,0:T(8,128)(2,1)S(1)}, u32[]{:S(2)}, u32[]{:S(2)}) collective-permute-start(bf16[32,640]{1,0:T(8,128)(2,1)S(1)} %pad_maximum_fusion.1), channel_id=1, source_target_pairs={{0,4},{1,5},{2,6},{3,7},{4,0},{5,1},{6,2},{7,3},{8,12},{9,13},{10,... | collective-permute-start | bytes 122888 | tf_op jit(solution)/shard_map/ppermute | solution.py:12
  13.4 2.2 %collective-permute-done.2 = bf16[32,640]{1,0:T(8,128)(2,1)S(1)} collective-permute-done((bf16[32,640]{1,0:T(8,128)(2,1)S(1)}, bf16[32,640]{1,0:T(8,128)(2,1)S(1)}, u32[]{:S(2)}, u32[]{:S(2)}) %collective-permute-start.2) | collective-permute-done | bytes 40992 | tf_op jit(solution)/shard_map/ppermute | solution.py:12
  15.5 0.0 copy-start
  15.6 1.9 %collective-permute-start.3 = (bf16[64,640]{1,0:T(8,128)(2,1)S(1)}, bf16[64,640]{1,0:T(8,128)(2,1)S(1)}, u32[]{:S(2)}, u32[]{:S(2)}) collective-permute-start(bf16[64,640]{1,0:T(8,128)(2,1)S(1)} %pad_maximum_fusion), channel_id=1, source_target_pairs={{0,2},{1,3},{2,0},{3,1},{4,6},{5,7},{6,4},{7,5},{8,10},{9,11},{10,... | collective-permute-start | bytes 245768 | tf_op jit(solution)/shard_map/ppermute | solution.py:12
  17.5 2.6 %collective-permute-done.3 = bf16[64,640]{1,0:T(8,128)(2,1)S(1)} collective-permute-done((bf16[64,640]{1,0:T(8,128)(2,1)S(1)}, bf16[64,640]{1,0:T(8,128)(2,1)S(1)}, u32[]{:S(2)}, u32[]{:S(2)}) %collective-permute-start.3) | collective-permute-done | bytes 81952 | tf_op jit(solution)/shard_map/ppermute | solution.py:12
  20.1 0.1 collective-permute-start.4
  20.2 1.5 %multiply_reduce_fusion = f32[1024]{0:T(1024)S(1)} fusion(bf16[1024,512]{1,0:T(8,128)(2,1)} %param.5), kind=kLoop, calls=%fused_computation.1 | loop fusion | flops 1571840 | bytes 1052672 | tf_op jit(solution)/shard_map/reduce_sum | solution.py:58
  21.7 0.0 collective-permute-done.4
  21.7 0.1 multiply_reduce_fusion.1
  21.8 0.1 multiply_reduce_fusion.2
  22.0 0.0 copy-done
  22.0 0.5 %fusion.5 = (f32[1024]{0:T(1024)S(1)}, f32[256,1024]{1,0:T(8,128)S(1)}) fusion(f32[256]{0:T(256)S(1)} %multiply_subtract_fusion, bf16[1024,512]{1,0:T(8,128)(2,1)S(1)} %copy-done, bf16[256,640]{1,0:T(8,128)(2,1)S(1)} %constant_dynamic-update-slice_fusion.5), kind=kOutput, calls=%fused_computation.39 | convolution fusion | flops 269220864 | bytes 2364416 | tf_op jit(solution)/shard_map/dot_general | solution.py:37
  22.5 0.0 copy-start.1
  22.5 0.2 exponential_reduce_fusion.1
  22.7 0.5 %copy-done.1 = f32[1024]{0:T(1024)S(1)} copy-done((f32[1024]{0:T(1024)S(1)}, f32[1024]{0:T(1024)}, u32[]{:S(2)}) %copy-start.1) | copy-done | bytes 4120
  23.2 0.6 %multiply_add_fusion = (f32[1024]{0:T(1024)}, f32[1024]{0:T(1024)S(1)}) fusion(f32[1024]{0:T(1024)S(1)} %multiply_reduce_fusion, f32[1024]{0:T(1024)S(1)} %copy-done.1, f32[1024]{0:T(1024)S(1)} %get-tuple-element.16, f32[1024]{0:T(1024)S(1)} %exponential_reduce_fusion.1), kind=kLoop, calls=%fused_computation.30 | loop fusion | flops 5120 | bytes 24576 | tf_op jit(solution)/shard_map/add | solution.py:58
  23.8 0.0 copy-start.2
  23.8 0.3 fusion.1
  24.0 0.4 %exponential_reduce_fusion = f32[256]{0:T(256)S(1)} fusion(f32[256,1024]{1,0:T(8,128)S(1)} %get-tuple-element.17, f32[256]{0:T(256)S(1)} %fusion.1, f32[1024]{0:T(1024)S(1)} %get-tuple-element.3, f32[256]{0:T(256)S(1)} %multiply_reduce_fusion.2), kind=kLoop, calls=%fused_computation.4 | loop fusion | flops 1048320 | bytes 1055744 | tf_op jit(solution)/shard_map/reduce_sum | solution.py:46
  24.4 0.1 stack.9
  24.5 0.1 stack.10
  24.6 0.1 pad_maximum_fusion.2
  24.7 0.6 %gather_fusion = f32[32,2,8]{2,1,0:T(2,128)S(1)} fusion(f32[2,32,8]{2,0,1:T(2,128)S(1)} %pad_maximum_fusion.2, s32[1024]{0:T(1024)S(1)} %pad_clamp_fusion), kind=kCustom, calls=%fused_computation | custom fusion | bytes 4224 | tf_op jit(solution)/shard_map/jit(_take)/gather | solution.py:52
  25.3 0.1 select_bitcast_fusion
  25.4 13.3 %all_to_all.5 = f32[2,32,8]{2,0,1:T(2,128)S(1)} all-to-all(f32[2,32,8]{2,0,1:T(2,128)S(1)} %select_bitcast_fusion), channel_id=1, replica_groups=mesh['group'=8,'blk'=4] {'group','blk'}, dimensions={1} | all-to-all | bytes 4096 | tf_op jit(solution)/shard_map/all_to_all | solution.py:53
  38.8 0.0 copy-done.2
  38.8 0.5 %subtract_multiply_fusion = f32[8]{0:T(128)} fusion(f32[8]{0:T(128)S(1)} %copy-done.2, f32[8]{0:T(128)S(1)} %reduce_max.29, f32[8]{0:T(128)S(1)} %multiply_reduce_fusion.3), kind=kLoop, calls=%fused_computation.37 | loop fusion | flops 24 | bytes 128 | tf_op jit(solution)/shard_map/mul | solution.py:61
  (16 shorter events, 0.2 us)
Async XLA Ops:
  2.1 5.7 %collective-permute-start = (bf16[8,640]{1,0:T(8,128)(2,1)S(1)}, bf16[8,640]{1,0:T(8,128)(2,1)S(1)}, u32[]{:S(2)}, u32[]{:S(2)}) collective-permute-start(bf16[8,640]{1,0:T(8,128)(2,1)S(1)} %pad_maximum_fusion.4), channel_id=1, source_target_pairs={{0,16},{1,17},{2,18},{3,19},{4,20},{5,21},{6,22},{7,23},{8,24},{9,... | collective-permute-start | bytes 30728 | tf_op jit(solution)/shard_map/ppermute | solution.py:12
  7.7 3.8 %collective-permute-start.1 = (bf16[16,640]{1,0:T(8,128)(2,1)S(1)}, bf16[16,640]{1,0:T(8,128)(2,1)S(1)}, u32[]{:S(2)}, u32[]{:S(2)}) collective-permute-start(bf16[16,640]{1,0:T(8,128)(2,1)S(1)} %pad_maximum_fusion.3), channel_id=1, source_target_pairs={{0,8},{1,9},{2,10},{3,11},{4,12},{5,13},{6,14},{7,15},{8,0},{9,1},... | collective-permute-start | bytes 61448 | tf_op jit(solution)/shard_map/ppermute | solution.py:12
  11.5 4.0 %collective-permute-start.2 = (bf16[32,640]{1,0:T(8,128)(2,1)S(1)}, bf16[32,640]{1,0:T(8,128)(2,1)S(1)}, u32[]{:S(2)}, u32[]{:S(2)}) collective-permute-start(bf16[32,640]{1,0:T(8,128)(2,1)S(1)} %pad_maximum_fusion.1), channel_id=1, source_target_pairs={{0,4},{1,5},{2,6},{3,7},{4,0},{5,1},{6,2},{7,3},{8,12},{9,13},{10,... | collective-permute-start | bytes 122888 | tf_op jit(solution)/shard_map/ppermute | solution.py:12
  15.5 6.4 %copy-start = (bf16[1024,512]{1,0:T(8,128)(2,1)S(1)}, bf16[1024,512]{1,0:T(8,128)(2,1)}, u32[]{:S(2)}) copy-start(bf16[1024,512]{1,0:T(8,128)(2,1)} %param.5) | copy-start | bytes 3145732
  15.6 4.5 %collective-permute-start.3 = (bf16[64,640]{1,0:T(8,128)(2,1)S(1)}, bf16[64,640]{1,0:T(8,128)(2,1)S(1)}, u32[]{:S(2)}, u32[]{:S(2)}) collective-permute-start(bf16[64,640]{1,0:T(8,128)(2,1)S(1)} %pad_maximum_fusion), channel_id=1, source_target_pairs={{0,2},{1,3},{2,0},{3,1},{4,6},{5,7},{6,4},{7,5},{8,10},{9,11},{10,... | collective-permute-start | bytes 245768 | tf_op jit(solution)/shard_map/ppermute | solution.py:12
  20.1 1.6 %collective-permute-start.4 = (bf16[128,640]{1,0:T(8,128)(2,1)S(1)}, bf16[128,640]{1,0:T(8,128)(2,1)S(1)}, u32[]{:S(2)}, u32[]{:S(2)}) collective-permute-start(bf16[128,640]{1,0:T(8,128)(2,1)S(1)} %get-tuple-element.4), channel_id=1, source_target_pairs={{0,1},{1,0},{2,3},{3,2},{4,5},{5,4},{6,7},{7,6},{8,9},{9,8},{10,11... | collective-permute-start | bytes 491528 | tf_op jit(solution)/shard_map/ppermute | solution.py:12
  22.5 0.7 %copy-start.1 = (f32[1024]{0:T(1024)S(1)}, f32[1024]{0:T(1024)}, u32[]{:S(2)}) copy-start(f32[1024]{0:T(1024)} %param.8) | copy-start | bytes 12292
  23.8 15.0 %copy-start.2 = (f32[8]{0:T(128)S(1)}, f32[8]{0:T(128)}, u32[]{:S(2)}) copy-start(f32[8]{0:T(128)} %param.9) | copy-start | bytes 100

commit v4 on v3

--- a/solution.py
+++ b/solution.py
@@ -21,9 +21,16 @@
     features = sources.shape[1]
     factor = 2.0 / (features * epsilon)
 
+    lanes = jnp.broadcast_to(target_potential.astype(jnp.float32)[:, None], (targets.shape[0], 128))
     held = lax.optimization_barrier(
-        jnp.concatenate(
-            [targets, jnp.broadcast_to(target_potential[:, None], (targets.shape[0], 128))], 1
+        jnp.concatenate([targets.astype(jnp.float32), lanes], 1).astype(jnp.bfloat16)
+    )
+    source_terms = lax.optimization_barrier(
+        jnp.stack(
+            [
+                jnp.sum(jnp.square(sources.astype(jnp.float32)), 1) / features,
+                log_source_mass,
+            ]
         )
     )
     for bit in order:
@@ -40,7 +47,7 @@
     logits = products * factor + offset[None, :]
     row_max = jnp.max(logits, 1)
     row_lse = row_max + jnp.log(jnp.sum(jnp.exp(logits - row_max[:, None]), 1))
-    source_dual = log_source_mass - row_lse
+    source_dual = source_terms[1] - row_lse
     columns = logits - pot_f32[None, :] / epsilon + source_dual[:, None]
     col_max = jnp.max(columns, 0)
     col_sum = jnp.sum(jnp.exp(columns - col_max[None, :]), 0)
@@ -48,16 +55,17 @@
     me = lax.axis_index(AXES)
     apart = me ^ jnp.arange(count)
     where = sum(((apart >> bit) & 1) << step for step, bit in enumerate(order))
-    part = jnp.stack([col_max, col_sum]).reshape(2, count, -1)
-    part = jnp.take(part, where, axis=1)
-    part = lax.all_to_all(part, AXES, 1, 1, tiled=True)
-    owned_max = jnp.max(part[0], 0)
-    owned_sum = jnp.sum(part[1] * jnp.exp(part[0] - owned_max[None, :]), 0)
+    choose = (where[:, None] == jnp.arange(count)[None, :]).astype(jnp.float32)
+    part = jnp.stack([col_max.reshape(count, -1), col_sum.reshape(count, -1)], 1)
+    part = jnp.dot(
+        choose, part.reshape(count, -1), precision=lax.Precision.HIGHEST
+    ).reshape(count, 2, -1)
+    part = lax.all_to_all(part, AXES, 0, 0, tiled=True)
+    owned_max = jnp.max(part[:, 0], 0)
+    owned_sum = jnp.sum(part[:, 1] * jnp.exp(part[:, 0] - owned_max[None, :]), 0)
     part = (owned_max, owned_sum)
 
-    source_potential = epsilon * source_dual + jnp.sum(
-        jnp.square(sources.astype(jnp.float32)), 1
-    ) / features
+    source_potential = epsilon * source_dual + source_terms[0]
     target_update = epsilon * (log_target_mass - (part[0] + jnp.log(part[1])))
     return (source_potential, target_update)
 

time: 39.6 us -> 38.5 us (0.972)
  local copies, waits for them, and re-layouts: 2.12 us -> 1.27 us
    gather x1 -> x0, local copies, waits for them, and re-layouts: 0.61 us -> none  [per_device(): part = jnp.take(part, where, axis=1)]
    unnamed x10, local copies, waits for them, and re-layouts: 0.56 us -> 0.05 us
where the time goes in v4:
time: 38.5 us; the launch traced here: 38.3 us
  blocking collectives  13.2 us (34%)
  starting transfers between devices  9.61 us (25%)
  waiting for transfers between devices  8.17 us (21%)
  other arithmetic  4.6 us (12%)
  local copies, waits for them, and re-layouts  1.27 us (3%)
  between operations  0.76 us (2%)
  matrix products  0.69 us (2%)
    all_to_all x1, blocking collectives, per_device(): part = lax.all_to_all(part, AXES, 0, 0, tiled=True)  13.2 us
    ppermute x5, starting transfers between devices, exchange(): return lax.ppermute(x, AXES, route)  9.61 us
    ppermute x5, waiting for transfers between devices, exchange(): return lax.ppermute(x, AXES, route)  8.17 us
    reduce_sum x1, other arithmetic, per_device(): jnp.sum(jnp.square(sources.astype(jnp.float32)), 1) / features  1.59 us
  transfers between devices with their start and end apart: 5, of which 4 were waited for; matrix products, arithmetic and copies ran while one was open for 4% of the time, Pallas kernels for 0%

profile of v4, /device:TPU:0, one launch (start us, length us, event | category | flops | bytes accessed | tf_op | source)
XLA Modules:
  0.0 38.3 jit_solution(6679681228915059186)
XLA Ops:
  0.6 0.0 copy-start.1
  0.6 0.7 %broadcast_in_dim.2 = bf16[8,128]{1,0:T(8,128)(2,1)S(1)} broadcast(bf16[8]{0:T(256)(128)(2,1)} %param.7), dimensions={0} | broadcast | bytes 2064 | tf_op jit(solution)/shard_map/broadcast_in_dim | solution.py:24
  1.4 0.7 %pad_maximum_fusion.3 = bf16[8,640]{1,0:T(8,128)(2,1)S(1)} fusion(bf16[8,128]{1,0:T(8,128)(2,1)S(1)} %broadcast_in_dim.2, bf16[8,512]{1,0:T(8,128)(2,1)} %param.6), kind=kLoop, calls=%fused_computation.28 | loop fusion | flops 20480 | bytes 20480 | tf_op jit(solution)/shard_map/concatenate | solution.py:26
  2.1 4.0 %collective-permute-start = (bf16[8,640]{1,0:T(8,128)(2,1)S(1)}, bf16[8,640]{1,0:T(8,128)(2,1)S(1)}, u32[]{:S(2)}, u32[]{:S(2)}) collective-permute-start(bf16[8,640]{1,0:T(8,128)(2,1)S(1)} %pad_maximum_fusion.3), channel_id=1, source_target_pairs={{0,16},{1,17},{2,18},{3,19},{4,20},{5,21},{6,22},{7,23},{8,24},{9,... | collective-permute-start | bytes 30728 | tf_op jit(solution)/shard_map/ppermute | solution.py:12
  6.1 0.0 copy-start
  6.1 1.6 %multiply_reduce_fusion = f32[1024]{0:T(1024)S(1)} fusion(bf16[1024,512]{1,0:T(8,128)(2,1)} %param.5), kind=kLoop, calls=%fused_computation | loop fusion | flops 1571840 | bytes 1052672 | tf_op jit(solution)/shard_map/reduce_sum | solution.py:31
  7.7 0.0 copy-done.1
  7.7 0.0 collective-permute-done
  7.8 1.9 %collective-permute-start.1 = (bf16[16,640]{1,0:T(8,128)(2,1)S(1)}, bf16[16,640]{1,0:T(8,128)(2,1)S(1)}, u32[]{:S(2)}, u32[]{:S(2)}) collective-permute-start(bf16[16,640]{1,0:T(8,128)(2,1)S(1)} %pad_maximum_fusion.2), channel_id=1, source_target_pairs={{0,8},{1,9},{2,10},{3,11},{4,12},{5,13},{6,14},{7,15},{8,0},{9,1},... | collective-permute-start | bytes 61448 | tf_op jit(solution)/shard_map/ppermute | solution.py:12
  9.7 1.9 %collective-permute-done.1 = bf16[16,640]{1,0:T(8,128)(2,1)S(1)} collective-permute-done((bf16[16,640]{1,0:T(8,128)(2,1)S(1)}, bf16[16,640]{1,0:T(8,128)(2,1)S(1)}, u32[]{:S(2)}, u32[]{:S(2)}) %collective-permute-start.1) | collective-permute-done | bytes 20512 | tf_op jit(solution)/shard_map/ppermute | solution.py:12
  11.6 1.8 %collective-permute-start.2 = (bf16[32,640]{1,0:T(8,128)(2,1)S(1)}, bf16[32,640]{1,0:T(8,128)(2,1)S(1)}, u32[]{:S(2)}, u32[]{:S(2)}) collective-permute-start(bf16[32,640]{1,0:T(8,128)(2,1)S(1)} %pad_maximum_fusion.1), channel_id=1, source_target_pairs={{0,4},{1,5},{2,6},{3,7},{4,0},{5,1},{6,2},{7,3},{8,12},{9,13},{10,... | collective-permute-start | bytes 122888 | tf_op jit(solution)/shard_map/ppermute | solution.py:12
  13.4 2.2 %collective-permute-done.2 = bf16[32,640]{1,0:T(8,128)(2,1)S(1)} collective-permute-done((bf16[32,640]{1,0:T(8,128)(2,1)S(1)}, bf16[32,640]{1,0:T(8,128)(2,1)S(1)}, u32[]{:S(2)}, u32[]{:S(2)}) %collective-permute-start.2) | collective-permute-done | bytes 40992 | tf_op jit(solution)/shard_map/ppermute | solution.py:12
  15.6 1.8 %collective-permute-start.3 = (bf16[64,640]{1,0:T(8,128)(2,1)S(1)}, bf16[64,640]{1,0:T(8,128)(2,1)S(1)}, u32[]{:S(2)}, u32[]{:S(2)}) collective-permute-start(bf16[64,640]{1,0:T(8,128)(2,1)S(1)} %pad_maximum_fusion), channel_id=1, source_target_pairs={{0,2},{1,3},{2,0},{3,1},{4,6},{5,7},{6,4},{7,5},{8,10},{9,11},{10,... | collective-permute-start | bytes 245768 | tf_op jit(solution)/shard_map/ppermute | solution.py:12
  17.5 2.6 %collective-permute-done.3 = bf16[64,640]{1,0:T(8,128)(2,1)S(1)} collective-permute-done((bf16[64,640]{1,0:T(8,128)(2,1)S(1)}, bf16[64,640]{1,0:T(8,128)(2,1)S(1)}, u32[]{:S(2)}, u32[]{:S(2)}) %collective-permute-start.3) | collective-permute-done | bytes 81952 | tf_op jit(solution)/shard_map/ppermute | solution.py:12
  20.2 0.1 collective-permute-start.4
  20.3 1.3 %collective-permute-done.4 = bf16[128,640]{1,0:T(8,128)(2,1)S(1)} collective-permute-done((bf16[128,640]{1,0:T(8,128)(2,1)S(1)}, bf16[128,640]{1,0:T(8,128)(2,1)S(1)}, u32[]{:S(2)}, u32[]{:S(2)}) %collective-permute-start.4) | collective-permute-done | bytes 163872 | tf_op jit(solution)/shard_map/ppermute | solution.py:12
  21.6 0.1 multiply_reduce_fusion.1
  21.8 0.1 multiply_reduce_fusion.2
  21.9 0.0 copy-done
  21.9 0.5 %fusion.12 = (f32[1024]{0:T(1024)S(1)}, f32[256,1024]{1,0:T(8,128)S(1)}) fusion(f32[256]{0:T(256)S(1)} %multiply_subtract_fusion, bf16[1024,512]{1,0:T(8,128)(2,1)S(1)} %copy-done, bf16[256,640]{1,0:T(8,128)(2,1)S(1)} %constant_dynamic-update-slice_fusion.5), kind=kOutput, calls=%fused_computation.43 | convolution fusion | flops 269220864 | bytes 2364416 | tf_op jit(solution)/shard_map/dot_general | solution.py:44
  22.4 0.2 exponential_reduce_fusion.1
  22.6 0.6 %multiply_add_fusion = (f32[1024]{0:T(1024)}, f32[1024]{0:T(1024)S(1)}) fusion(f32[1024]{0:T(1024)S(1)} %bitcast.24, f32[1024]{0:T(1024)S(1)} %bitcast.23, f32[1024]{0:T(1024)S(1)} %get-tuple-element.18, f32[1024]{0:T(1024)S(1)} %exponential_reduce_fusion.1), kind=kLoop, calls=%fused_computation.34 | loop fusion | flops 4096 | bytes 24576 | tf_op jit(solution)/shard_map/add | solution.py:68
  23.2 0.0 copy-start.2
  23.2 0.3 fusion.1
  23.5 0.4 %exponential_reduce_fusion = f32[256]{0:T(256)S(1)} fusion(f32[256,1024]{1,0:T(8,128)S(1)} %get-tuple-element.19, f32[256]{0:T(256)S(1)} %fusion.1, f32[1024]{0:T(1024)S(1)} %get-tuple-element.3, f32[256]{0:T(256)S(1)} %multiply_reduce_fusion.2), kind=kLoop, calls=%fused_computation.3 | loop fusion | flops 1048320 | bytes 1055744 | tf_op jit(solution)/shard_map/reduce_sum | solution.py:53
  23.9 0.1 stack_reshape.6
  23.9 0.1 stack_reshape.7
  24.0 0.1 copy.9
  24.1 0.1 copy.8
  24.2 0.2 fusion.4
  24.4 0.1 copy.10
  24.5 13.2 %all_to_all.5 = f32[32,2,8]{2,1,0:T(2,128)S(1)} all-to-all(f32[32,2,8]{2,1,0:T(2,128)S(1)} %copy.10), channel_id=1, replica_groups=mesh['group'=8,'blk'=4] {'group','blk'}, dimensions={0} | all-to-all | bytes 4096 | tf_op jit(solution)/shard_map/all_to_all | solution.py:63
  37.7 0.0 copy-done.2
  37.7 0.5 %subtract_multiply_fusion = f32[8]{0:T(128)} fusion(f32[8]{0:T(128)S(1)} %copy-done.2, f32[8]{0:T(128)S(1)} %reduce_max.29, f32[8]{0:T(128)S(1)} %multiply_reduce_fusion.3), kind=kLoop, calls=%fused_computation.38 | loop fusion | flops 24 | bytes 128 | tf_op jit(solution)/shard_map/mul | solution.py:69
  (17 shorter events, 0.2 us)
Async XLA Ops:
  0.6 7.1 %copy-start.1 = (f32[1024]{0:T(1024)S(1)}, f32[1024]{0:T(1024)}, u32[]{:S(2)}) copy-start(f32[1024]{0:T(1024)} %param.8) | copy-start | bytes 12292
  2.1 5.7 %collective-permute-start = (bf16[8,640]{1,0:T(8,128)(2,1)S(1)}, bf16[8,640]{1,0:T(8,128)(2,1)S(1)}, u32[]{:S(2)}, u32[]{:S(2)}) collective-permute-start(bf16[8,640]{1,0:T(8,128)(2,1)S(1)} %pad_maximum_fusion.3), channel_id=1, source_target_pairs={{0,16},{1,17},{2,18},{3,19},{4,20},{5,21},{6,22},{7,23},{8,24},{9,... | collective-permute-start | bytes 30728 | tf_op jit(solution)/shard_map/ppermute | solution.py:12
  6.1 15.8 %copy-start = (bf16[1024,512]{1,0:T(8,128)(2,1)S(1)}, bf16[1024,512]{1,0:T(8,128)(2,1)}, u32[]{:S(2)}) copy-start(bf16[1024,512]{1,0:T(8,128)(2,1)} %param.5) | copy-start | bytes 3145732
  7.8 3.8 %collective-permute-start.1 = (bf16[16,640]{1,0:T(8,128)(2,1)S(1)}, bf16[16,640]{1,0:T(8,128)(2,1)S(1)}, u32[]{:S(2)}, u32[]{:S(2)}) collective-permute-start(bf16[16,640]{1,0:T(8,128)(2,1)S(1)} %pad_maximum_fusion.2), channel_id=1, source_target_pairs={{0,8},{1,9},{2,10},{3,11},{4,12},{5,13},{6,14},{7,15},{8,0},{9,1},... | collective-permute-start | bytes 61448 | tf_op jit(solution)/shard_map/ppermute | solution.py:12
  11.6 4.0 %collective-permute-start.2 = (bf16[32,640]{1,0:T(8,128)(2,1)S(1)}, bf16[32,640]{1,0:T(8,128)(2,1)S(1)}, u32[]{:S(2)}, u32[]{:S(2)}) collective-permute-start(bf16[32,640]{1,0:T(8,128)(2,1)S(1)} %pad_maximum_fusion.1), channel_id=1, source_target_pairs={{0,4},{1,5},{2,6},{3,7},{4,0},{5,1},{6,2},{7,3},{8,12},{9,13},{10,... | collective-permute-start | bytes 122888 | tf_op jit(solution)/shard_map/ppermute | solution.py:12
  15.6 4.5 %collective-permute-start.3 = (bf16[64,640]{1,0:T(8,128)(2,1)S(1)}, bf16[64,640]{1,0:T(8,128)(2,1)S(1)}, u32[]{:S(2)}, u32[]{:S(2)}) collective-permute-start(bf16[64,640]{1,0:T(8,128)(2,1)S(1)} %pad_maximum_fusion), channel_id=1, source_target_pairs={{0,2},{1,3},{2,0},{3,1},{4,6},{5,7},{6,4},{7,5},{8,10},{9,11},{10,... | collective-permute-start | bytes 245768 | tf_op jit(solution)/shard_map/ppermute | solution.py:12
  20.2 1.5 %collective-permute-start.4 = (bf16[128,640]{1,0:T(8,128)(2,1)S(1)}, bf16[128,640]{1,0:T(8,128)(2,1)S(1)}, u32[]{:S(2)}, u32[]{:S(2)}) collective-permute-start(bf16[128,640]{1,0:T(8,128)(2,1)S(1)} %get-tuple-element.4), channel_id=1, source_target_pairs={{0,1},{1,0},{2,3},{3,2},{4,5},{5,4},{6,7},{7,6},{8,9},{9,8},{10,11... | collective-permute-start | bytes 491528 | tf_op jit(solution)/shard_map/ppermute | solution.py:12
  23.2 14.5 %copy-start.2 = (f32[8]{0:T(128)S(1)}, f32[8]{0:T(128)}, u32[]{:S(2)}) copy-start(f32[8]{0:T(128)} %param.9) | copy-start | bytes 100

commit v5 on v4

--- a/solution.py
+++ b/solution.py
@@ -21,9 +21,13 @@
     features = sources.shape[1]
     factor = 2.0 / (features * epsilon)
 
-    lanes = jnp.broadcast_to(target_potential.astype(jnp.float32)[:, None], (targets.shape[0], 128))
+    lane = lax.broadcasted_iota(jnp.int32, (targets.shape[0], features + 128), 1)
     held = lax.optimization_barrier(
-        jnp.concatenate([targets.astype(jnp.float32), lanes], 1).astype(jnp.bfloat16)
+        jnp.where(
+            lane < features,
+            jnp.pad(targets, ((0, 0), (0, 128))),
+            target_potential[:, None],
+        )
     )
     source_terms = lax.optimization_barrier(
         jnp.stack(
@@ -33,20 +37,30 @@
             ]
         )
     )
-    for bit in order:
+    for bit in order[:-1]:
         held = jnp.concatenate([held, exchange(held, bit, count)], 0)
-    held_rows, held_pots = held[:, :features], held[:, features]
+    last = exchange(held, order[-1], count)
 
-    pot_f32 = held_pots.astype(jnp.float32)
-    offset = pot_f32 / epsilon - jnp.sum(jnp.square(held_rows.astype(jnp.float32)), 1) / (
-        features * epsilon
+    def row_pass(block):
+        pots = block[:, features].astype(jnp.float32)
+        offset = pots / epsilon - jnp.sum(jnp.square(block[:, :features].astype(jnp.float32)), 1) / (
+            features * epsilon
+        )
+        products = lax.dot_general(
+            sources, block[:, :features], (((1,), (1,)), ((), ())),
+            preferred_element_type=jnp.float32,
+        )
+        logits = products * factor + offset[None, :]
+        block_max = jnp.max(logits, 1)
+        return logits, pots, block_max, jnp.sum(jnp.exp(logits - block_max[:, None]), 1)
+
+    first, second = row_pass(held), row_pass(last)
+    row_max = jnp.maximum(first[2], second[2])
+    row_lse = row_max + jnp.log(
+        first[3] * jnp.exp(first[2] - row_max) + second[3] * jnp.exp(second[2] - row_max)
     )
-    products = lax.dot_general(
-        sources, held_rows, (((1,), (1,)), ((), ())), preferred_element_type=jnp.float32
-    )
-    logits = products * factor + offset[None, :]
-    row_max = jnp.max(logits, 1)
-    row_lse = row_max + jnp.log(jnp.sum(jnp.exp(logits - row_max[:, None]), 1))
+    logits = jnp.concatenate([first[0], second[0]], 1)
+    pot_f32 = jnp.concatenate([first[1], second[1]], 0)
     source_dual = source_terms[1] - row_lse
     columns = logits - pot_f32[None, :] / epsilon + source_dual[:, None]
     col_max = jnp.max(columns, 0)

time: 38.5 us -> 37.8 us (0.982)
  waiting for transfers between devices: 8.17 us -> 7.27 us
  local copies, waits for them, and re-layouts: 1.27 us -> 0.5 us
  matrix products: 0.69 us -> 1.18 us
    ppermute x5, waiting for transfers between devices: 8.17 us -> 7.27 us  [exchange(): return lax.ppermute(x, AXES, route)]
    select_n x0 -> x1, other arithmetic: none -> 0.86 us  [per_device(): jnp.where(lane < features, jnp.pad(targets, ((0, 0), (0, 128))), target_p...]
    broadcast_in_dim x1 -> x0, local copies, waits for them, and re-layouts: 0.73 us -> none  [per_device(): jnp.broadcast_to(target_potential.astype(jnp.float32)[:, None], (targets....]
    concatenate x1 -> x0, other arithmetic: 0.7 us -> none  [per_device(): jnp.concatenate([targets.astype(jnp.float32), lanes], 1)]
    dot_general x1 -> x2, matrix products: 0.49 us -> 0.98 us  [row_pass(): lax.dot_general(sources, block[:, :features], (((1,), (1,)), ((), ())), p...]
  transfers between devices with their start and end apart: 5 -> 5, of which waited for: 4 -> 5; matrix products, arithmetic and copies ran while one was open for 4% -> 6% of each run, Pallas kernels for 0% -> 0%
where the time goes in v5:
time: 37.8 us; the launch traced here: 37.6 us
  blocking collectives  13.2 us (35%)
  starting transfers between devices  9.72 us (26%)
  waiting for transfers between devices  7.27 us (19%)
  other arithmetic  4.9 us (13%)
  matrix products  1.18 us (3%)
  between operations  0.81 us (2%)
  local copies, waits for them, and re-layouts  0.5 us (1%)
    all_to_all x1, blocking collectives, per_device(): part = lax.all_to_all(part, AXES, 0, 0, tiled=True)  13.2 us
    ppermute x5, starting transfers between devices, exchange(): return lax.ppermute(x, AXES, route)  9.72 us
    ppermute x5, waiting for transfers between devices, exchange(): return lax.ppermute(x, AXES, route)  7.27 us
    reduce_sum x1, other arithmetic, per_device(): jnp.sum(jnp.square(sources.astype(jnp.float32)), 1) / features  1.5 us
    dot_general x2, matrix products, row_pass(): lax.dot_general(sources, block[:, :features], (((1,), (1,)), ((), ())), p...  0.98 us
    select_n x1, other arithmetic, per_device(): jnp.where(lane < features, jnp.pad(targets, ((0, 0), (0, 128))), target_p...  0.86 us
  transfers between devices with their start and end apart: 5, of which 5 were waited for; matrix products, arithmetic and copies ran while one was open for 6% of the time, Pallas kernels for 0%

profile of v5, /device:TPU:0, one launch (start us, length us, event | category | flops | bytes accessed | tf_op | source)
XLA Modules:
  0.0 37.6 jit_solution(17851978876996668758)
XLA Ops:
  0.6 0.0 copy-start
  0.6 0.0 copy-start.1
  0.7 0.9 %pad_select_fusion = bf16[8,640]{1,0:T(8,128)(2,1)S(1)} fusion(bf16[8,512]{1,0:T(8,128)(2,1)} %param.6, pred[640]{0:T(1024)(128)(4,1)S(1)} %iota_compare_fusion.1, bf16[8]{0:T(256)(128)(2,1)} %param.7), kind=kLoop, calls=%fused_computation.29 | loop fusion | flops 5120 | bytes 19088 | tf_op jit(solution)/shard_map/jit(_where)/select_n | solution.py:26
  1.5 4.0 %collective-permute-start = (bf16[8,640]{1,0:T(8,128)(2,1)S(1)}, bf16[8,640]{1,0:T(8,128)(2,1)S(1)}, u32[]{:S(2)}, u32[]{:S(2)}) collective-permute-start(bf16[8,640]{1,0:T(8,128)(2,1)S(1)} %pad_select_fusion), channel_id=1, source_target_pairs={{0,16},{1,17},{2,18},{3,19},{4,20},{5,21},{6,22},{7,23},{8,24},{9,... | collective-permute-start | bytes 30728 | tf_op jit(solution)/shard_map/ppermute | solution.py:12
  5.6 1.5 %multiply_reduce_fusion = f32[1024]{0:T(1024)S(1)} fusion(bf16[1024,512]{1,0:T(8,128)(2,1)} %param.5), kind=kLoop, calls=%fused_computation | loop fusion | flops 1571840 | bytes 1052672 | tf_op jit(solution)/shard_map/reduce_sum | solution.py:35
  7.1 0.0 copy-done.1
  7.1 0.1 collective-permute-done
  7.2 1.9 %collective-permute-start.1 = (bf16[16,640]{1,0:T(8,128)(2,1)S(1)}, bf16[16,640]{1,0:T(8,128)(2,1)S(1)}, u32[]{:S(2)}, u32[]{:S(2)}) collective-permute-start(bf16[16,640]{1,0:T(8,128)(2,1)S(1)} %pad_maximum_fusion.2), channel_id=1, source_target_pairs={{0,8},{1,9},{2,10},{3,11},{4,12},{5,13},{6,14},{7,15},{8,0},{9,1},... | collective-permute-start | bytes 61448 | tf_op jit(solution)/shard_map/ppermute | solution.py:12
  9.1 1.9 %collective-permute-done.1 = bf16[16,640]{1,0:T(8,128)(2,1)S(1)} collective-permute-done((bf16[16,640]{1,0:T(8,128)(2,1)S(1)}, bf16[16,640]{1,0:T(8,128)(2,1)S(1)}, u32[]{:S(2)}, u32[]{:S(2)}) %collective-permute-start.1) | collective-permute-done | bytes 20512 | tf_op jit(solution)/shard_map/ppermute | solution.py:12
  11.0 1.8 %collective-permute-start.2 = (bf16[32,640]{1,0:T(8,128)(2,1)S(1)}, bf16[32,640]{1,0:T(8,128)(2,1)S(1)}, u32[]{:S(2)}, u32[]{:S(2)}) collective-permute-start(bf16[32,640]{1,0:T(8,128)(2,1)S(1)} %pad_maximum_fusion.1), channel_id=1, source_target_pairs={{0,4},{1,5},{2,6},{3,7},{4,0},{5,1},{6,2},{7,3},{8,12},{9,13},{10,... | collective-permute-start | bytes 122888 | tf_op jit(solution)/shard_map/ppermute | solution.py:12
  12.8 2.2 %collective-permute-done.2 = bf16[32,640]{1,0:T(8,128)(2,1)S(1)} collective-permute-done((bf16[32,640]{1,0:T(8,128)(2,1)S(1)}, bf16[32,640]{1,0:T(8,128)(2,1)S(1)}, u32[]{:S(2)}, u32[]{:S(2)}) %collective-permute-start.2) | collective-permute-done | bytes 40992 | tf_op jit(solution)/shard_map/ppermute | solution.py:12
  15.0 1.9 %collective-permute-start.3 = (bf16[64,640]{1,0:T(8,128)(2,1)S(1)}, bf16[64,640]{1,0:T(8,128)(2,1)S(1)}, u32[]{:S(2)}, u32[]{:S(2)}) collective-permute-start(bf16[64,640]{1,0:T(8,128)(2,1)S(1)} %pad_maximum_fusion), channel_id=1, source_target_pairs={{0,2},{1,3},{2,0},{3,1},{4,6},{5,7},{6,4},{7,5},{8,10},{9,11},{10,... | collective-permute-start | bytes 245768 | tf_op jit(solution)/shard_map/ppermute | solution.py:12
  16.9 2.6 %collective-permute-done.3 = bf16[64,640]{1,0:T(8,128)(2,1)S(1)} collective-permute-done((bf16[64,640]{1,0:T(8,128)(2,1)S(1)}, bf16[64,640]{1,0:T(8,128)(2,1)S(1)}, u32[]{:S(2)}, u32[]{:S(2)}) %collective-permute-start.3) | collective-permute-done | bytes 81952 | tf_op jit(solution)/shard_map/ppermute | solution.py:12
  19.6 0.1 collective-permute-start.4
  19.6 0.1 convert_reduce_fusion.1
  19.7 0.1 multiply_reduce_fusion.2
  19.9 0.0 copy-done
  19.9 0.5 %fusion.18 = (f32[1024]{0:T(1024)S(1)}, f32[128,1024]{1,0:T(8,128)S(1)}) fusion(f32[128]{0:T(128)S(1)} %multiply_subtract_fusion.1, bf16[1024,512]{1,0:T(8,128)(2,1)S(1)} %copy-done, bf16[128,640]{1,0:T(8,128)(2,1)S(1)} %constant_dynamic-update-slice_fusion), kind=kOutput, calls=%fused_computation.51 | convolution fusion | flops 134609920 | bytes 1708544 | tf_op jit(solution)/shard_map/dot_general | solution.py:49
  20.4 0.1 exponential_reduce_fusion.2
  20.5 0.5 %collective-permute-done.4 = bf16[128,640]{1,0:T(8,128)(2,1)S(1)} collective-permute-done((bf16[128,640]{1,0:T(8,128)(2,1)S(1)}, bf16[128,640]{1,0:T(8,128)(2,1)S(1)}, u32[]{:S(2)}, u32[]{:S(2)}) %collective-permute-start.4) | collective-permute-done | bytes 163872 | tf_op jit(solution)/shard_map/ppermute | solution.py:12
  21.0 0.1 convert_reduce_fusion
  21.1 0.1 multiply_reduce_fusion.1
  21.3 0.5 %fusion.17 = (f32[1024]{0:T(1024)S(1)}, f32[128,1024]{1,0:T(8,128)S(1)}) fusion(f32[128]{0:T(128)S(1)} %multiply_subtract_fusion, bf16[1024,512]{1,0:T(8,128)(2,1)S(1)} %copy-done, bf16[128,640]{1,0:T(8,128)(2,1)S(1)} %collective-permute-done.4), kind=kOutput, calls=%fused_computation.50 | convolution fusion | flops 134609920 | bytes 1708544 | tf_op jit(solution)/shard_map/dot_general | solution.py:49
  21.8 0.1 exponential_reduce_fusion.1
  21.9 0.6 %multiply_add_fusion = (f32[1024]{0:T(1024)}, f32[1024]{0:T(1024)S(1)}) fusion(f32[1024]{0:T(1024)S(1)} %bitcast.33, f32[1024]{0:T(1024)S(1)} %bitcast.32, f32[1024]{0:T(1024)S(1)} %exponential_reduce_fusion.1, f32[1024]{0:T(1024)S(1)} %get-tuple-element.8, f32[1024]{0:T(1024)S(1)} %exponential_reduce_fusion.2, f32[1024]{0:T(1024)S(1)} %get-tuple-element.10), kind=kLoop, calls=%fused_computation.35 | loop fusion | flops 10240 | bytes 32768 | tf_op jit(solution)/shard_map/add | solution.py:82
  22.5 0.0 copy-start.2
  22.5 0.3 fusion.3
  22.7 0.4 %exponential_reduce_fusion = f32[256]{0:T(256)S(1)} fusion(f32[1024,128]{0,1:T(8,128)S(1)} %bitcast.27, f32[1024,128]{0,1:T(8,128)S(1)} %bitcast.25, f32[256]{0:T(256)S(1)} %fusion.3, f32[1024]{0:T(1024)S(1)} %get-tuple-element.3, f32[256]{0:T(256)S(1)} %maximum_multiply_fusion), kind=kLoop, calls=%fused_computation.7 | loop fusion | flops 1310464 | bytes 1055744 | tf_op jit(solution)/shard_map/reduce_sum | solution.py:67
  23.1 0.1 stack_reshape.6
  23.2 0.1 stack_reshape.7
  23.3 0.1 copy.9
  23.4 0.1 copy.8
  23.4 0.2 fusion.7
  23.7 0.1 copy.10
  23.8 13.2 %all_to_all.5 = f32[32,2,8]{2,1,0:T(2,128)S(1)} all-to-all(f32[32,2,8]{2,1,0:T(2,128)S(1)} %copy.10), channel_id=1, replica_groups=mesh['group'=8,'blk'=4] {'group','blk'}, dimensions={0} | all-to-all | bytes 4096 | tf_op jit(solution)/shard_map/all_to_all | solution.py:77
  37.1 0.0 copy-done.2
  37.1 0.5 %subtract_multiply_fusion = f32[8]{0:T(128)} fusion(f32[8]{0:T(128)S(1)} %copy-done.2, f32[8]{0:T(128)S(1)} %reduce_max.39, f32[8]{0:T(128)S(1)} %multiply_reduce_fusion.3), kind=kLoop, calls=%fused_computation.43 | loop fusion | flops 24 | bytes 128 | tf_op jit(solution)/shard_map/mul | solution.py:83
  (19 shorter events, 0.2 us)
Async XLA Ops:
  0.6 19.2 %copy-start = (bf16[1024,512]{1,0:T(8,128)(2,1)S(1)}, bf16[1024,512]{1,0:T(8,128)(2,1)}, u32[]{:S(2)}) copy-start(bf16[1024,512]{1,0:T(8,128)(2,1)} %param.5) | copy-start | bytes 3145732
  0.6 6.4 %copy-start.1 = (f32[1024]{0:T(1024)S(1)}, f32[1024]{0:T(1024)}, u32[]{:S(2)}) copy-start(f32[1024]{0:T(1024)} %param.8) | copy-start | bytes 12292
  1.5 5.7 %collective-permute-start = (bf16[8,640]{1,0:T(8,128)(2,1)S(1)}, bf16[8,640]{1,0:T(8,128)(2,1)S(1)}, u32[]{:S(2)}, u32[]{:S(2)}) collective-permute-start(bf16[8,640]{1,0:T(8,128)(2,1)S(1)} %pad_select_fusion), channel_id=1, source_target_pairs={{0,16},{1,17},{2,18},{3,19},{4,20},{5,21},{6,22},{7,23},{8,24},{9,... | collective-permute-start | bytes 30728 | tf_op jit(solution)/shard_map/ppermute | solution.py:12
  7.2 3.8 %collective-permute-start.1 = (bf16[16,640]{1,0:T(8,128)(2,1)S(1)}, bf16[16,640]{1,0:T(8,128)(2,1)S(1)}, u32[]{:S(2)}, u32[]{:S(2)}) collective-permute-start(bf16[16,640]{1,0:T(8,128)(2,1)S(1)} %pad_maximum_fusion.2), channel_id=1, source_target_pairs={{0,8},{1,9},{2,10},{3,11},{4,12},{5,13},{6,14},{7,15},{8,0},{9,1},... | collective-permute-start | bytes 61448 | tf_op jit(solution)/shard_map/ppermute | solution.py:12
  11.0 4.0 %collective-permute-start.2 = (bf16[32,640]{1,0:T(8,128)(2,1)S(1)}, bf16[32,640]{1,0:T(8,128)(2,1)S(1)}, u32[]{:S(2)}, u32[]{:S(2)}) collective-permute-start(bf16[32,640]{1,0:T(8,128)(2,1)S(1)} %pad_maximum_fusion.1), channel_id=1, source_target_pairs={{0,4},{1,5},{2,6},{3,7},{4,0},{5,1},{6,2},{7,3},{8,12},{9,13},{10,... | collective-permute-start | bytes 122888 | tf_op jit(solution)/shard_map/ppermute | solution.py:12
  15.0 4.5 %collective-permute-start.3 = (bf16[64,640]{1,0:T(8,128)(2,1)S(1)}, bf16[64,640]{1,0:T(8,128)(2,1)S(1)}, u32[]{:S(2)}, u32[]{:S(2)}) collective-permute-start(bf16[64,640]{1,0:T(8,128)(2,1)S(1)} %pad_maximum_fusion), channel_id=1, source_target_pairs={{0,2},{1,3},{2,0},{3,1},{4,6},{5,7},{6,4},{7,5},{8,10},{9,11},{10,... | collective-permute-start | bytes 245768 | tf_op jit(solution)/shard_map/ppermute | solution.py:12
  19.6 1.5 %collective-permute-start.4 = (bf16[128,640]{1,0:T(8,128)(2,1)S(1)}, bf16[128,640]{1,0:T(8,128)(2,1)S(1)}, u32[]{:S(2)}, u32[]{:S(2)}) collective-permute-start(bf16[128,640]{1,0:T(8,128)(2,1)S(1)} %constant_dynamic-update-slice_fusion), channel_id=1, source_target_pairs={{0,1},{1,0},{2,3},{3,2},{4,5},{5,4},{6,7},{7,6},{8,9},{9,8},{10,11... | collective-permute-start | bytes 491528 | tf_op jit(solution)/shard_map/ppermute | solution.py:12
  22.5 14.6 %copy-start.2 = (f32[8]{0:T(128)S(1)}, f32[8]{0:T(128)}, u32[]{:S(2)}) copy-start(f32[8]{0:T(128)} %param.9) | copy-start | bytes 100

commit v6 on v5

v6 whole, which is shorter than its diff:
```python
import functools

import jax
import jax.numpy as jnp
from jax import lax
from jax.sharding import PartitionSpec as P
from jax.experimental import pallas as pl
from jax.experimental.pallas import tpu as pltpu

epsilon = 0.05
AXES = ("group", "blk")


def exchange(x, bit, count):
    route = [(i, i ^ (1 << bit)) for i in range(count)]
    return lax.ppermute(x, AXES, route)


def tail(features, factor, src_ref, early_ref, last_ref, logits_ref, stats_ref, terms_ref,
         col_ref, pot_ref):
    block = last_ref[...]
    rows = block[:, :features]
    pots = block[:, features:features + 1].astype(jnp.float32)
    offset = pots / epsilon - jnp.sum(jnp.square(rows.astype(jnp.float32)), 1, keepdims=True) / (
        features * epsilon
    )
    late = lax.dot_general(
        rows, src_ref[...], (((1,), (1,)), ((), ())), preferred_element_type=jnp.float32
    ) * factor + offset
    late_max = jnp.max(late, 0, keepdims=True)
    late_sum = jnp.sum(jnp.exp(late - late_max), 0, keepdims=True)
    early_max = stats_ref[0:1, :]
    row_max = jnp.maximum(early_max, late_max)
    row_lse = row_max + jnp.log(
        stats_ref[1:2, :] * jnp.exp(early_max - row_max) + late_sum * jnp.exp(late_max - row_max)
    )
    dual = terms_ref[1:2, :] - row_lse
    pot_ref[...] = epsilon * dual + terms_ref[0:1, :]
    half = block.shape[0]
    for start, logits, block_pots in (
        (0, logits_ref[...], early_ref[:, features:features + 1].astype(jnp.float32)),
        (half, late, pots),
    ):
        column = logits - block_pots / epsilon + dual
        col_max = jnp.max(column, 1, keepdims=True)
        col_ref[start:start + half, 0:1] = col_max
        col_ref[start:start + half, 1:2] = jnp.sum(jnp.exp(column - col_max), 1, keepdims=True)

def per_device(sources, targets, target_potential, log_source_mass, log_target_mass):
    count = lax.axis_size("group") * lax.axis_size("blk")
    levels = count.bit_length() - 1
    if (1 << levels) != count:
        raise ValueError("count not pow2")
    order = list(reversed(range(levels)))
    features = sources.shape[1]
    factor = 2.0 / (features * epsilon)

    lane = lax.broadcasted_iota(jnp.int32, (targets.shape[0], features + 128), 1)
    held = lax.optimization_barrier(
        jnp.where(
            lane < features,
            jnp.pad(targets, ((0, 0), (0, 128))),
            target_potential[:, None],
        )
    )
    source_terms = lax.optimization_barrier(
        jnp.stack(
            [
                jnp.sum(jnp.square(sources.astype(jnp.float32)), 1) / features,
                log_source_mass,
            ]
        )
    )
    for bit in order[:-1]:
        held = jnp.concatenate([held, exchange(held, bit, count)], 0)
    last = exchange(held, order[-1], count)

    early_rows = held[:, :features]
    early_pots = held[:, features].astype(jnp.float32)
    early_offset = early_pots / epsilon - jnp.sum(
        jnp.square(early_rows.astype(jnp.float32)), 1
    ) / (features * epsilon)
    early_logits = lax.dot_general(
        early_rows, sources, (((1,), (1,)), ((), ())), preferred_element_type=jnp.float32
    ) * factor + early_offset[:, None]
    early_max = jnp.max(early_logits, 0)
    early_stats = jnp.stack([early_max, jnp.sum(jnp.exp(early_logits - early_max[None, :]), 0)])

    half = held.shape[0]
    vmem = pl.BlockSpec(memory_space=pltpu.VMEM)
    columns, source_potential = pl.pallas_call(
        functools.partial(tail, features, factor),
        out_shape=(
            jax.ShapeDtypeStruct((2 * half, 2), jnp.float32),
            jax.ShapeDtypeStruct((1, sources.shape[0]), jnp.float32),
        ),
        in_specs=[vmem] * 6,
        out_specs=(vmem, vmem),
        compiler_params=pltpu.CompilerParams(vmem_limit_bytes=24 * 1024 * 1024),
    )(sources, held, last, early_logits, early_stats, source_terms)
    source_potential = source_potential.reshape(-1)

    me = lax.axis_index(AXES)
    width = columns.shape[0] // count
    apart = me ^ (jnp.arange(count * width) // width)
    where = sum(((apart >> bit) & 1) << step for step, bit in enumerate(order))
    where = where * width + jnp.arange(count * width) % width
    choose = (where[:, None] == jnp.arange(count * width)[None, :]).astype(jnp.float32)
    part = jnp.dot(choose, columns, precision=lax.Precision.HIGHEST).reshape(count, width, 2)
    part = lax.all_to_all(part, AXES, 0, 0, tiled=True)
    owned_max = jnp.max(part[:, :, 0], 0)
    owned_sum = jnp.sum(part[:, :, 1] * jnp.exp(part[:, :, 0] - owned_max[None, :]), 0)
    part = (owned_max, owned_sum)

    target_update = epsilon * (log_target_mass - (part[0] + jnp.log(part[1])))
    return (source_potential, target_update)


def solution(mesh):
    return jax.shard_map(
        per_device,
        mesh=mesh,
        in_specs=(
            P(AXES, None),
            P(AXES, None),
            P(AXES),
            P(AXES),
            P(AXES),
        ),
        out_specs=(P(AXES), P(AXES)),
        check_vma=False,
    )
```

time: 37.8 us -> 36.9 us (0.976)
  other arithmetic: 4.9 us -> 3.3 us
  Pallas kernels: 0 us -> 1.29 us
  matrix products: 1.18 us -> 0.77 us
    pallas_call x0 -> x1, Pallas kernels: none -> 1.29 us  [per_device(): pl.pallas_call(functools.partial(tail, features, factor), out_shape=(jax....]
    reduce_sum x6 -> x3, other arithmetic: 0.85 us -> 0.23 us  [the longest x1 0.11 us: per_device(): jnp.sum(jnp.square(early_rows.astype(jnp.float32)), 1)]
    add x2 -> x1, other arithmetic: 0.63 us -> 0.01 us  [per_device(): where = where * width + jnp.arange(count * width) % width]
    dot_general x3 -> x2, matrix products: 1.18 us -> 0.77 us  [the longest x1 0.49 us: per_device(): lax.dot_general(early_rows, sources, (((1,), (1,)), ((), ())), preferred_...]
where the time goes in v6:
time: 36.9 us; the launch traced here: 36.7 us
  blocking collectives  13.2 us (36%)
  starting transfers between devices  9.74 us (26%)
  waiting for transfers between devices  7.23 us (20%)
  other arithmetic  3.3 us (9%)
  Pallas kernels  1.29 us (3%)
  between operations  0.79 us (2%)
  matrix products  0.77 us (2%)
    all_to_all x1, blocking collectives, per_device(): part = lax.all_to_all(part, AXES, 0, 0, tiled=True)  13.2 us
    ppermute x5, starting transfers between devices, exchange(): return lax.ppermute(x, AXES, route)  9.74 us
    ppermute x5, waiting for transfers between devices, exchange(): return lax.ppermute(x, AXES, route)  7.23 us
    reduce_sum x1, other arithmetic, per_device(): jnp.sum(jnp.square(sources.astype(jnp.float32)), 1) / features  1.5 us
    pallas_call x1, Pallas kernels, per_device(): pl.pallas_call(functools.partial(tail, features, factor), out_shape=(jax....  1.29 us
    select_n x1, other arithmetic, per_device(): jnp.where(lane < features, jnp.pad(targets, ((0, 0), (0, 128))), target_p...  0.86 us
  transfers between devices with their start and end apart: 5, of which 5 were waited for; matrix products, arithmetic and copies ran while one was open for 6% of the time, Pallas kernels for 0%

profile of v6, /device:TPU:0, one launch (start us, length us, event | category | flops | bytes accessed | tf_op | source)
XLA Modules:
  0.0 36.7 jit_solution(11387552096760262657)
XLA Ops:
  0.6 0.0 copy-start
  0.6 0.0 copy-start.1
  0.7 0.9 %pad_select_fusion = bf16[8,640]{1,0:T(8,128)(2,1)S(1)} fusion(bf16[8,512]{1,0:T(8,128)(2,1)} %param.6, pred[640]{0:T(1024)(128)(4,1)S(1)} %iota_compare_fusion.2, bf16[8]{0:T(256)(128)(2,1)} %param.7), kind=kLoop, calls=%fused_computation.19 | loop fusion | flops 5120 | bytes 19088 | tf_op jit(solution)/shard_map/jit(_where)/select_n | solution.py:60
  1.5 4.0 %collective-permute-start = (bf16[8,640]{1,0:T(8,128)(2,1)S(1)}, bf16[8,640]{1,0:T(8,128)(2,1)S(1)}, u32[]{:S(2)}, u32[]{:S(2)}) collective-permute-start(bf16[8,640]{1,0:T(8,128)(2,1)S(1)} %pad_select_fusion), channel_id=1, source_target_pairs={{0,16},{1,17},{2,18},{3,19},{4,20},{5,21},{6,22},{7,23},{8,24},{9,... | collective-permute-start | bytes 30728 | tf_op jit(solution)/shard_map/ppermute | solution.py:16
  5.6 1.5 %multiply_reduce_fusion = f32[1024]{0:T(1024)S(1)} fusion(bf16[1024,512]{1,0:T(8,128)(2,1)} %src_ref.1), kind=kLoop, calls=%fused_computation | loop fusion | flops 1571840 | bytes 1052672 | tf_op jit(solution)/shard_map/reduce_sum | solution.py:69
  7.1 0.0 copy-done.1
  7.1 0.1 collective-permute-done
  7.2 1.9 %collective-permute-start.1 = (bf16[16,640]{1,0:T(8,128)(2,1)S(1)}, bf16[16,640]{1,0:T(8,128)(2,1)S(1)}, u32[]{:S(2)}, u32[]{:S(2)}) collective-permute-start(bf16[16,640]{1,0:T(8,128)(2,1)S(1)} %pad_maximum_fusion.2), channel_id=1, source_target_pairs={{0,8},{1,9},{2,10},{3,11},{4,12},{5,13},{6,14},{7,15},{8,0},{9,1},... | collective-permute-start | bytes 61448 | tf_op jit(solution)/shard_map/ppermute | solution.py:16
  9.1 1.9 %collective-permute-done.1 = bf16[16,640]{1,0:T(8,128)(2,1)S(1)} collective-permute-done((bf16[16,640]{1,0:T(8,128)(2,1)S(1)}, bf16[16,640]{1,0:T(8,128)(2,1)S(1)}, u32[]{:S(2)}, u32[]{:S(2)}) %collective-permute-start.1) | collective-permute-done | bytes 20512 | tf_op jit(solution)/shard_map/ppermute | solution.py:16
  11.0 1.8 %collective-permute-start.2 = (bf16[32,640]{1,0:T(8,128)(2,1)S(1)}, bf16[32,640]{1,0:T(8,128)(2,1)S(1)}, u32[]{:S(2)}, u32[]{:S(2)}) collective-permute-start(bf16[32,640]{1,0:T(8,128)(2,1)S(1)} %pad_maximum_fusion.1), channel_id=1, source_target_pairs={{0,4},{1,5},{2,6},{3,7},{4,0},{5,1},{6,2},{7,3},{8,12},{9,13},{10,... | collective-permute-start | bytes 122888 | tf_op jit(solution)/shard_map/ppermute | solution.py:16
  12.8 2.2 %collective-permute-done.2 = bf16[32,640]{1,0:T(8,128)(2,1)S(1)} collective-permute-done((bf16[32,640]{1,0:T(8,128)(2,1)S(1)}, bf16[32,640]{1,0:T(8,128)(2,1)S(1)}, u32[]{:S(2)}, u32[]{:S(2)}) %collective-permute-start.2) | collective-permute-done | bytes 40992 | tf_op jit(solution)/shard_map/ppermute | solution.py:16
  15.0 1.9 %collective-permute-start.3 = (bf16[64,640]{1,0:T(8,128)(2,1)S(1)}, bf16[64,640]{1,0:T(8,128)(2,1)S(1)}, u32[]{:S(2)}, u32[]{:S(2)}) collective-permute-start(bf16[64,640]{1,0:T(8,128)(2,1)S(1)} %pad_maximum_fusion), channel_id=1, source_target_pairs={{0,2},{1,3},{2,0},{3,1},{4,6},{5,7},{6,4},{7,5},{8,10},{9,11},{10,... | collective-permute-start | bytes 245768 | tf_op jit(solution)/shard_map/ppermute | solution.py:16
  16.9 2.6 %collective-permute-done.3 = bf16[64,640]{1,0:T(8,128)(2,1)S(1)} collective-permute-done((bf16[64,640]{1,0:T(8,128)(2,1)S(1)}, bf16[64,640]{1,0:T(8,128)(2,1)S(1)}, u32[]{:S(2)}, u32[]{:S(2)}) %collective-permute-start.3) | collective-permute-done | bytes 81952 | tf_op jit(solution)/shard_map/ppermute | solution.py:16
  19.5 0.1 multiply_reduce_fusion.1
  19.7 0.1 collective-permute-start.4
  19.7 0.1 copy.12
  19.9 0.1 subtract_reduce_fusion
  20.0 0.0 copy-done
  20.0 0.5 %fusion.9 = (f32[1024]{0:T(1024)S(1)}, f32[128,1024]{1,0:T(8,128)S(1)}) fusion(f32[128]{0:T(128)S(1)} %subtract_reduce_fusion, bf16[1024,512]{1,0:T(8,128)(2,1)S(1)} %copy-done, bf16[128,640]{1,0:T(8,128)(2,1)S(1)} %constant_dynamic-update-slice_fusion.early_ref), kind=kOutput, calls=%fused_computation.36 | convolution fusion | flops 134609920 | bytes 1708544 | tf_op jit(solution)/shard_map/dot_general | solution.py:83
  20.5 0.1 exponential_reduce_fusion
  20.6 0.0 copy-start.2
  20.6 0.5 %collective-permute-done.4.last_ref = bf16[128,640]{1,0:T(8,128)(2,1)S(1)} collective-permute-done((bf16[128,640]{1,0:T(8,128)(2,1)S(1)}, bf16[128,640]{1,0:T(8,128)(2,1)S(1)}, u32[]{:S(2)}, u32[]{:S(2)}) %collective-permute-start.4) | collective-permute-done | bytes 163872 | tf_op jit(solution)/shard_map/ppermute | solution.py:16
  21.1 1.3 %shard_map.68 = (f32[256,2]{1,0:T(8,128)S(1)}, f32[1,1024]{1,0:T(1,128)}) custom-call(bf16[1024,512]{1,0:T(8,128)(2,1)S(1)} %copy-done, bf16[128,640]{1,0:T(8,128)(2,1)S(1)} %constant_dynamic-update-slice_fusion.early_ref, bf16[128,640]{1,0:T(8,128)(2,1)S(1)} %collective-permute-done.4.last_ref, f32[128,1024]{1,0:T(8,128)S(1)} %get-tuple-element.9.logits_ref, ...), custom_call_target="tpu_custom_call" | custom-call | tf_op jit(solution)/shard_map/pallas_call | solution.py:91
  22.4 0.3 fusion.1
  22.7 0.1 reshape.76
  22.9 13.2 %all_to_all.5 = f32[32,8,2]{1,2,0:T(2,128)S(1)} all-to-all(f32[32,8,2]{1,2,0:T(2,128)S(1)} %copy.13), channel_id=1, replica_groups=mesh['group'=8,'blk'=4] {'group','blk'}, dimensions={0} | all-to-all | bytes 4096 | tf_op jit(solution)/shard_map/all_to_all | solution.py:110
  36.2 0.0 copy-done.2
  36.2 0.5 %subtract_multiply_fusion = f32[8]{0:T(128)} fusion(f32[8]{0:T(128)S(1)} %copy-done.2, f32[8]{0:T(128)S(1)} %reduce_max.19, f32[8]{0:T(128)S(1)} %multiply_reduce_fusion.2), kind=kLoop, calls=%fused_computation.33 | loop fusion | flops 24 | bytes 128 | tf_op jit(solution)/shard_map/mul | solution.py:115
  (18 shorter events, 0.2 us)
Async XLA Ops:
  0.6 19.3 %copy-start = (bf16[1024,512]{1,0:T(8,128)(2,1)S(1)}, bf16[1024,512]{1,0:T(8,128)(2,1)}, u32[]{:S(2)}) copy-start(bf16[1024,512]{1,0:T(8,128)(2,1)} %src_ref.1) | copy-start | bytes 3145732
  0.6 6.4 %copy-start.1 = (f32[1024]{0:T(1024)S(1)}, f32[1024]{0:T(1024)}, u32[]{:S(2)}) copy-start(f32[1024]{0:T(1024)} %param.8) | copy-start | bytes 12292
  1.5 5.7 %collective-permute-start = (bf16[8,640]{1,0:T(8,128)(2,1)S(1)}, bf16[8,640]{1,0:T(8,128)(2,1)S(1)}, u32[]{:S(2)}, u32[]{:S(2)}) collective-permute-start(bf16[8,640]{1,0:T(8,128)(2,1)S(1)} %pad_select_fusion), channel_id=1, source_target_pairs={{0,16},{1,17},{2,18},{3,19},{4,20},{5,21},{6,22},{7,23},{8,24},{9,... | collective-permute-start | bytes 30728 | tf_op jit(solution)/shard_map/ppermute | solution.py:16
  7.2 3.8 %collective-permute-start.1 = (bf16[16,640]{1,0:T(8,128)(2,1)S(1)}, bf16[16,640]{1,0:T(8,128)(2,1)S(1)}, u32[]{:S(2)}, u32[]{:S(2)}) collective-permute-start(bf16[16,640]{1,0:T(8,128)(2,1)S(1)} %pad_maximum_fusion.2), channel_id=1, source_target_pairs={{0,8},{1,9},{2,10},{3,11},{4,12},{5,13},{6,14},{7,15},{8,0},{9,1},... | collective-permute-start | bytes 61448 | tf_op jit(solution)/shard_map/ppermute | solution.py:16
  11.0 4.0 %collective-permute-start.2 = (bf16[32,640]{1,0:T(8,128)(2,1)S(1)}, bf16[32,640]{1,0:T(8,128)(2,1)S(1)}, u32[]{:S(2)}, u32[]{:S(2)}) collective-permute-start(bf16[32,640]{1,0:T(8,128)(2,1)S(1)} %pad_maximum_fusion.1), channel_id=1, source_target_pairs={{0,4},{1,5},{2,6},{3,7},{4,0},{5,1},{6,2},{7,3},{8,12},{9,13},{10,... | collective-permute-start | bytes 122888 | tf_op jit(solution)/shard_map/ppermute | solution.py:16
  15.0 4.5 %collective-permute-start.3 = (bf16[64,640]{1,0:T(8,128)(2,1)S(1)}, bf16[64,640]{1,0:T(8,128)(2,1)S(1)}, u32[]{:S(2)}, u32[]{:S(2)}) collective-permute-start(bf16[64,640]{1,0:T(8,128)(2,1)S(1)} %pad_maximum_fusion), channel_id=1, source_target_pairs={{0,2},{1,3},{2,0},{3,1},{4,6},{5,7},{6,4},{7,5},{8,10},{9,11},{10,... | collective-permute-start | bytes 245768 | tf_op jit(solution)/shard_map/ppermute | solution.py:16
  19.7 1.5 %collective-permute-start.4 = (bf16[128,640]{1,0:T(8,128)(2,1)S(1)}, bf16[128,640]{1,0:T(8,128)(2,1)S(1)}, u32[]{:S(2)}, u32[]{:S(2)}) collective-permute-start(bf16[128,640]{1,0:T(8,128)(2,1)S(1)} %constant_dynamic-update-slice_fusion.early_ref), channel_id=1, source_target_pairs={{0,1},{1,0},{2,3},{3,2},{4,5},{5,4},{6,7},{7,6},{8,9},{9,8},{10,11... | collective-permute-start | bytes 491528 | tf_op jit(solution)/shard_map/ppermute | solution.py:16
  20.6 15.6 %copy-start.2 = (f32[8]{0:T(128)S(1)}, f32[8]{0:T(128)}, u32[]{:S(2)}) copy-start(f32[8]{0:T(128)} %param.9) | copy-start | bytes 100

commit v7 on v6

--- a/solution.py
+++ b/solution.py
@@ -11,9 +11,13 @@
 AXES = ("group", "blk")
 
 
-def exchange(x, bit, count):
-    route = [(i, i ^ (1 << bit)) for i in range(count)]
+def exchange(x, bits, count):
+    route = [(i, i ^ (1 << bits[i & 1])) for i in range(count)]
     return lax.ppermute(x, AXES, route)
+
+
+def place(x, order):
+    return sum(((x >> bit) & 1) << step for step, bit in enumerate(order))
 
 
 def tail(features, factor, src_ref, early_ref, last_ref, logits_ref, stats_ref, terms_ref,
@@ -51,7 +55,12 @@
     levels = count.bit_length() - 1
     if (1 << levels) != count:
         raise ValueError("count not pow2")
-    order = list(reversed(range(levels)))
+    outer = list(range(levels - 1, 0, -1))
+    swapped = []
+    for j in range(0, len(outer) - 1, 2):
+        swapped += [outer[j + 1], outer[j]]
+    swapped += outer[len(swapped):]
+    orders = (outer, swapped)
     features = sources.shape[1]
     factor = 2.0 / (features * epsilon)
 
@@ -71,9 +80,9 @@
             ]
         )
     )
-    for bit in order[:-1]:
-        held = jnp.concatenate([held, exchange(held, bit, count)], 0)
-    last = exchange(held, order[-1], count)
+    for bits in zip(*orders):
+        held = jnp.concatenate([held, exchange(held, bits, count)], 0)
+    last = exchange(held, (0, 0), count)
 
     early_rows = held[:, :features]
     early_pots = held[:, features].astype(jnp.float32)
@@ -103,7 +112,9 @@
     me = lax.axis_index(AXES)
     width = columns.shape[0] // count
     apart = me ^ (jnp.arange(count * width) // width)
-    where = sum(((apart >> bit) & 1) << step for step, bit in enumerate(order))
+    mine = jnp.where(me & 1 == 0, place(apart, orders[0]), place(apart, orders[1]))
+    other = jnp.where(me & 1 == 0, place(apart, orders[1]), place(apart, orders[0]))
+    where = jnp.where(apart & 1 == 0, mine, count // 2 + other)
     where = where * width + jnp.arange(count * width) % width
     choose = (where[:, None] == jnp.arange(count * width)[None, :]).astype(jnp.float32)
     part = jnp.dot(choose, columns, precision=lax.Precision.HIGHEST).reshape(count, width, 2)

time: 36.9 us -> 37.3 us (1.011)
  no operation moved by 1% of the time
where the time goes in v7:
time: 37.3 us; the launch traced here: 37.1 us
  blocking collectives  13.3 us (36%)
  starting transfers between devices  9.98 us (27%)
  waiting for transfers between devices  7.24 us (19%)
  other arithmetic  3.31 us (9%)
  Pallas kernels  1.29 us (3%)
  between operations  0.79 us (2%)
  matrix products  0.77 us (2%)
    all_to_all x1, blocking collectives, per_device(): part = lax.all_to_all(part, AXES, 0, 0, tiled=True)  13.3 us
    ppermute x5, starting transfers between devices, exchange(): return lax.ppermute(x, AXES, route)  9.98 us
    ppermute x5, waiting for transfers between devices, exchange(): return lax.ppermute(x, AXES, route)  7.24 us
    reduce_sum x1, other arithmetic, per_device(): jnp.sum(jnp.square(sources.astype(jnp.float32)), 1) / features  1.5 us
    pallas_call x1, Pallas kernels, per_device(): pl.pallas_call(functools.partial(tail, features, factor), out_shape=(jax....  1.29 us
    select_n x1, other arithmetic, per_device(): jnp.where(lane < features, jnp.pad(targets, ((0, 0), (0, 128))), target_p...  0.86 us
  transfers between devices with their start and end apart: 5, of which 5 were waited for; matrix products, arithmetic and copies ran while one was open for 6% of the time, Pallas kernels for 0%

profile of v7, /device:TPU:0, one launch (start us, length us, event | category | flops | bytes accessed | tf_op | source)
XLA Modules:
  0.0 37.1 jit_solution(8573606856589661325)
XLA Ops:
  0.6 0.0 copy-start
  0.6 0.0 copy-start.1
  0.7 0.9 %pad_select_fusion = bf16[8,640]{1,0:T(8,128)(2,1)S(1)} fusion(bf16[8,512]{1,0:T(8,128)(2,1)} %param.6, pred[640]{0:T(1024)(128)(4,1)S(1)} %iota_compare_fusion.2, bf16[8]{0:T(256)(128)(2,1)} %param.7), kind=kLoop, calls=%fused_computation.19 | loop fusion | flops 5120 | bytes 19088 | tf_op jit(solution)/shard_map/jit(_where)/select_n | solution.py:69
  1.5 4.0 %collective-permute-start = (bf16[8,640]{1,0:T(8,128)(2,1)S(1)}, bf16[8,640]{1,0:T(8,128)(2,1)S(1)}, u32[]{:S(2)}, u32[]{:S(2)}) collective-permute-start(bf16[8,640]{1,0:T(8,128)(2,1)S(1)} %pad_select_fusion), channel_id=1, source_target_pairs={{0,16},{1,9},{2,18},{3,11},{4,20},{5,13},{6,22},{7,15},{8,24},{9,1... | collective-permute-start | bytes 30728 | tf_op jit(solution)/shard_map/ppermute | solution.py:16
  5.6 1.5 %multiply_reduce_fusion = f32[1024]{0:T(1024)S(1)} fusion(bf16[1024,512]{1,0:T(8,128)(2,1)} %src_ref.1), kind=kLoop, calls=%fused_computation | loop fusion | flops 1571840 | bytes 1052672 | tf_op jit(solution)/shard_map/reduce_sum | solution.py:78
  7.1 0.0 copy-done.1
  7.1 0.1 collective-permute-done
  7.2 1.9 %collective-permute-start.1 = (bf16[16,640]{1,0:T(8,128)(2,1)S(1)}, bf16[16,640]{1,0:T(8,128)(2,1)S(1)}, u32[]{:S(2)}, u32[]{:S(2)}) collective-permute-start(bf16[16,640]{1,0:T(8,128)(2,1)S(1)} %pad_maximum_fusion.2), channel_id=1, source_target_pairs={{0,8},{1,17},{2,10},{3,19},{4,12},{5,21},{6,14},{7,23},{8,0},{9,25... | collective-permute-start | bytes 61448 | tf_op jit(solution)/shard_map/ppermute | solution.py:16
  9.1 1.9 %collective-permute-done.1 = bf16[16,640]{1,0:T(8,128)(2,1)S(1)} collective-permute-done((bf16[16,640]{1,0:T(8,128)(2,1)S(1)}, bf16[16,640]{1,0:T(8,128)(2,1)S(1)}, u32[]{:S(2)}, u32[]{:S(2)}) %collective-permute-start.1) | collective-permute-done | bytes 20512 | tf_op jit(solution)/shard_map/ppermute | solution.py:16
  11.0 1.8 %collective-permute-start.2 = (bf16[32,640]{1,0:T(8,128)(2,1)S(1)}, bf16[32,640]{1,0:T(8,128)(2,1)S(1)}, u32[]{:S(2)}, u32[]{:S(2)}) collective-permute-start(bf16[32,640]{1,0:T(8,128)(2,1)S(1)} %pad_maximum_fusion.1), channel_id=1, source_target_pairs={{0,4},{1,3},{2,6},{3,1},{4,0},{5,7},{6,2},{7,5},{8,12},{9,11},{10,... | collective-permute-start | bytes 122888 | tf_op jit(solution)/shard_map/ppermute | solution.py:16
  12.8 2.4 %collective-permute-done.2 = bf16[32,640]{1,0:T(8,128)(2,1)S(1)} collective-permute-done((bf16[32,640]{1,0:T(8,128)(2,1)S(1)}, bf16[32,640]{1,0:T(8,128)(2,1)S(1)}, u32[]{:S(2)}, u32[]{:S(2)}) %collective-permute-start.2) | collective-permute-done | bytes 40992 | tf_op jit(solution)/shard_map/ppermute | solution.py:16
  15.2 2.2 %collective-permute-start.3 = (bf16[64,640]{1,0:T(8,128)(2,1)S(1)}, bf16[64,640]{1,0:T(8,128)(2,1)S(1)}, u32[]{:S(2)}, u32[]{:S(2)}) collective-permute-start(bf16[64,640]{1,0:T(8,128)(2,1)S(1)} %pad_maximum_fusion), channel_id=1, source_target_pairs={{0,2},{1,5},{2,0},{3,7},{4,6},{5,1},{6,4},{7,3},{8,10},{9,13},{10,... | collective-permute-start | bytes 245768 | tf_op jit(solution)/shard_map/ppermute | solution.py:16
  17.4 2.4 %collective-permute-done.3 = bf16[64,640]{1,0:T(8,128)(2,1)S(1)} collective-permute-done((bf16[64,640]{1,0:T(8,128)(2,1)S(1)}, bf16[64,640]{1,0:T(8,128)(2,1)S(1)}, u32[]{:S(2)}, u32[]{:S(2)}) %collective-permute-start.3) | collective-permute-done | bytes 81952 | tf_op jit(solution)/shard_map/ppermute | solution.py:16
  19.8 0.1 multiply_reduce_fusion.1
  19.9 0.1 collective-permute-start.4
  20.0 0.1 copy.12
  20.1 0.1 subtract_reduce_fusion
  20.2 0.0 copy-done
  20.2 0.5 %fusion.10 = (f32[1024]{0:T(1024)S(1)}, f32[128,1024]{1,0:T(8,128)S(1)}) fusion(f32[128]{0:T(128)S(1)} %subtract_reduce_fusion, bf16[1024,512]{1,0:T(8,128)(2,1)S(1)} %copy-done, bf16[128,640]{1,0:T(8,128)(2,1)S(1)} %constant_dynamic-update-slice_fusion.early_ref), kind=kOutput, calls=%fused_computation.38 | convolution fusion | flops 134609920 | bytes 1708544 | tf_op jit(solution)/shard_map/dot_general | solution.py:92
  20.7 0.1 exponential_reduce_fusion
  20.8 0.0 copy-start.2
  20.9 0.5 %collective-permute-done.4.last_ref = bf16[128,640]{1,0:T(8,128)(2,1)S(1)} collective-permute-done((bf16[128,640]{1,0:T(8,128)(2,1)S(1)}, bf16[128,640]{1,0:T(8,128)(2,1)S(1)}, u32[]{:S(2)}, u32[]{:S(2)}) %collective-permute-start.4) | collective-permute-done | bytes 163872 | tf_op jit(solution)/shard_map/ppermute | solution.py:16
  21.4 1.3 %shard_map.68 = (f32[256,2]{1,0:T(8,128)S(1)}, f32[1,1024]{1,0:T(1,128)}) custom-call(bf16[1024,512]{1,0:T(8,128)(2,1)S(1)} %copy-done, bf16[128,640]{1,0:T(8,128)(2,1)S(1)} %constant_dynamic-update-slice_fusion.early_ref, bf16[128,640]{1,0:T(8,128)(2,1)S(1)} %collective-permute-done.4.last_ref, f32[128,1024]{1,0:T(8,128)S(1)} %get-tuple-element.9.logits_ref, ...), custom_call_target="tpu_custom_call" | custom-call | tf_op jit(solution)/shard_map/pallas_call | solution.py:100
  22.7 0.3 fusion.1
  22.9 0.1 reshape.85
  23.1 13.3 %all_to_all.5 = f32[32,8,2]{1,2,0:T(2,128)S(1)} all-to-all(f32[32,8,2]{1,2,0:T(2,128)S(1)} %copy.13), channel_id=1, replica_groups=mesh['group'=8,'blk'=4] {'group','blk'}, dimensions={0} | all-to-all | bytes 4096 | tf_op jit(solution)/shard_map/all_to_all | solution.py:121
  36.5 0.0 copy-done.2
  36.5 0.5 %subtract_multiply_fusion = f32[8]{0:T(128)} fusion(f32[8]{0:T(128)S(1)} %copy-done.2, f32[8]{0:T(128)S(1)} %reduce_max.19, f32[8]{0:T(128)S(1)} %multiply_reduce_fusion.2), kind=kLoop, calls=%fused_computation.35 | loop fusion | flops 24 | bytes 128 | tf_op jit(solution)/shard_map/mul | solution.py:126
  (18 shorter events, 0.2 us)
Async XLA Ops:
  0.6 19.6 %copy-start = (bf16[1024,512]{1,0:T(8,128)(2,1)S(1)}, bf16[1024,512]{1,0:T(8,128)(2,1)}, u32[]{:S(2)}) copy-start(bf16[1024,512]{1,0:T(8,128)(2,1)} %src_ref.1) | copy-start | bytes 3145732
  0.6 6.4 %copy-start.1 = (f32[1024]{0:T(1024)S(1)}, f32[1024]{0:T(1024)}, u32[]{:S(2)}) copy-start(f32[1024]{0:T(1024)} %param.8) | copy-start | bytes 12292
  1.5 5.7 %collective-permute-start = (bf16[8,640]{1,0:T(8,128)(2,1)S(1)}, bf16[8,640]{1,0:T(8,128)(2,1)S(1)}, u32[]{:S(2)}, u32[]{:S(2)}) collective-permute-start(bf16[8,640]{1,0:T(8,128)(2,1)S(1)} %pad_select_fusion), channel_id=1, source_target_pairs={{0,16},{1,9},{2,18},{3,11},{4,20},{5,13},{6,22},{7,15},{8,24},{9,1... | collective-permute-start | bytes 30728 | tf_op jit(solution)/shard_map/ppermute | solution.py:16
  7.2 3.8 %collective-permute-start.1 = (bf16[16,640]{1,0:T(8,128)(2,1)S(1)}, bf16[16,640]{1,0:T(8,128)(2,1)S(1)}, u32[]{:S(2)}, u32[]{:S(2)}) collective-permute-start(bf16[16,640]{1,0:T(8,128)(2,1)S(1)} %pad_maximum_fusion.2), channel_id=1, source_target_pairs={{0,8},{1,17},{2,10},{3,19},{4,12},{5,21},{6,14},{7,23},{8,0},{9,25... | collective-permute-start | bytes 61448 | tf_op jit(solution)/shard_map/ppermute | solution.py:16
  11.0 4.2 %collective-permute-start.2 = (bf16[32,640]{1,0:T(8,128)(2,1)S(1)}, bf16[32,640]{1,0:T(8,128)(2,1)S(1)}, u32[]{:S(2)}, u32[]{:S(2)}) collective-permute-start(bf16[32,640]{1,0:T(8,128)(2,1)S(1)} %pad_maximum_fusion.1), channel_id=1, source_target_pairs={{0,4},{1,3},{2,6},{3,1},{4,0},{5,7},{6,2},{7,5},{8,12},{9,11},{10,... | collective-permute-start | bytes 122888 | tf_op jit(solution)/shard_map/ppermute | solution.py:16
  15.2 4.6 %collective-permute-start.3 = (bf16[64,640]{1,0:T(8,128)(2,1)S(1)}, bf16[64,640]{1,0:T(8,128)(2,1)S(1)}, u32[]{:S(2)}, u32[]{:S(2)}) collective-permute-start(bf16[64,640]{1,0:T(8,128)(2,1)S(1)} %pad_maximum_fusion), channel_id=1, source_target_pairs={{0,2},{1,5},{2,0},{3,7},{4,6},{5,1},{6,4},{7,3},{8,10},{9,13},{10,... | collective-permute-start | bytes 245768 | tf_op jit(solution)/shard_map/ppermute | solution.py:16
  19.9 1.5 %collective-permute-start.4 = (bf16[128,640]{1,0:T(8,128)(2,1)S(1)}, bf16[128,640]{1,0:T(8,128)(2,1)S(1)}, u32[]{:S(2)}, u32[]{:S(2)}) collective-permute-start(bf16[128,640]{1,0:T(8,128)(2,1)S(1)} %constant_dynamic-update-slice_fusion.early_ref), channel_id=1, source_target_pairs={{0,1},{1,0},{2,3},{3,2},{4,5},{5,4},{6,7},{7,6},{8,9},{9,8},{10,11... | collective-permute-start | bytes 491528 | tf_op jit(solution)/shard_map/ppermute | solution.py:16
  20.8 15.7 %copy-start.2 = (f32[8]{0:T(128)S(1)}, f32[8]{0:T(128)}, u32[]{:S(2)}) copy-start(f32[8]{0:T(128)} %param.9) | copy-start | bytes 100

commit v8 on v6

--- a/solution.py
+++ b/solution.py
@@ -55,14 +55,14 @@
     features = sources.shape[1]
     factor = 2.0 / (features * epsilon)
 
-    lane = lax.broadcasted_iota(jnp.int32, (targets.shape[0], features + 128), 1)
-    held = lax.optimization_barrier(
-        jnp.where(
-            lane < features,
-            jnp.pad(targets, ((0, 0), (0, 128))),
-            target_potential[:, None],
-        )
-    )
+    def pack(rows, pots):
+        lane = lax.broadcasted_iota(jnp.int32, (rows.shape[0], features + 128), 1)
+        return jnp.where(lane < features, jnp.pad(rows, ((0, 0), (0, 128))), pots[:, None])
+
+    got_rows = exchange(targets, order[0], count)
+    got_pots = exchange(target_potential, order[0], count)
+    held = lax.optimization_barrier(pack(targets, target_potential))
+    held = jnp.concatenate([held, pack(got_rows, got_pots)], 0)
     source_terms = lax.optimization_barrier(
         jnp.stack(
             [
@@ -71,7 +71,7 @@
             ]
         )
     )
-    for bit in order[:-1]:
+    for bit in order[1:-1]:
         held = jnp.concatenate([held, exchange(held, bit, count)], 0)
     last = exchange(held, order[-1], count)
 

time: 36.9 us -> 36.9 us (level)
  waiting for transfers between devices: 7.23 us -> 10.3 us
  blocking collectives: 13.2 us -> 11 us
  starting transfers between devices: 9.74 us -> 8.93 us
    ppermute x5 -> x6, waiting for transfers between devices: 7.23 us -> 10.3 us  [exchange(): return lax.ppermute(x, AXES, route)]
    all_to_all x1, blocking collectives: 13.2 us -> 11 us  [per_device(): part = lax.all_to_all(part, AXES, 0, 0, tiled=True)]
    ppermute x5 -> x6, starting transfers between devices: 9.74 us -> 8.93 us  [exchange(): return lax.ppermute(x, AXES, route)]
    select_n x1 -> x2, other arithmetic: 0.86 us -> 0.85 us  [pack(): jnp.where(lane < features, jnp.pad(rows, ((0, 0), (0, 128))), pots[:, None])]
  transfers between devices with their start and end apart: 5 -> 6, of which waited for: 5 -> 5; matrix products, arithmetic and copies ran while one was open for 6% -> 9% of each run, Pallas kernels for 0% -> 0%
where the time goes in v8:
time: 36.9 us; the launch traced here: 36.7 us
  blocking collectives  11 us (30%)
  waiting for transfers between devices  10.3 us (28%)
  starting transfers between devices  8.93 us (24%)
  other arithmetic  3.3 us (9%)
  Pallas kernels  1.29 us (3%)
  between operations  0.78 us (2%)
  matrix products  0.77 us (2%)
    all_to_all x1, blocking collectives, per_device(): part = lax.all_to_all(part, AXES, 0, 0, tiled=True)  11 us
    ppermute x6, waiting for transfers between devices, exchange(): return lax.ppermute(x, AXES, route)  10.3 us
    ppermute x6, starting transfers between devices, exchange(): return lax.ppermute(x, AXES, route)  8.93 us
    reduce_sum x1, other arithmetic, per_device(): jnp.sum(jnp.square(sources.astype(jnp.float32)), 1) / features  1.5 us
    pallas_call x1, Pallas kernels, per_device(): pl.pallas_call(functools.partial(tail, features, factor), out_shape=(jax....  1.29 us
    select_n x2, other arithmetic, pack(): jnp.where(lane < features, jnp.pad(rows, ((0, 0), (0, 128))), pots[:, None])  0.85 us
  transfers between devices with their start and end apart: 6, of which 5 were waited for; matrix products, arithmetic and copies ran while one was open for 9% of the time, Pallas kernels for 0%

profile of v8, /device:TPU:0, one launch (start us, length us, event | category | flops | bytes accessed | tf_op | source)
XLA Modules:
  0.0 36.7 jit_solution(16711272604799188183)
XLA Ops:
  0.6 0.0 copy-start
  0.6 0.0 copy-start.1
  0.7 4.1 %collective-permute-start = (bf16[8,512]{1,0:T(8,128)(2,1)}, bf16[8,512]{1,0:T(8,128)(2,1)S(1)}, u32[]{:S(2)}, u32[]{:S(2)}) collective-permute-start(bf16[8,512]{1,0:T(8,128)(2,1)} %param.6), channel_id=1, source_target_pairs={{0,16},{1,17},{2,18},{3,19},{4,20},{5,21},{6,22},{7,23},{8,24},{9,... | collective-permute-start | bytes 24584 | tf_op jit(solution)/shard_map/ppermute | solution.py:16
  4.8 0.1 collective-permute-start.1
  4.8 0.8 %pad_select_fusion.1 = bf16[8,640]{1,0:T(8,128)(2,1)S(1)} fusion(bf16[8,512]{1,0:T(8,128)(2,1)} %param.6, pred[640]{0:T(1024)(128)(4,1)S(1)} %iota_compare_fusion.2, bf16[8]{0:T(256)(128)(2,1)} %param.7), kind=kLoop, calls=%fused_computation.20 | loop fusion | flops 5120 | bytes 19088 | tf_op jit(solution)/shard_map/jit(_where)/select_n | solution.py:60
  5.6 1.5 %multiply_reduce_fusion = f32[1024]{0:T(1024)S(1)} fusion(bf16[1024,512]{1,0:T(8,128)(2,1)} %src_ref.1), kind=kLoop, calls=%fused_computation | loop fusion | flops 1571840 | bytes 1052672 | tf_op jit(solution)/shard_map/reduce_sum | solution.py:69
  7.1 0.0 copy-done.1
  7.2 2.2 %collective-permute-done.1 = bf16[8]{0:T(256)(128)(2,1)S(1)} collective-permute-done((bf16[8]{0:T(256)(128)(2,1)}, bf16[8]{0:T(256)(128)(2,1)S(1)}, u32[]{:S(2)}, u32[]{:S(2)}) %collective-permute-start.1) | collective-permute-done | bytes 48 | tf_op jit(solution)/shard_map/ppermute | solution.py:16
  9.3 0.0 collective-permute-done
  9.3 0.1 pad_select_fusion
  9.4 1.6 %collective-permute-start.2 = (bf16[16,640]{1,0:T(8,128)(2,1)S(1)}, bf16[16,640]{1,0:T(8,128)(2,1)S(1)}, u32[]{:S(2)}, u32[]{:S(2)}) collective-permute-start(bf16[16,640]{1,0:T(8,128)(2,1)S(1)} %pad_maximum_fusion.2), channel_id=1, source_target_pairs={{0,8},{1,9},{2,10},{3,11},{4,12},{5,13},{6,14},{7,15},{8,0},{9,1},... | collective-permute-start | bytes 61448 | tf_op jit(solution)/shard_map/ppermute | solution.py:16
  11.0 2.2 %collective-permute-done.2 = bf16[16,640]{1,0:T(8,128)(2,1)S(1)} collective-permute-done((bf16[16,640]{1,0:T(8,128)(2,1)S(1)}, bf16[16,640]{1,0:T(8,128)(2,1)S(1)}, u32[]{:S(2)}, u32[]{:S(2)}) %collective-permute-start.2) | collective-permute-done | bytes 20512 | tf_op jit(solution)/shard_map/ppermute | solution.py:16
  13.2 1.5 %collective-permute-start.3 = (bf16[32,640]{1,0:T(8,128)(2,1)S(1)}, bf16[32,640]{1,0:T(8,128)(2,1)S(1)}, u32[]{:S(2)}, u32[]{:S(2)}) collective-permute-start(bf16[32,640]{1,0:T(8,128)(2,1)S(1)} %pad_maximum_fusion.1), channel_id=1, source_target_pairs={{0,4},{1,5},{2,6},{3,7},{4,0},{5,1},{6,2},{7,3},{8,12},{9,13},{10,... | collective-permute-start | bytes 122888 | tf_op jit(solution)/shard_map/ppermute | solution.py:16
  14.7 2.5 %collective-permute-done.3 = bf16[32,640]{1,0:T(8,128)(2,1)S(1)} collective-permute-done((bf16[32,640]{1,0:T(8,128)(2,1)S(1)}, bf16[32,640]{1,0:T(8,128)(2,1)S(1)}, u32[]{:S(2)}, u32[]{:S(2)}) %collective-permute-start.3) | collective-permute-done | bytes 40992 | tf_op jit(solution)/shard_map/ppermute | solution.py:16
  17.2 1.6 %collective-permute-start.4 = (bf16[64,640]{1,0:T(8,128)(2,1)S(1)}, bf16[64,640]{1,0:T(8,128)(2,1)S(1)}, u32[]{:S(2)}, u32[]{:S(2)}) collective-permute-start(bf16[64,640]{1,0:T(8,128)(2,1)S(1)} %pad_maximum_fusion), channel_id=1, source_target_pairs={{0,2},{1,3},{2,0},{3,1},{4,6},{5,7},{6,4},{7,5},{8,10},{9,11},{10,... | collective-permute-start | bytes 245768 | tf_op jit(solution)/shard_map/ppermute | solution.py:16
  18.8 2.9 %collective-permute-done.4 = bf16[64,640]{1,0:T(8,128)(2,1)S(1)} collective-permute-done((bf16[64,640]{1,0:T(8,128)(2,1)S(1)}, bf16[64,640]{1,0:T(8,128)(2,1)S(1)}, u32[]{:S(2)}, u32[]{:S(2)}) %collective-permute-start.4) | collective-permute-done | bytes 81952 | tf_op jit(solution)/shard_map/ppermute | solution.py:16
  21.8 0.1 multiply_reduce_fusion.1
  21.9 0.1 collective-permute-start.5
  22.0 0.1 copy.12
  22.1 0.1 subtract_reduce_fusion
  22.2 0.0 copy-done
  22.2 0.5 %fusion.9 = (f32[1024]{0:T(1024)S(1)}, f32[128,1024]{1,0:T(8,128)S(1)}) fusion(f32[128]{0:T(128)S(1)} %subtract_reduce_fusion, bf16[1024,512]{1,0:T(8,128)(2,1)S(1)} %copy-done, bf16[128,640]{1,0:T(8,128)(2,1)S(1)} %constant_dynamic-update-slice_fusion.early_ref), kind=kOutput, calls=%fused_computation.37 | convolution fusion | flops 134609920 | bytes 1708544 | tf_op jit(solution)/shard_map/dot_general | solution.py:83
  22.7 0.1 exponential_reduce_fusion
  22.8 0.0 copy-start.2
  22.8 0.5 %collective-permute-done.5.last_ref = bf16[128,640]{1,0:T(8,128)(2,1)S(1)} collective-permute-done((bf16[128,640]{1,0:T(8,128)(2,1)S(1)}, bf16[128,640]{1,0:T(8,128)(2,1)S(1)}, u32[]{:S(2)}, u32[]{:S(2)}) %collective-permute-start.5) | collective-permute-done | bytes 163872 | tf_op jit(solution)/shard_map/ppermute | solution.py:16
  23.3 1.3 %shard_map.68 = (f32[256,2]{1,0:T(8,128)S(1)}, f32[1,1024]{1,0:T(1,128)}) custom-call(bf16[1024,512]{1,0:T(8,128)(2,1)S(1)} %copy-done, bf16[128,640]{1,0:T(8,128)(2,1)S(1)} %constant_dynamic-update-slice_fusion.early_ref, bf16[128,640]{1,0:T(8,128)(2,1)S(1)} %collective-permute-done.5.last_ref, f32[128,1024]{1,0:T(8,128)S(1)} %get-tuple-element.11.logits_ref, ...), custom_call_target="tpu_custom_call" | custom-call | tf_op jit(solution)/shard_map/pallas_call | solution.py:91
  24.6 0.3 fusion.1
  24.9 0.1 reshape.77
  25.1 11.0 %all_to_all.5 = f32[32,8,2]{1,2,0:T(2,128)S(1)} all-to-all(f32[32,8,2]{1,2,0:T(2,128)S(1)} %copy.13), channel_id=1, replica_groups=mesh['group'=8,'blk'=4] {'group','blk'}, dimensions={0} | all-to-all | bytes 4096 | tf_op jit(solution)/shard_map/all_to_all | solution.py:110
  36.2 0.0 copy-done.2
  36.2 0.5 %subtract_multiply_fusion = f32[8]{0:T(128)} fusion(f32[8]{0:T(128)S(1)} %copy-done.2, f32[8]{0:T(128)S(1)} %reduce_max.19, f32[8]{0:T(128)S(1)} %multiply_reduce_fusion.2), kind=kLoop, calls=%fused_computation.34 | loop fusion | flops 24 | bytes 128 | tf_op jit(solution)/shard_map/mul | solution.py:115
  (17 shorter events, 0.2 us)
Async XLA Ops:
  0.6 21.6 %copy-start = (bf16[1024,512]{1,0:T(8,128)(2,1)S(1)}, bf16[1024,512]{1,0:T(8,128)(2,1)}, u32[]{:S(2)}) copy-start(bf16[1024,512]{1,0:T(8,128)(2,1)} %src_ref.1) | copy-start | bytes 3145732
  0.6 6.5 %copy-start.1 = (f32[1024]{0:T(1024)S(1)}, f32[1024]{0:T(1024)}, u32[]{:S(2)}) copy-start(f32[1024]{0:T(1024)} %param.8) | copy-start | bytes 12292
  0.7 8.7 %collective-permute-start = (bf16[8,512]{1,0:T(8,128)(2,1)}, bf16[8,512]{1,0:T(8,128)(2,1)S(1)}, u32[]{:S(2)}, u32[]{:S(2)}) collective-permute-start(bf16[8,512]{1,0:T(8,128)(2,1)} %param.6), channel_id=1, source_target_pairs={{0,16},{1,17},{2,18},{3,19},{4,20},{5,21},{6,22},{7,23},{8,24},{9,... | collective-permute-start | bytes 24584 | tf_op jit(solution)/shard_map/ppermute | solution.py:16
  4.8 4.6 %collective-permute-start.1 = (bf16[8]{0:T(256)(128)(2,1)}, bf16[8]{0:T(256)(128)(2,1)S(1)}, u32[]{:S(2)}, u32[]{:S(2)}) collective-permute-start(bf16[8]{0:T(256)(128)(2,1)} %param.7), channel_id=1, source_target_pairs={{0,16},{1,17},{2,18},{3,19},{4,20},{5,21},{6,22},{7,23},{8,24},{9,... | collective-permute-start | bytes 56 | tf_op jit(solution)/shard_map/ppermute | solution.py:16
  9.4 3.8 %collective-permute-start.2 = (bf16[16,640]{1,0:T(8,128)(2,1)S(1)}, bf16[16,640]{1,0:T(8,128)(2,1)S(1)}, u32[]{:S(2)}, u32[]{:S(2)}) collective-permute-start(bf16[16,640]{1,0:T(8,128)(2,1)S(1)} %pad_maximum_fusion.2), channel_id=1, source_target_pairs={{0,8},{1,9},{2,10},{3,11},{4,12},{5,13},{6,14},{7,15},{8,0},{9,1},... | collective-permute-start | bytes 61448 | tf_op jit(solution)/shard_map/ppermute | solution.py:16
  13.2 4.0 %collective-permute-start.3 = (bf16[32,640]{1,0:T(8,128)(2,1)S(1)}, bf16[32,640]{1,0:T(8,128)(2,1)S(1)}, u32[]{:S(2)}, u32[]{:S(2)}) collective-permute-start(bf16[32,640]{1,0:T(8,128)(2,1)S(1)} %pad_maximum_fusion.1), channel_id=1, source_target_pairs={{0,4},{1,5},{2,6},{3,7},{4,0},{5,1},{6,2},{7,3},{8,12},{9,13},{10,... | collective-permute-start | bytes 122888 | tf_op jit(solution)/shard_map/ppermute | solution.py:16
  17.2 4.5 %collective-permute-start.4 = (bf16[64,640]{1,0:T(8,128)(2,1)S(1)}, bf16[64,640]{1,0:T(8,128)(2,1)S(1)}, u32[]{:S(2)}, u32[]{:S(2)}) collective-permute-start(bf16[64,640]{1,0:T(8,128)(2,1)S(1)} %pad_maximum_fusion), channel_id=1, source_target_pairs={{0,2},{1,3},{2,0},{3,1},{4,6},{5,7},{6,4},{7,5},{8,10},{9,11},{10,... | collective-permute-start | bytes 245768 | tf_op jit(solution)/shard_map/ppermute | solution.py:16
  21.9 1.5 %collective-permute-start.5 = (bf16[128,640]{1,0:T(8,128)(2,1)S(1)}, bf16[128,640]{1,0:T(8,128)(2,1)S(1)}, u32[]{:S(2)}, u32[]{:S(2)}) collective-permute-start(bf16[128,640]{1,0:T(8,128)(2,1)S(1)} %constant_dynamic-update-slice_fusion.early_ref), channel_id=1, source_target_pairs={{0,1},{1,0},{2,3},{3,2},{4,5},{5,4},{6,7},{7,6},{8,9},{9,8},{10,11... | collective-permute-start | bytes 491528 | tf_op jit(solution)/shard_map/ppermute | solution.py:16
  22.8 13.4 %copy-start.2 = (f32[8]{0:T(128)S(1)}, f32[8]{0:T(128)}, u32[]{:S(2)}) copy-start(f32[8]{0:T(128)} %param.9) | copy-start | bytes 100

commit v9 on v6

--- a/solution.py
+++ b/solution.py
@@ -16,8 +16,8 @@
     return lax.ppermute(x, AXES, route)
 
 
-def tail(features, factor, src_ref, early_ref, last_ref, logits_ref, stats_ref, terms_ref,
-         col_ref, pot_ref):
+def tail(features, factor, width, order, me_ref, src_ref, early_ref, last_ref, logits_ref,
+         stats_ref, terms_ref, col_ref, pot_ref):
     block = last_ref[...]
     rows = block[:, :features]
     pots = block[:, features:features + 1].astype(jnp.float32)
@@ -43,8 +43,13 @@
     ):
         column = logits - block_pots / epsilon + dual
         col_max = jnp.max(column, 1, keepdims=True)
-        col_ref[start:start + half, 0:1] = col_max
-        col_ref[start:start + half, 1:2] = jnp.sum(jnp.exp(column - col_max), 1, keepdims=True)
+        col_sum = jnp.sum(jnp.exp(column - col_max), 1, keepdims=True)
+        for first in range(0, half, width):
+            position = (start + first) // width
+            owner = me_ref[0] ^ sum(((position >> step) & 1) << bit for step, bit in enumerate(order))
+            slot = pl.ds(pl.multiple_of(owner * width, width), width)
+            col_ref[slot, 0:1] = col_max[first:first + width]
+            col_ref[slot, 1:2] = col_sum[first:first + width]
 
 def per_device(sources, targets, target_potential, log_source_mass, log_target_mass):
     count = lax.axis_size("group") * lax.axis_size("blk")
@@ -87,26 +92,22 @@
     early_stats = jnp.stack([early_max, jnp.sum(jnp.exp(early_logits - early_max[None, :]), 0)])
 
     half = held.shape[0]
+    width = targets.shape[0]
+    me = lax.axis_index(AXES)
     vmem = pl.BlockSpec(memory_space=pltpu.VMEM)
     columns, source_potential = pl.pallas_call(
-        functools.partial(tail, features, factor),
+        functools.partial(tail, features, factor, width, order),
         out_shape=(
             jax.ShapeDtypeStruct((2 * half, 2), jnp.float32),
             jax.ShapeDtypeStruct((1, sources.shape[0]), jnp.float32),
         ),
-        in_specs=[vmem] * 6,
+        in_specs=[pl.BlockSpec(memory_space=pltpu.SMEM)] + [vmem] * 6,
         out_specs=(vmem, vmem),
         compiler_params=pltpu.CompilerParams(vmem_limit_bytes=24 * 1024 * 1024),
-    )(sources, held, last, early_logits, early_stats, source_terms)
+    )(me.astype(jnp.int32).reshape(1), sources, held, last, early_logits, early_stats, source_terms)
     source_potential = source_potential.reshape(-1)
 
-    me = lax.axis_index(AXES)
-    width = columns.shape[0] // count
-    apart = me ^ (jnp.arange(count * width) // width)
-    where = sum(((apart >> bit) & 1) << step for step, bit in enumerate(order))
-    where = where * width + jnp.arange(count * width) % width
-    choose = (where[:, None] == jnp.arange(count * width)[None, :]).astype(jnp.float32)
-    part = jnp.dot(choose, columns, precision=lax.Precision.HIGHEST).reshape(count, width, 2)
+    part = columns.reshape(count, width, 2)
     part = lax.all_to_all(part, AXES, 0, 0, tiled=True)
     owned_max = jnp.max(part[:, :, 0], 0)
     owned_sum = jnp.sum(part[:, :, 1] * jnp.exp(part[:, :, 0] - owned_max[None, :]), 0)

time: 36.9 us -> 37 us (level)
  no operation moved by 1% of the time
where the time goes in v9:
time: 37 us; the launch traced here: 36.8 us
  blocking collectives  13.2 us (36%)
  starting transfers between devices  9.76 us (26%)
  waiting for transfers between devices  7.24 us (20%)
  other arithmetic  3.48 us (9%)
  Pallas kernels  1.29 us (3%)
  between operations  0.76 us (2%)
  local copies, waits for them, and re-layouts  0.55 us (1%)
  matrix products  0.49 us (1%)
    all_to_all x1, blocking collectives, per_device(): part = lax.all_to_all(part, AXES, 0, 0, tiled=True)  13.2 us
    ppermute x5, starting transfers between devices, exchange(): return lax.ppermute(x, AXES, route)  9.76 us
    ppermute x5, waiting for transfers between devices, exchange(): return lax.ppermute(x, AXES, route)  7.24 us
    reduce_sum x1, other arithmetic, per_device(): jnp.sum(jnp.square(sources.astype(jnp.float32)), 1) / features  1.5 us
    pallas_call x1, Pallas kernels, per_device(): pl.pallas_call(functools.partial(tail, features, factor, width, order), o...  1.29 us
    select_n x1, other arithmetic, per_device(): jnp.where(lane < features, jnp.pad(targets, ((0, 0), (0, 128))), target_p...  0.86 us
  transfers between devices with their start and end apart: 5, of which 5 were waited for; matrix products, arithmetic and copies ran while one was open for 6% of the time, Pallas kernels for 0%

profile of v9, /device:TPU:0, one launch (start us, length us, event | category | flops | bytes accessed | tf_op | source)
XLA Modules:
  0.0 36.8 jit_solution(17564609939846704402)
XLA Ops:
  0.6 0.0 copy-start
  0.6 0.0 copy-start.1
  0.7 0.9 %pad_select_fusion = bf16[8,640]{1,0:T(8,128)(2,1)S(1)} fusion(bf16[8,512]{1,0:T(8,128)(2,1)} %param.6, pred[640]{0:T(1024)(128)(4,1)S(1)} %iota_compare_fusion, bf16[8]{0:T(256)(128)(2,1)} %param.7), kind=kLoop, calls=%fused_computation.15 | loop fusion | flops 5120 | bytes 19088 | tf_op jit(solution)/shard_map/jit(_where)/select_n | solution.py:65
  1.5 4.0 %collective-permute-start = (bf16[8,640]{1,0:T(8,128)(2,1)S(1)}, bf16[8,640]{1,0:T(8,128)(2,1)S(1)}, u32[]{:S(2)}, u32[]{:S(2)}) collective-permute-start(bf16[8,640]{1,0:T(8,128)(2,1)S(1)} %pad_select_fusion), channel_id=1, source_target_pairs={{0,16},{1,17},{2,18},{3,19},{4,20},{5,21},{6,22},{7,23},{8,24},{9,... | collective-permute-start | bytes 30728 | tf_op jit(solution)/shard_map/ppermute | solution.py:16
  5.6 1.5 %multiply_reduce_fusion = f32[1024]{0:T(1024)S(1)} fusion(bf16[1024,512]{1,0:T(8,128)(2,1)} %src_ref.1), kind=kLoop, calls=%fused_computation | loop fusion | flops 1571840 | bytes 1052672 | tf_op jit(solution)/shard_map/reduce_sum | solution.py:74
  7.1 0.0 copy-done.1
  7.1 0.1 collective-permute-done
  7.2 1.9 %collective-permute-start.1 = (bf16[16,640]{1,0:T(8,128)(2,1)S(1)}, bf16[16,640]{1,0:T(8,128)(2,1)S(1)}, u32[]{:S(2)}, u32[]{:S(2)}) collective-permute-start(bf16[16,640]{1,0:T(8,128)(2,1)S(1)} %pad_maximum_fusion.2), channel_id=1, source_target_pairs={{0,8},{1,9},{2,10},{3,11},{4,12},{5,13},{6,14},{7,15},{8,0},{9,1},... | collective-permute-start | bytes 61448 | tf_op jit(solution)/shard_map/ppermute | solution.py:16
  9.1 1.9 %collective-permute-done.1 = bf16[16,640]{1,0:T(8,128)(2,1)S(1)} collective-permute-done((bf16[16,640]{1,0:T(8,128)(2,1)S(1)}, bf16[16,640]{1,0:T(8,128)(2,1)S(1)}, u32[]{:S(2)}, u32[]{:S(2)}) %collective-permute-start.1) | collective-permute-done | bytes 20512 | tf_op jit(solution)/shard_map/ppermute | solution.py:16
  11.0 1.8 %collective-permute-start.2 = (bf16[32,640]{1,0:T(8,128)(2,1)S(1)}, bf16[32,640]{1,0:T(8,128)(2,1)S(1)}, u32[]{:S(2)}, u32[]{:S(2)}) collective-permute-start(bf16[32,640]{1,0:T(8,128)(2,1)S(1)} %pad_maximum_fusion.1), channel_id=1, source_target_pairs={{0,4},{1,5},{2,6},{3,7},{4,0},{5,1},{6,2},{7,3},{8,12},{9,13},{10,... | collective-permute-start | bytes 122888 | tf_op jit(solution)/shard_map/ppermute | solution.py:16
  12.8 2.2 %collective-permute-done.2 = bf16[32,640]{1,0:T(8,128)(2,1)S(1)} collective-permute-done((bf16[32,640]{1,0:T(8,128)(2,1)S(1)}, bf16[32,640]{1,0:T(8,128)(2,1)S(1)}, u32[]{:S(2)}, u32[]{:S(2)}) %collective-permute-start.2) | collective-permute-done | bytes 40992 | tf_op jit(solution)/shard_map/ppermute | solution.py:16
  15.0 1.9 %collective-permute-start.3 = (bf16[64,640]{1,0:T(8,128)(2,1)S(1)}, bf16[64,640]{1,0:T(8,128)(2,1)S(1)}, u32[]{:S(2)}, u32[]{:S(2)}) collective-permute-start(bf16[64,640]{1,0:T(8,128)(2,1)S(1)} %pad_maximum_fusion), channel_id=1, source_target_pairs={{0,2},{1,3},{2,0},{3,1},{4,6},{5,7},{6,4},{7,5},{8,10},{9,11},{10,... | collective-permute-start | bytes 245768 | tf_op jit(solution)/shard_map/ppermute | solution.py:16
  16.9 2.6 %collective-permute-done.3 = bf16[64,640]{1,0:T(8,128)(2,1)S(1)} collective-permute-done((bf16[64,640]{1,0:T(8,128)(2,1)S(1)}, bf16[64,640]{1,0:T(8,128)(2,1)S(1)}, u32[]{:S(2)}, u32[]{:S(2)}) %collective-permute-start.3) | collective-permute-done | bytes 81952 | tf_op jit(solution)/shard_map/ppermute | solution.py:16
  19.5 0.1 multiply_reduce_fusion.1
  19.6 0.1 collective-permute-start.4
  19.7 0.1 copy.15
  19.8 0.1 subtract_reduce_fusion
  20.0 0.0 copy-done
  20.0 0.5 %fusion.6 = (f32[1024]{0:T(1024)S(1)}, f32[128,1024]{1,0:T(8,128)S(1)}) fusion(f32[128]{0:T(128)S(1)} %subtract_reduce_fusion, bf16[1024,512]{1,0:T(8,128)(2,1)S(1)} %copy-done, bf16[128,640]{1,0:T(8,128)(2,1)S(1)} %constant_dynamic-update-slice_fusion.early_ref), kind=kOutput, calls=%fused_computation.28 | convolution fusion | flops 134609920 | bytes 1708544 | tf_op jit(solution)/shard_map/dot_general | solution.py:88
  20.5 0.1 exponential_reduce_fusion
  20.6 0.5 %collective-permute-done.4.last_ref = bf16[128,640]{1,0:T(8,128)(2,1)S(1)} collective-permute-done((bf16[128,640]{1,0:T(8,128)(2,1)S(1)}, bf16[128,640]{1,0:T(8,128)(2,1)S(1)}, u32[]{:S(2)}, u32[]{:S(2)}) %collective-permute-start.4) | collective-permute-done | bytes 163872 | tf_op jit(solution)/shard_map/ppermute | solution.py:16
  21.1 0.0 copy-start.2
  21.1 1.3 %shard_map.68 = (f32[256,2]{1,0:T(8,128)S(1)}, f32[1,1024]{1,0:T(1,128)}) custom-call(s32[1]{0:T(128)} %bitcast.me_ref, bf16[1024,512]{1,0:T(8,128)(2,1)S(1)} %copy-done, bf16[128,640]{1,0:T(8,128)(2,1)S(1)} %constant_dynamic-update-slice_fusion.early_ref, bf16[128,640]{1,0:T(8,128)(2,1)S(1)} %collective-permute-done.4.last_ref, ...), custom_call_target="tpu_custom_call" | custom-call | tf_op jit(solution)/shard_map/pallas_call | solution.py:98
  22.4 0.2 copy.16
  22.6 13.2 %all_to_all.5 = f32[32,8,2]{1,2,0:T(2,128)S(1)} all-to-all(f32[32,8,2]{1,2,0:T(2,128)S(1)} %copy.16), channel_id=1, replica_groups=mesh['group'=8,'blk'=4] {'group','blk'}, dimensions={0} | all-to-all | bytes 4096 | tf_op jit(solution)/shard_map/all_to_all | solution.py:111
  35.9 0.1 fusion.5
  36.0 0.1 copy.20
  36.0 0.1 copy.19
  36.1 0.2 fusion.4
  36.3 0.0 copy-done.2
  36.3 0.5 %subtract_multiply_fusion = f32[8]{0:T(128)} fusion(f32[8]{0:T(128)S(1)} %copy-done.2, f32[8]{0:T(128)S(1)} %get-tuple-element.7, f32[8]{0:T(128)S(1)} %fusion.4), kind=kLoop, calls=%fused_computation.24 | loop fusion | flops 24 | bytes 128 | tf_op jit(solution)/shard_map/mul | solution.py:116
  (13 shorter events, 0.1 us)
Async XLA Ops:
  0.6 19.3 %copy-start = (bf16[1024,512]{1,0:T(8,128)(2,1)S(1)}, bf16[1024,512]{1,0:T(8,128)(2,1)}, u32[]{:S(2)}) copy-start(bf16[1024,512]{1,0:T(8,128)(2,1)} %src_ref.1) | copy-start | bytes 3145732
  0.6 6.4 %copy-start.1 = (f32[1024]{0:T(1024)S(1)}, f32[1024]{0:T(1024)}, u32[]{:S(2)}) copy-start(f32[1024]{0:T(1024)} %param.8) | copy-start | bytes 12292
  1.5 5.7 %collective-permute-start = (bf16[8,640]{1,0:T(8,128)(2,1)S(1)}, bf16[8,640]{1,0:T(8,128)(2,1)S(1)}, u32[]{:S(2)}, u32[]{:S(2)}) collective-permute-start(bf16[8,640]{1,0:T(8,128)(2,1)S(1)} %pad_select_fusion), channel_id=1, source_target_pairs={{0,16},{1,17},{2,18},{3,19},{4,20},{5,21},{6,22},{7,23},{8,24},{9,... | collective-permute-start | bytes 30728 | tf_op jit(solution)/shard_map/ppermute | solution.py:16
  7.2 3.8 %collective-permute-start.1 = (bf16[16,640]{1,0:T(8,128)(2,1)S(1)}, bf16[16,640]{1,0:T(8,128)(2,1)S(1)}, u32[]{:S(2)}, u32[]{:S(2)}) collective-permute-start(bf16[16,640]{1,0:T(8,128)(2,1)S(1)} %pad_maximum_fusion.2), channel_id=1, source_target_pairs={{0,8},{1,9},{2,10},{3,11},{4,12},{5,13},{6,14},{7,15},{8,0},{9,1},... | collective-permute-start | bytes 61448 | tf_op jit(solution)/shard_map/ppermute | solution.py:16
  11.0 4.0 %collective-permute-start.2 = (bf16[32,640]{1,0:T(8,128)(2,1)S(1)}, bf16[32,640]{1,0:T(8,128)(2,1)S(1)}, u32[]{:S(2)}, u32[]{:S(2)}) collective-permute-start(bf16[32,640]{1,0:T(8,128)(2,1)S(1)} %pad_maximum_fusion.1), channel_id=1, source_target_pairs={{0,4},{1,5},{2,6},{3,7},{4,0},{5,1},{6,2},{7,3},{8,12},{9,13},{10,... | collective-permute-start | bytes 122888 | tf_op jit(solution)/shard_map/ppermute | solution.py:16
  15.0 4.5 %collective-permute-start.3 = (bf16[64,640]{1,0:T(8,128)(2,1)S(1)}, bf16[64,640]{1,0:T(8,128)(2,1)S(1)}, u32[]{:S(2)}, u32[]{:S(2)}) collective-permute-start(bf16[64,640]{1,0:T(8,128)(2,1)S(1)} %pad_maximum_fusion), channel_id=1, source_target_pairs={{0,2},{1,3},{2,0},{3,1},{4,6},{5,7},{6,4},{7,5},{8,10},{9,11},{10,... | collective-permute-start | bytes 245768 | tf_op jit(solution)/shard_map/ppermute | solution.py:16
  19.6 1.5 %collective-permute-start.4 = (bf16[128,640]{1,0:T(8,128)(2,1)S(1)}, bf16[128,640]{1,0:T(8,128)(2,1)S(1)}, u32[]{:S(2)}, u32[]{:S(2)}) collective-permute-start(bf16[128,640]{1,0:T(8,128)(2,1)S(1)} %constant_dynamic-update-slice_fusion.early_ref), channel_id=1, source_target_pairs={{0,1},{1,0},{2,3},{3,2},{4,5},{5,4},{6,7},{7,6},{8,9},{9,8},{10,11... | collective-permute-start | bytes 491528 | tf_op jit(solution)/shard_map/ppermute | solution.py:16
  21.1 15.2 %copy-start.2 = (f32[8]{0:T(128)S(1)}, f32[8]{0:T(128)}, u32[]{:S(2)}) copy-start(f32[8]{0:T(128)} %param.9) | copy-start | bytes 100

commit v10 on v9

--- a/solution.py
+++ b/solution.py
@@ -44,12 +44,15 @@
         column = logits - block_pots / epsilon + dual
         col_max = jnp.max(column, 1, keepdims=True)
         col_sum = jnp.sum(jnp.exp(column - col_max), 1, keepdims=True)
+        diagonal = lax.broadcasted_iota(jnp.int32, (width, width), 0) == lax.broadcasted_iota(
+            jnp.int32, (width, width), 1
+        )
         for first in range(0, half, width):
             position = (start + first) // width
             owner = me_ref[0] ^ sum(((position >> step) & 1) << bit for step, bit in enumerate(order))
-            slot = pl.ds(pl.multiple_of(owner * width, width), width)
-            col_ref[slot, 0:1] = col_max[first:first + width]
-            col_ref[slot, 1:2] = col_sum[first:first + width]
+            for lanes, stat in ((0, col_max), (width, col_sum)):
+                piece = jnp.where(diagonal, stat[first:first + width], 0.0)
+                col_ref[pl.ds(owner, 1), lanes:lanes + width] = jnp.sum(piece, 0, keepdims=True)
 
 def per_device(sources, targets, target_potential, log_source_mass, log_target_mass):
     count = lax.axis_size("group") * lax.axis_size("blk")
@@ -98,7 +101,7 @@
     columns, source_potential = pl.pallas_call(
         functools.partial(tail, features, factor, width, order),
         out_shape=(
-            jax.ShapeDtypeStruct((2 * half, 2), jnp.float32),
+            jax.ShapeDtypeStruct((count, 2 * width), jnp.float32),
             jax.ShapeDtypeStruct((1, sources.shape[0]), jnp.float32),
         ),
         in_specs=[pl.BlockSpec(memory_space=pltpu.SMEM)] + [vmem] * 6,
@@ -107,10 +110,9 @@
     )(me.astype(jnp.int32).reshape(1), sources, held, last, early_logits, early_stats, source_terms)
     source_potential = source_potential.reshape(-1)
 
-    part = columns.reshape(count, width, 2)
-    part = lax.all_to_all(part, AXES, 0, 0, tiled=True)
-    owned_max = jnp.max(part[:, :, 0], 0)
-    owned_sum = jnp.sum(part[:, :, 1] * jnp.exp(part[:, :, 0] - owned_max[None, :]), 0)
+    part = lax.all_to_all(columns, AXES, 0, 0, tiled=True)
+    owned_max = jnp.max(part[:, :width], 0)
+    owned_sum = jnp.sum(part[:, width:] * jnp.exp(part[:, :width] - owned_max[None, :]), 0)
     part = (owned_max, owned_sum)
 
     target_update = epsilon * (log_target_mass - (part[0] + jnp.log(part[1])))

time: 37 us -> 36.6 us (0.989)
  local copies, waits for them, and re-layouts: 0.55 us -> 0.17 us
where the time goes in v10:
time: 36.6 us; the launch traced here: 36.4 us
  blocking collectives  13.1 us (36%)
  starting transfers between devices  9.76 us (27%)
  waiting for transfers between devices  7.23 us (20%)
  other arithmetic  3.35 us (9%)
  Pallas kernels  1.52 us (4%)
  between operations  0.76 us (2%)
  matrix products  0.49 us (1%)
    all_to_all x1, blocking collectives, per_device(): part = lax.all_to_all(columns, AXES, 0, 0, tiled=True)  13.1 us
    ppermute x5, starting transfers between devices, exchange(): return lax.ppermute(x, AXES, route)  9.76 us
    ppermute x5, waiting for transfers between devices, exchange(): return lax.ppermute(x, AXES, route)  7.23 us
    pallas_call x1, Pallas kernels, per_device(): pl.pallas_call(functools.partial(tail, features, factor, width, order), o...  1.52 us
    reduce_sum x1, other arithmetic, per_device(): jnp.sum(jnp.square(sources.astype(jnp.float32)), 1) / features  1.5 us
    select_n x1, other arithmetic, per_device(): jnp.where(lane < features, jnp.pad(targets, ((0, 0), (0, 128))), target_p...  0.86 us
  transfers between devices with their start and end apart: 5, of which 5 were waited for; matrix products, arithmetic and copies ran while one was open for 6% of the time, Pallas kernels for 0%

profile of v10, /device:TPU:0, one launch (start us, length us, event | category | flops | bytes accessed | tf_op | source)
XLA Modules:
  0.0 36.4 jit_solution(498868628056892788)
XLA Ops:
  0.6 0.0 copy-start
  0.6 0.0 copy-start.1
  0.7 0.9 %pad_select_fusion = bf16[8,640]{1,0:T(8,128)(2,1)S(1)} fusion(bf16[8,512]{1,0:T(8,128)(2,1)} %param.6, pred[640]{0:T(1024)(128)(4,1)S(1)} %iota_compare_fusion, bf16[8]{0:T(256)(128)(2,1)} %param.7), kind=kLoop, calls=%fused_computation.18 | loop fusion | flops 5120 | bytes 19088 | tf_op jit(solution)/shard_map/jit(_where)/select_n | solution.py:68
  1.5 4.0 %collective-permute-start = (bf16[8,640]{1,0:T(8,128)(2,1)S(1)}, bf16[8,640]{1,0:T(8,128)(2,1)S(1)}, u32[]{:S(2)}, u32[]{:S(2)}) collective-permute-start(bf16[8,640]{1,0:T(8,128)(2,1)S(1)} %pad_select_fusion), channel_id=1, source_target_pairs={{0,16},{1,17},{2,18},{3,19},{4,20},{5,21},{6,22},{7,23},{8,24},{9,... | collective-permute-start | bytes 30728 | tf_op jit(solution)/shard_map/ppermute | solution.py:16
  5.6 1.5 %multiply_reduce_fusion = f32[1024]{0:T(1024)S(1)} fusion(bf16[1024,512]{1,0:T(8,128)(2,1)} %src_ref.1), kind=kLoop, calls=%fused_computation | loop fusion | flops 1571840 | bytes 1052672 | tf_op jit(solution)/shard_map/reduce_sum | solution.py:77
  7.1 0.0 copy-done.1
  7.1 0.1 collective-permute-done
  7.2 1.9 %collective-permute-start.1 = (bf16[16,640]{1,0:T(8,128)(2,1)S(1)}, bf16[16,640]{1,0:T(8,128)(2,1)S(1)}, u32[]{:S(2)}, u32[]{:S(2)}) collective-permute-start(bf16[16,640]{1,0:T(8,128)(2,1)S(1)} %pad_maximum_fusion.2), channel_id=1, source_target_pairs={{0,8},{1,9},{2,10},{3,11},{4,12},{5,13},{6,14},{7,15},{8,0},{9,1},... | collective-permute-start | bytes 61448 | tf_op jit(solution)/shard_map/ppermute | solution.py:16
  9.1 1.9 %collective-permute-done.1 = bf16[16,640]{1,0:T(8,128)(2,1)S(1)} collective-permute-done((bf16[16,640]{1,0:T(8,128)(2,1)S(1)}, bf16[16,640]{1,0:T(8,128)(2,1)S(1)}, u32[]{:S(2)}, u32[]{:S(2)}) %collective-permute-start.1) | collective-permute-done | bytes 20512 | tf_op jit(solution)/shard_map/ppermute | solution.py:16
  11.0 1.8 %collective-permute-start.2 = (bf16[32,640]{1,0:T(8,128)(2,1)S(1)}, bf16[32,640]{1,0:T(8,128)(2,1)S(1)}, u32[]{:S(2)}, u32[]{:S(2)}) collective-permute-start(bf16[32,640]{1,0:T(8,128)(2,1)S(1)} %pad_maximum_fusion.1), channel_id=1, source_target_pairs={{0,4},{1,5},{2,6},{3,7},{4,0},{5,1},{6,2},{7,3},{8,12},{9,13},{10,... | collective-permute-start | bytes 122888 | tf_op jit(solution)/shard_map/ppermute | solution.py:16
  12.8 2.2 %collective-permute-done.2 = bf16[32,640]{1,0:T(8,128)(2,1)S(1)} collective-permute-done((bf16[32,640]{1,0:T(8,128)(2,1)S(1)}, bf16[32,640]{1,0:T(8,128)(2,1)S(1)}, u32[]{:S(2)}, u32[]{:S(2)}) %collective-permute-start.2) | collective-permute-done | bytes 40992 | tf_op jit(solution)/shard_map/ppermute | solution.py:16
  15.0 1.9 %collective-permute-start.3 = (bf16[64,640]{1,0:T(8,128)(2,1)S(1)}, bf16[64,640]{1,0:T(8,128)(2,1)S(1)}, u32[]{:S(2)}, u32[]{:S(2)}) collective-permute-start(bf16[64,640]{1,0:T(8,128)(2,1)S(1)} %pad_maximum_fusion), channel_id=1, source_target_pairs={{0,2},{1,3},{2,0},{3,1},{4,6},{5,7},{6,4},{7,5},{8,10},{9,11},{10,... | collective-permute-start | bytes 245768 | tf_op jit(solution)/shard_map/ppermute | solution.py:16
  16.9 2.6 %collective-permute-done.3 = bf16[64,640]{1,0:T(8,128)(2,1)S(1)} collective-permute-done((bf16[64,640]{1,0:T(8,128)(2,1)S(1)}, bf16[64,640]{1,0:T(8,128)(2,1)S(1)}, u32[]{:S(2)}, u32[]{:S(2)}) %collective-permute-start.3) | collective-permute-done | bytes 81952 | tf_op jit(solution)/shard_map/ppermute | solution.py:16
  19.5 0.1 multiply_reduce_fusion.1
  19.6 0.1 collective-permute-start.4
  19.7 0.1 copy.11
  19.8 0.1 subtract_reduce_fusion
  20.0 0.0 copy-done
  20.0 0.5 %fusion.3 = (f32[1024]{0:T(1024)S(1)}, f32[128,1024]{1,0:T(8,128)S(1)}) fusion(f32[128]{0:T(128)S(1)} %subtract_reduce_fusion, bf16[1024,512]{1,0:T(8,128)(2,1)S(1)} %copy-done, bf16[128,640]{1,0:T(8,128)(2,1)S(1)} %constant_dynamic-update-slice_fusion.early_ref), kind=kOutput, calls=%fused_computation.25 | convolution fusion | flops 134609920 | bytes 1708544 | tf_op jit(solution)/shard_map/dot_general | solution.py:91
  20.5 0.1 exponential_reduce_fusion
  20.6 0.0 copy-start.2
  20.6 0.5 %collective-permute-done.4.last_ref = bf16[128,640]{1,0:T(8,128)(2,1)S(1)} collective-permute-done((bf16[128,640]{1,0:T(8,128)(2,1)S(1)}, bf16[128,640]{1,0:T(8,128)(2,1)S(1)}, u32[]{:S(2)}, u32[]{:S(2)}) %collective-permute-start.4) | collective-permute-done | bytes 163872 | tf_op jit(solution)/shard_map/ppermute | solution.py:16
  21.1 1.5 %shard_map.68 = (f32[32,16]{1,0:T(8,128)S(1)}, f32[1,1024]{1,0:T(1,128)}) custom-call(s32[1]{0:T(128)} %bitcast.me_ref, bf16[1024,512]{1,0:T(8,128)(2,1)S(1)} %copy-done, bf16[128,640]{1,0:T(8,128)(2,1)S(1)} %constant_dynamic-update-slice_fusion.early_ref, bf16[128,640]{1,0:T(8,128)(2,1)S(1)} %collective-permute-done.4.last_ref, ...), custom_call_target="tpu_custom_call" | custom-call | tf_op jit(solution)/shard_map/pallas_call | solution.py:101
  22.6 13.1 %all_to_all.12 = f32[32,1,16]{2,1,0:T(1,128)S(1)} all-to-all(f32[32,1,16]{2,1,0:T(1,128)S(1)} %bitcast.13), channel_id=1, replica_groups=mesh['group'=8,'blk'=4] {'group','blk'}, dimensions={0} | all-to-all | bytes 4096 | tf_op jit(solution)/shard_map/all_to_all | solution.py:113
  35.8 0.1 fusion.2
  35.9 0.0 copy-done.2
  35.9 0.5 %subtract_multiply_fusion = f32[8]{0:T(128)} fusion(f32[8]{0:T(128)S(1)} %copy-done.2, f32[8]{0:T(128)S(1)} %slice_reduce_fusion, f32[8]{0:T(128)S(1)} %fusion.2), kind=kLoop, calls=%fused_computation.23 | loop fusion | flops 24 | bytes 128 | tf_op jit(solution)/shard_map/mul | solution.py:118
  (14 shorter events, 0.1 us)
Async XLA Ops:
  0.6 19.3 %copy-start = (bf16[1024,512]{1,0:T(8,128)(2,1)S(1)}, bf16[1024,512]{1,0:T(8,128)(2,1)}, u32[]{:S(2)}) copy-start(bf16[1024,512]{1,0:T(8,128)(2,1)} %src_ref.1) | copy-start | bytes 3145732
  0.6 6.4 %copy-start.1 = (f32[1024]{0:T(1024)S(1)}, f32[1024]{0:T(1024)}, u32[]{:S(2)}) copy-start(f32[1024]{0:T(1024)} %param.8) | copy-start | bytes 12292
  1.5 5.7 %collective-permute-start = (bf16[8,640]{1,0:T(8,128)(2,1)S(1)}, bf16[8,640]{1,0:T(8,128)(2,1)S(1)}, u32[]{:S(2)}, u32[]{:S(2)}) collective-permute-start(bf16[8,640]{1,0:T(8,128)(2,1)S(1)} %pad_select_fusion), channel_id=1, source_target_pairs={{0,16},{1,17},{2,18},{3,19},{4,20},{5,21},{6,22},{7,23},{8,24},{9,... | collective-permute-start | bytes 30728 | tf_op jit(solution)/shard_map/ppermute | solution.py:16
  7.2 3.8 %collective-permute-start.1 = (bf16[16,640]{1,0:T(8,128)(2,1)S(1)}, bf16[16,640]{1,0:T(8,128)(2,1)S(1)}, u32[]{:S(2)}, u32[]{:S(2)}) collective-permute-start(bf16[16,640]{1,0:T(8,128)(2,1)S(1)} %pad_maximum_fusion.2), channel_id=1, source_target_pairs={{0,8},{1,9},{2,10},{3,11},{4,12},{5,13},{6,14},{7,15},{8,0},{9,1},... | collective-permute-start | bytes 61448 | tf_op jit(solution)/shard_map/ppermute | solution.py:16
  11.0 4.0 %collective-permute-start.2 = (bf16[32,640]{1,0:T(8,128)(2,1)S(1)}, bf16[32,640]{1,0:T(8,128)(2,1)S(1)}, u32[]{:S(2)}, u32[]{:S(2)}) collective-permute-start(bf16[32,640]{1,0:T(8,128)(2,1)S(1)} %pad_maximum_fusion.1), channel_id=1, source_target_pairs={{0,4},{1,5},{2,6},{3,7},{4,0},{5,1},{6,2},{7,3},{8,12},{9,13},{10,... | collective-permute-start | bytes 122888 | tf_op jit(solution)/shard_map/ppermute | solution.py:16
  15.0 4.5 %collective-permute-start.3 = (bf16[64,640]{1,0:T(8,128)(2,1)S(1)}, bf16[64,640]{1,0:T(8,128)(2,1)S(1)}, u32[]{:S(2)}, u32[]{:S(2)}) collective-permute-start(bf16[64,640]{1,0:T(8,128)(2,1)S(1)} %pad_maximum_fusion), channel_id=1, source_target_pairs={{0,2},{1,3},{2,0},{3,1},{4,6},{5,7},{6,4},{7,5},{8,10},{9,11},{10,... | collective-permute-start | bytes 245768 | tf_op jit(solution)/shard_map/ppermute | solution.py:16
  19.6 1.5 %collective-permute-start.4 = (bf16[128,640]{1,0:T(8,128)(2,1)S(1)}, bf16[128,640]{1,0:T(8,128)(2,1)S(1)}, u32[]{:S(2)}, u32[]{:S(2)}) collective-permute-start(bf16[128,640]{1,0:T(8,128)(2,1)S(1)} %constant_dynamic-update-slice_fusion.early_ref), channel_id=1, source_target_pairs={{0,1},{1,0},{2,3},{3,2},{4,5},{5,4},{6,7},{7,6},{8,9},{9,8},{10,11... | collective-permute-start | bytes 491528 | tf_op jit(solution)/shard_map/ppermute | solution.py:16
  20.6 15.3 %copy-start.2 = (f32[8]{0:T(128)S(1)}, f32[8]{0:T(128)}, u32[]{:S(2)}) copy-start(f32[8]{0:T(128)} %param.9) | copy-start | bytes 100

commit v11 on v10

--- a/solution.py
+++ b/solution.py
@@ -60,6 +60,7 @@
     if (1 << levels) != count:
         raise ValueError("count not pow2")
     order = list(reversed(range(levels)))
+    order[0], order[1] = order[1], order[0]
     features = sources.shape[1]
     factor = 2.0 / (features * epsilon)
 

time: 36.6 us -> 36.7 us (level)
  no operation moved by 1% of the time
where the time goes in v11:
time: 36.7 us; the launch traced here: 36.5 us
  blocking collectives  13.2 us (36%)
  starting transfers between devices  9.87 us (27%)
  waiting for transfers between devices  7.11 us (19%)
  other arithmetic  3.35 us (9%)
  Pallas kernels  1.52 us (4%)
  between operations  0.76 us (2%)
  matrix products  0.49 us (1%)
    all_to_all x1, blocking collectives, per_device(): part = lax.all_to_all(columns, AXES, 0, 0, tiled=True)  13.2 us
    ppermute x5, starting transfers between devices, exchange(): return lax.ppermute(x, AXES, route)  9.87 us
    ppermute x5, waiting for transfers between devices, exchange(): return lax.ppermute(x, AXES, route)  7.11 us
    pallas_call x1, Pallas kernels, per_device(): pl.pallas_call(functools.partial(tail, features, factor, width, order), o...  1.52 us
    reduce_sum x1, other arithmetic, per_device(): jnp.sum(jnp.square(sources.astype(jnp.float32)), 1) / features  1.5 us
    select_n x1, other arithmetic, per_device(): jnp.where(lane < features, jnp.pad(targets, ((0, 0), (0, 128))), target_p...  0.86 us
  transfers between devices with their start and end apart: 5, of which 5 were waited for; matrix products, arithmetic and copies ran while one was open for 6% of the time, Pallas kernels for 0%

profile of v11, /device:TPU:0, one launch (start us, length us, event | category | flops | bytes accessed | tf_op | source)
XLA Modules:
  0.0 36.5 jit_solution(17476624692221838432)
XLA Ops:
  0.6 0.0 copy-start
  0.6 0.0 copy-start.1
  0.7 0.9 %pad_select_fusion = bf16[8,640]{1,0:T(8,128)(2,1)S(1)} fusion(bf16[8,512]{1,0:T(8,128)(2,1)} %param.6, pred[640]{0:T(1024)(128)(4,1)S(1)} %iota_compare_fusion, bf16[8]{0:T(256)(128)(2,1)} %param.7), kind=kLoop, calls=%fused_computation.18 | loop fusion | flops 5120 | bytes 19088 | tf_op jit(solution)/shard_map/jit(_where)/select_n | solution.py:69
  1.5 3.0 %collective-permute-start = (bf16[8,640]{1,0:T(8,128)(2,1)S(1)}, bf16[8,640]{1,0:T(8,128)(2,1)S(1)}, u32[]{:S(2)}, u32[]{:S(2)}) collective-permute-start(bf16[8,640]{1,0:T(8,128)(2,1)S(1)} %pad_select_fusion), channel_id=1, source_target_pairs={{0,8},{1,9},{2,10},{3,11},{4,12},{5,13},{6,14},{7,15},{8,0},{9,1},... | collective-permute-start | bytes 30728 | tf_op jit(solution)/shard_map/ppermute | solution.py:16
  4.5 1.5 %multiply_reduce_fusion = f32[1024]{0:T(1024)S(1)} fusion(bf16[1024,512]{1,0:T(8,128)(2,1)} %src_ref.1), kind=kLoop, calls=%fused_computation | loop fusion | flops 1571840 | bytes 1052672 | tf_op jit(solution)/shard_map/reduce_sum | solution.py:78
  6.1 0.0 copy-done.1
  6.1 0.1 collective-permute-done
  6.2 3.0 %collective-permute-start.1 = (bf16[16,640]{1,0:T(8,128)(2,1)S(1)}, bf16[16,640]{1,0:T(8,128)(2,1)S(1)}, u32[]{:S(2)}, u32[]{:S(2)}) collective-permute-start(bf16[16,640]{1,0:T(8,128)(2,1)S(1)} %pad_maximum_fusion.2), channel_id=1, source_target_pairs={{0,16},{1,17},{2,18},{3,19},{4,20},{5,21},{6,22},{7,23},{8,24},{9,... | collective-permute-start | bytes 61448 | tf_op jit(solution)/shard_map/ppermute | solution.py:16
  9.2 1.8 %collective-permute-done.1 = bf16[16,640]{1,0:T(8,128)(2,1)S(1)} collective-permute-done((bf16[16,640]{1,0:T(8,128)(2,1)S(1)}, bf16[16,640]{1,0:T(8,128)(2,1)S(1)}, u32[]{:S(2)}, u32[]{:S(2)}) %collective-permute-start.1) | collective-permute-done | bytes 20512 | tf_op jit(solution)/shard_map/ppermute | solution.py:16
  11.0 1.8 %collective-permute-start.2 = (bf16[32,640]{1,0:T(8,128)(2,1)S(1)}, bf16[32,640]{1,0:T(8,128)(2,1)S(1)}, u32[]{:S(2)}, u32[]{:S(2)}) collective-permute-start(bf16[32,640]{1,0:T(8,128)(2,1)S(1)} %pad_maximum_fusion.1), channel_id=1, source_target_pairs={{0,4},{1,5},{2,6},{3,7},{4,0},{5,1},{6,2},{7,3},{8,12},{9,13},{10,... | collective-permute-start | bytes 122888 | tf_op jit(solution)/shard_map/ppermute | solution.py:16
  12.8 2.2 %collective-permute-done.2 = bf16[32,640]{1,0:T(8,128)(2,1)S(1)} collective-permute-done((bf16[32,640]{1,0:T(8,128)(2,1)S(1)}, bf16[32,640]{1,0:T(8,128)(2,1)S(1)}, u32[]{:S(2)}, u32[]{:S(2)}) %collective-permute-start.2) | collective-permute-done | bytes 40992 | tf_op jit(solution)/shard_map/ppermute | solution.py:16
  15.0 1.9 %collective-permute-start.3 = (bf16[64,640]{1,0:T(8,128)(2,1)S(1)}, bf16[64,640]{1,0:T(8,128)(2,1)S(1)}, u32[]{:S(2)}, u32[]{:S(2)}) collective-permute-start(bf16[64,640]{1,0:T(8,128)(2,1)S(1)} %pad_maximum_fusion), channel_id=1, source_target_pairs={{0,2},{1,3},{2,0},{3,1},{4,6},{5,7},{6,4},{7,5},{8,10},{9,11},{10,... | collective-permute-start | bytes 245768 | tf_op jit(solution)/shard_map/ppermute | solution.py:16
  16.9 2.6 %collective-permute-done.3 = bf16[64,640]{1,0:T(8,128)(2,1)S(1)} collective-permute-done((bf16[64,640]{1,0:T(8,128)(2,1)S(1)}, bf16[64,640]{1,0:T(8,128)(2,1)S(1)}, u32[]{:S(2)}, u32[]{:S(2)}) %collective-permute-start.3) | collective-permute-done | bytes 81952 | tf_op jit(solution)/shard_map/ppermute | solution.py:16
  19.5 0.1 multiply_reduce_fusion.1
  19.6 0.1 collective-permute-start.4
  19.7 0.1 copy.11
  19.8 0.1 subtract_reduce_fusion
  20.0 0.0 copy-done
  20.0 0.5 %fusion.3 = (f32[1024]{0:T(1024)S(1)}, f32[128,1024]{1,0:T(8,128)S(1)}) fusion(f32[128]{0:T(128)S(1)} %subtract_reduce_fusion, bf16[1024,512]{1,0:T(8,128)(2,1)S(1)} %copy-done, bf16[128,640]{1,0:T(8,128)(2,1)S(1)} %constant_dynamic-update-slice_fusion.early_ref), kind=kOutput, calls=%fused_computation.25 | convolution fusion | flops 134609920 | bytes 1708544 | tf_op jit(solution)/shard_map/dot_general | solution.py:92
  20.5 0.1 exponential_reduce_fusion
  20.6 0.0 copy-start.2
  20.6 0.5 %collective-permute-done.4.last_ref = bf16[128,640]{1,0:T(8,128)(2,1)S(1)} collective-permute-done((bf16[128,640]{1,0:T(8,128)(2,1)S(1)}, bf16[128,640]{1,0:T(8,128)(2,1)S(1)}, u32[]{:S(2)}, u32[]{:S(2)}) %collective-permute-start.4) | collective-permute-done | bytes 163872 | tf_op jit(solution)/shard_map/ppermute | solution.py:16
  21.1 1.5 %shard_map.68 = (f32[32,16]{1,0:T(8,128)S(1)}, f32[1,1024]{1,0:T(1,128)}) custom-call(s32[1]{0:T(128)} %bitcast.me_ref, bf16[1024,512]{1,0:T(8,128)(2,1)S(1)} %copy-done, bf16[128,640]{1,0:T(8,128)(2,1)S(1)} %constant_dynamic-update-slice_fusion.early_ref, bf16[128,640]{1,0:T(8,128)(2,1)S(1)} %collective-permute-done.4.last_ref, ...), custom_call_target="tpu_custom_call" | custom-call | tf_op jit(solution)/shard_map/pallas_call | solution.py:102
  22.6 13.2 %all_to_all.12 = f32[32,1,16]{2,1,0:T(1,128)S(1)} all-to-all(f32[32,1,16]{2,1,0:T(1,128)S(1)} %bitcast.13), channel_id=1, replica_groups=mesh['group'=8,'blk'=4] {'group','blk'}, dimensions={0} | all-to-all | bytes 4096 | tf_op jit(solution)/shard_map/all_to_all | solution.py:114
  35.9 0.1 fusion.2
  36.0 0.0 copy-done.2
  36.0 0.5 %subtract_multiply_fusion = f32[8]{0:T(128)} fusion(f32[8]{0:T(128)S(1)} %copy-done.2, f32[8]{0:T(128)S(1)} %slice_reduce_fusion, f32[8]{0:T(128)S(1)} %fusion.2), kind=kLoop, calls=%fused_computation.23 | loop fusion | flops 24 | bytes 128 | tf_op jit(solution)/shard_map/mul | solution.py:119
  (14 shorter events, 0.1 us)
Async XLA Ops:
  0.6 19.3 %copy-start = (bf16[1024,512]{1,0:T(8,128)(2,1)S(1)}, bf16[1024,512]{1,0:T(8,128)(2,1)}, u32[]{:S(2)}) copy-start(bf16[1024,512]{1,0:T(8,128)(2,1)} %src_ref.1) | copy-start | bytes 3145732
  0.6 5.4 %copy-start.1 = (f32[1024]{0:T(1024)S(1)}, f32[1024]{0:T(1024)}, u32[]{:S(2)}) copy-start(f32[1024]{0:T(1024)} %param.8) | copy-start | bytes 12292
  1.5 4.7 %collective-permute-start = (bf16[8,640]{1,0:T(8,128)(2,1)S(1)}, bf16[8,640]{1,0:T(8,128)(2,1)S(1)}, u32[]{:S(2)}, u32[]{:S(2)}) collective-permute-start(bf16[8,640]{1,0:T(8,128)(2,1)S(1)} %pad_select_fusion), channel_id=1, source_target_pairs={{0,8},{1,9},{2,10},{3,11},{4,12},{5,13},{6,14},{7,15},{8,0},{9,1},... | collective-permute-start | bytes 30728 | tf_op jit(solution)/shard_map/ppermute | solution.py:16
  6.2 4.8 %collective-permute-start.1 = (bf16[16,640]{1,0:T(8,128)(2,1)S(1)}, bf16[16,640]{1,0:T(8,128)(2,1)S(1)}, u32[]{:S(2)}, u32[]{:S(2)}) collective-permute-start(bf16[16,640]{1,0:T(8,128)(2,1)S(1)} %pad_maximum_fusion.2), channel_id=1, source_target_pairs={{0,16},{1,17},{2,18},{3,19},{4,20},{5,21},{6,22},{7,23},{8,24},{9,... | collective-permute-start | bytes 61448 | tf_op jit(solution)/shard_map/ppermute | solution.py:16
  11.0 4.0 %collective-permute-start.2 = (bf16[32,640]{1,0:T(8,128)(2,1)S(1)}, bf16[32,640]{1,0:T(8,128)(2,1)S(1)}, u32[]{:S(2)}, u32[]{:S(2)}) collective-permute-start(bf16[32,640]{1,0:T(8,128)(2,1)S(1)} %pad_maximum_fusion.1), channel_id=1, source_target_pairs={{0,4},{1,5},{2,6},{3,7},{4,0},{5,1},{6,2},{7,3},{8,12},{9,13},{10,... | collective-permute-start | bytes 122888 | tf_op jit(solution)/shard_map/ppermute | solution.py:16
  15.0 4.5 %collective-permute-start.3 = (bf16[64,640]{1,0:T(8,128)(2,1)S(1)}, bf16[64,640]{1,0:T(8,128)(2,1)S(1)}, u32[]{:S(2)}, u32[]{:S(2)}) collective-permute-start(bf16[64,640]{1,0:T(8,128)(2,1)S(1)} %pad_maximum_fusion), channel_id=1, source_target_pairs={{0,2},{1,3},{2,0},{3,1},{4,6},{5,7},{6,4},{7,5},{8,10},{9,11},{10,... | collective-permute-start | bytes 245768 | tf_op jit(solution)/shard_map/ppermute | solution.py:16
  19.6 1.5 %collective-permute-start.4 = (bf16[128,640]{1,0:T(8,128)(2,1)S(1)}, bf16[128,640]{1,0:T(8,128)(2,1)S(1)}, u32[]{:S(2)}, u32[]{:S(2)}) collective-permute-start(bf16[128,640]{1,0:T(8,128)(2,1)S(1)} %constant_dynamic-update-slice_fusion.early_ref), channel_id=1, source_target_pairs={{0,1},{1,0},{2,3},{3,2},{4,5},{5,4},{6,7},{7,6},{8,9},{9,8},{10,11... | collective-permute-start | bytes 491528 | tf_op jit(solution)/shard_map/ppermute | solution.py:16
  20.6 15.4 %copy-start.2 = (f32[8]{0:T(128)S(1)}, f32[8]{0:T(128)}, u32[]{:S(2)}) copy-start(f32[8]{0:T(128)} %param.9) | copy-start | bytes 100

commit v12 on v10

v12 whole, which is shorter than its diff:
```python
import functools

import jax
import jax.numpy as jnp
from jax import lax
from jax.sharding import PartitionSpec as P
from jax.experimental import pallas as pl
from jax.experimental.pallas import tpu as pltpu

epsilon = 0.05
AXES = ("group", "blk")


def exchange(x, bit, count):
    route = [(i, i ^ (1 << bit)) for i in range(count)]
    return lax.ppermute(x, AXES, route)


def tail(features, factor, width, src_ref, rows_ref, terms_ref, col_ref, pot_ref):
    block = rows_ref[...]
    rows = block[:, :features]
    pots = block[:, features:features + 1].astype(jnp.float32)
    offset = pots / epsilon - jnp.sum(jnp.square(rows.astype(jnp.float32)), 1, keepdims=True) / (
        features * epsilon
    )
    logits = lax.dot_general(
        rows, src_ref[...], (((1,), (1,)), ((), ())), preferred_element_type=jnp.float32
    ) * factor + offset
    row_max = jnp.max(logits, 0, keepdims=True)
    row_lse = row_max + jnp.log(jnp.sum(jnp.exp(logits - row_max), 0, keepdims=True))
    dual = terms_ref[1:2, :] - row_lse
    pot_ref[...] = epsilon * dual + terms_ref[0:1, :]
    column = logits - pots / epsilon + dual
    col_max = jnp.max(column, 1, keepdims=True)
    col_sum = jnp.sum(jnp.exp(column - col_max), 1, keepdims=True)
    diagonal = lax.broadcasted_iota(jnp.int32, (width, width), 0) == lax.broadcasted_iota(
        jnp.int32, (width, width), 1
    )
    for owner in range(block.shape[0] // width):
        first = owner * width
        for lanes, stat in ((0, col_max), (width, col_sum)):
            piece = jnp.where(diagonal, stat[first:first + width], 0.0)
            col_ref[owner:owner + 1, lanes:lanes + width] = jnp.sum(piece, 0, keepdims=True)


def per_device(sources, targets, target_potential, log_source_mass, log_target_mass):
    count = lax.axis_size("group") * lax.axis_size("blk")
    levels = count.bit_length() - 1
    if (1 << levels) != count:
        raise ValueError("count not pow2")
    order = list(reversed(range(levels)))
    features = sources.shape[1]
    factor = 2.0 / (features * epsilon)

    lane = lax.broadcasted_iota(jnp.int32, (targets.shape[0], features + 128), 1)
    held = lax.optimization_barrier(
        jnp.where(
            lane < features,
            jnp.pad(targets, ((0, 0), (0, 128))),
            target_potential[:, None],
        )
    )
    source_terms = lax.optimization_barrier(
        jnp.stack(
            [
                jnp.sum(jnp.square(sources.astype(jnp.float32)), 1) / features,
                log_source_mass,
            ]
        )
    )
    everything = lax.all_to_all(
        jnp.broadcast_to(held[None], (count,) + held.shape), AXES, 0, 0, tiled=True
    ).reshape(count * held.shape[0], held.shape[1])

    width = targets.shape[0]
    vmem = pl.BlockSpec(memory_space=pltpu.VMEM)
    columns, source_potential = pl.pallas_call(
        functools.partial(tail, features, factor, width),
        out_shape=(
            jax.ShapeDtypeStruct((count, 2 * width), jnp.float32),
            jax.ShapeDtypeStruct((1, sources.shape[0]), jnp.float32),
        ),
        in_specs=[vmem] * 3,
        out_specs=(vmem, vmem),
        compiler_params=pltpu.CompilerParams(vmem_limit_bytes=24 * 1024 * 1024),
    )(sources, everything, source_terms)
    source_potential = source_potential.reshape(-1)

    part = lax.all_to_all(columns, AXES, 0, 0, tiled=True)
    owned_max = jnp.max(part[:, :width], 0)
    owned_sum = jnp.sum(part[:, width:] * jnp.exp(part[:, :width] - owned_max[None, :]), 0)
    part = (owned_max, owned_sum)

    target_update = epsilon * (log_target_mass - (part[0] + jnp.log(part[1])))
    return (source_potential, target_update)


def solution(mesh):
    return jax.shard_map(
        per_device,
        mesh=mesh,
        in_specs=(
            P(AXES, None),
            P(AXES, None),
            P(AXES),
            P(AXES),
            P(AXES),
        ),
        out_specs=(P(AXES), P(AXES)),
        check_vma=False,
    )
```

time: 36.6 us -> 33.4 us (0.913)
  blocking collectives: 13.1 us -> 9.37 us
  waiting for transfers between devices: 7.23 us -> 10.4 us
  starting transfers between devices: 9.76 us -> 7.3 us
  local copies, waits for them, and re-layouts: 0.17 us -> 0.75 us
  matrix products: 0.49 us -> 0 us
    all_to_all x0 -> x1, waiting for transfers between devices: none -> 10.4 us  [per_device(): lax.all_to_all(jnp.broadcast_to(held[None], (count,) + held.shape), AXES,...]
    ppermute x5 -> x0, starting transfers between devices: 9.76 us -> none  [exchange(): return lax.ppermute(x, AXES, route)]
    all_to_all x0 -> x1, starting transfers between devices: none -> 7.3 us  [per_device(): lax.all_to_all(jnp.broadcast_to(held[None], (count,) + held.shape), AXES,...]
    ppermute x5 -> x0, waiting for transfers between devices: 7.23 us -> none  [exchange(): return lax.ppermute(x, AXES, route)]
    all_to_all x1, blocking collectives: 13.1 us -> 9.37 us  [per_device(): part = lax.all_to_all(columns, AXES, 0, 0, tiled=True)]
    broadcast_in_dim x0 -> x1, local copies, waits for them, and re-layouts: none -> 0.74 us  [per_device(): jnp.broadcast_to(held[None], (count,) + held.shape)]
    dot_general x1 -> x0, matrix products: 0.49 us -> none  [per_device(): lax.dot_general(early_rows, sources, (((1,), (1,)), ((), ())), preferred_...]
  transfers between devices with their start and end apart: 5 -> 1, of which waited for: 5 -> 1; matrix products, arithmetic and copies ran while one was open for 6% -> 5% of each run, Pallas kernels for 0% -> 0%
where the time goes in v12:
time: 33.4 us; the launch traced here: 33.1 us
  waiting for transfers between devices  10.4 us (31%)
  blocking collectives  9.37 us (28%)
  starting transfers between devices  7.3 us (22%)
  other arithmetic  3.02 us (9%)
  Pallas kernels  1.58 us (5%)
  local copies, waits for them, and re-layouts  0.75 us (2%)
  between operations  0.7 us (2%)
    all_to_all x1, waiting for transfers between devices, per_device(): lax.all_to_all(jnp.broadcast_to(held[None], (count,) + held.shape), AXES,...  10.4 us
    all_to_all x1, blocking collectives, per_device(): part = lax.all_to_all(columns, AXES, 0, 0, tiled=True)  9.37 us
    all_to_all x1, starting transfers between devices, per_device(): lax.all_to_all(jnp.broadcast_to(held[None], (count,) + held.shape), AXES,...  7.3 us
    pallas_call x1, Pallas kernels, per_device(): pl.pallas_call(functools.partial(tail, features, factor, width), out_shap...  1.58 us
    reduce_sum x1, other arithmetic, per_device(): jnp.sum(jnp.square(sources.astype(jnp.float32)), 1) / features  1.5 us
    select_n x1, other arithmetic, per_device(): jnp.where(lane < features, jnp.pad(targets, ((0, 0), (0, 128))), target_p...  0.86 us
    broadcast_in_dim x1, local copies, waits for them, and re-layouts, per_device(): jnp.broadcast_to(held[None], (count,) + held.shape)  0.74 us
  transfers between devices with their start and end apart: 1, of which 1 were waited for; matrix products, arithmetic and copies ran while one was open for 5% of the time, Pallas kernels for 0%

profile of v12, /device:TPU:0, one launch (start us, length us, event | category | flops | bytes accessed | tf_op | source)
XLA Modules:
  0.0 33.1 jit_solution(12109719929745963740)
XLA Ops:
  0.6 0.0 copy-start.1
  0.7 0.0 copy-start
  0.7 0.9 %pad_select_fusion = bf16[8,640]{1,0:T(8,128)(2,1)S(1)} fusion(bf16[8,512]{1,0:T(8,128)(2,1)} %param.6, pred[640]{0:T(1024)(128)(4,1)S(1)} %iota_compare_fusion, bf16[8]{0:T(256)(128)(2,1)} %param.7), kind=kLoop, calls=%fused_computation.4 | loop fusion | flops 5120 | bytes 19088 | tf_op jit(solution)/shard_map/jit(_where)/select_n | solution.py:57
  1.5 0.7 %broadcast_in_dim.11 = bf16[32,8,640]{2,1,0:T(8,128)(2,1)} broadcast(bf16[8,640]{1,0:T(8,128)(2,1)S(1)} %pad_select_fusion), dimensions={1,2} | broadcast | bytes 337920 | tf_op jit(solution)/shard_map/broadcast_in_dim | solution.py:72
  2.3 7.3 %all-to-all-start = ((bf16[32,8,640]{2,1,0:T(8,128)(2,1)}), bf16[32,8,640]{2,1,0:T(8,128)(2,1)S(1)}, u32[]{:S(2)}, u32[]{:S(2)}) async-start(bf16[32,8,640]{2,1,0:T(8,128)(2,1)} %broadcast_in_dim.11), calls=%async_computation | async-start | bytes 655360 | tf_op jit(solution)/shard_map/all_to_all | solution.py:71
  9.6 0.0 copy-start.2
  9.6 1.5 %multiply_reduce_fusion = f32[1024]{0:T(1024)S(1)} fusion(bf16[1024,512]{1,0:T(8,128)(2,1)} %src_ref.1), kind=kLoop, calls=%fused_computation | loop fusion | flops 1571840 | bytes 1052672 | tf_op jit(solution)/shard_map/reduce_sum | solution.py:66
  11.1 0.0 copy-done.1
  11.1 10.4 %all-to-all-done = bf16[32,8,640]{2,1,0:T(8,128)(2,1)S(1)} async-done(((bf16[32,8,640]{2,1,0:T(8,128)(2,1)}), bf16[32,8,640]{2,1,0:T(8,128)(2,1)S(1)}, u32[]{:S(2)}, u32[]{:S(2)}) %all-to-all-start) | async-done | bytes 327712 | tf_op jit(solution)/shard_map/all_to_all | solution.py:71
  21.6 0.0 copy-done
  21.6 1.6 %shard_map.68 = (f32[32,16]{1,0:T(8,128)S(1)}, f32[1,1024]{1,0:T(1,128)}) custom-call(bf16[1024,512]{1,0:T(8,128)(2,1)S(1)} %copy-done, bf16[256,640]{1,0:T(8,128)(2,1)S(1)} %bitcast.8, f32[2,1024]{1,0:T(2,128)S(1)} %pad_maximum_fusion.terms_ref), custom_call_target="tpu_custom_call" | custom-call | tf_op jit(solution)/shard_map/pallas_call | solution.py:77
  23.1 9.4 %all_to_all.17 = f32[32,1,16]{2,1,0:T(1,128)S(1)} all-to-all(f32[32,1,16]{2,1,0:T(1,128)S(1)} %bitcast.9), channel_id=1, replica_groups=mesh['group'=8,'blk'=4] {'group','blk'}, dimensions={0} | all-to-all | bytes 4096 | tf_op jit(solution)/shard_map/all_to_all | solution.py:89
  32.5 0.1 fusion
  32.6 0.0 copy-done.2
  32.6 0.5 %subtract_multiply_fusion = f32[8]{0:T(128)} fusion(f32[8]{0:T(128)S(1)} %copy-done.2, f32[8]{0:T(128)S(1)} %slice_reduce_fusion, f32[8]{0:T(128)S(1)} %fusion), kind=kLoop, calls=%fused_computation.8 | loop fusion | flops 24 | bytes 128 | tf_op jit(solution)/shard_map/mul | solution.py:94
  (4 shorter events, 0.0 us)
Async XLA Ops:
  0.6 10.5 %copy-start.1 = (f32[1024]{0:T(1024)S(1)}, f32[1024]{0:T(1024)}, u32[]{:S(2)}) copy-start(f32[1024]{0:T(1024)} %param.8) | copy-start | bytes 12292
  0.7 20.9 %copy-start = (bf16[1024,512]{1,0:T(8,128)(2,1)S(1)}, bf16[1024,512]{1,0:T(8,128)(2,1)}, u32[]{:S(2)}) copy-start(bf16[1024,512]{1,0:T(8,128)(2,1)} %src_ref.1) | copy-start | bytes 3145732
  2.3 19.3 %all-to-all-start = ((bf16[32,8,640]{2,1,0:T(8,128)(2,1)}), bf16[32,8,640]{2,1,0:T(8,128)(2,1)S(1)}, u32[]{:S(2)}, u32[]{:S(2)}) async-start(bf16[32,8,640]{2,1,0:T(8,128)(2,1)} %broadcast_in_dim.11), calls=%async_computation | async-start | bytes 655360 | tf_op jit(solution)/shard_map/all_to_all | solution.py:71
  9.6 23.1 %copy-start.2 = (f32[8]{0:T(128)S(1)}, f32[8]{0:T(128)}, u32[]{:S(2)}) copy-start(f32[8]{0:T(128)} %param.9) | copy-start | bytes 100

commit v13 on v12

--- a/solution.py
+++ b/solution.py
@@ -52,13 +52,11 @@
     features = sources.shape[1]
     factor = 2.0 / (features * epsilon)
 
-    lane = lax.broadcasted_iota(jnp.int32, (targets.shape[0], features + 128), 1)
-    held = lax.optimization_barrier(
-        jnp.where(
-            lane < features,
-            jnp.pad(targets, ((0, 0), (0, 128))),
-            target_potential[:, None],
-        )
+    lane = lax.broadcasted_iota(jnp.int32, (count, targets.shape[0], features + 128), 2)
+    outgoing = jnp.where(
+        lane < features,
+        jnp.pad(targets, ((0, 0), (0, 128)))[None],
+        target_potential[None, :, None],
     )
     source_terms = lax.optimization_barrier(
         jnp.stack(
@@ -68,9 +66,9 @@
             ]
         )
     )
-    everything = lax.all_to_all(
-        jnp.broadcast_to(held[None], (count,) + held.shape), AXES, 0, 0, tiled=True
-    ).reshape(count * held.shape[0], held.shape[1])
+    everything = lax.all_to_all(outgoing, AXES, 0, 0, tiled=True).reshape(
+        count * targets.shape[0], features + 128
+    )
 
     width = targets.shape[0]
     vmem = pl.BlockSpec(memory_space=pltpu.VMEM)

time: 33.4 us -> 34.1 us (1.021)
  other arithmetic: 3.02 us -> 3.62 us
    pad x0 -> x1, local copies, waits for them, and re-layouts: none -> 0.79 us  [per_device(): jnp.pad(targets, ((0, 0), (0, 128)))[None]]
    broadcast_in_dim x1 -> x0, local copies, waits for them, and re-layouts: 0.74 us -> none  [per_device(): jnp.broadcast_to(held[None], (count,) + held.shape)]
    select_n x1, other arithmetic: 0.86 us -> 1.46 us  [per_device(): jnp.where(lane < features, jnp.pad(targets, ((0, 0), (0, 128)))[None], ta...]
  transfers between devices with their start and end apart: 1 -> 1, of which waited for: 1 -> 1; matrix products, arithmetic and copies ran while one was open for 5% -> 4% of each run, Pallas kernels for 0% -> 0%
where the time goes in v13:
time: 34.1 us; the launch traced here: 33.8 us
  waiting for transfers between devices  10.4 us (30%)
  blocking collectives  9.36 us (27%)
  starting transfers between devices  7.3 us (21%)
  other arithmetic  3.62 us (11%)
  Pallas kernels  1.58 us (5%)
  local copies, waits for them, and re-layouts  0.81 us (2%)
  between operations  0.7 us (2%)
    all_to_all x1, waiting for transfers between devices, per_device(): lax.all_to_all(outgoing, AXES, 0, 0, tiled=True)  10.4 us
    all_to_all x1, blocking collectives, per_device(): part = lax.all_to_all(columns, AXES, 0, 0, tiled=True)  9.36 us
    all_to_all x1, starting transfers between devices, per_device(): lax.all_to_all(outgoing, AXES, 0, 0, tiled=True)  7.3 us
    pallas_call x1, Pallas kernels, per_device(): pl.pallas_call(functools.partial(tail, features, factor, width), out_shap...  1.58 us
    reduce_sum x1, other arithmetic, per_device(): jnp.sum(jnp.square(sources.astype(jnp.float32)), 1) / features  1.5 us
    select_n x1, other arithmetic, per_device(): jnp.where(lane < features, jnp.pad(targets, ((0, 0), (0, 128)))[None], ta...  1.46 us
    pad x1, local copies, waits for them, and re-layouts, per_device(): jnp.pad(targets, ((0, 0), (0, 128)))[None]  0.79 us
  transfers between devices with their start and end apart: 1, of which 1 were waited for; matrix products, arithmetic and copies ran while one was open for 4% of the time, Pallas kernels for 0%

profile of v13, /device:TPU:0, one launch (start us, length us, event | category | flops | bytes accessed | tf_op | source)
XLA Modules:
  0.0 33.8 jit_solution(2370221372402657314)
XLA Ops:
  0.6 0.0 copy-start.1
  0.7 0.0 copy-start
  0.7 0.8 %pad.4 = bf16[8,640]{1,0:T(8,128)(2,1)S(1)} pad(bf16[8,512]{1,0:T(8,128)(2,1)} %param.6, bf16[]{:T(256)} %constant.3.clone.1), padding=0_0x0_128 | pad | bytes 18434 | tf_op jit(solution)/shard_map/jit(_pad)/pad | solution.py:58
  1.5 1.5 %broadcast_select_fusion = bf16[32,8,640]{2,1,0:T(8,128)(2,1)} fusion(pred[640]{0:T(1024)(128)(4,1)S(1)} %iota_compare_fusion, bf16[8]{0:T(256)(128)(2,1)} %param.7, bf16[8,640]{1,0:T(8,128)(2,1)S(1)} %pad.4), kind=kLoop, calls=%fused_computation.1 | loop fusion | flops 163840 | bytes 338576 | tf_op jit(solution)/shard_map/jit(_where)/select_n | solution.py:56
  2.9 7.3 %all-to-all-start = ((bf16[32,8,640]{2,1,0:T(8,128)(2,1)}), bf16[32,8,640]{2,1,0:T(8,128)(2,1)S(1)}, u32[]{:S(2)}, u32[]{:S(2)}) async-start(bf16[32,8,640]{2,1,0:T(8,128)(2,1)} %broadcast_select_fusion), calls=%async_computation | async-start | bytes 655360 | tf_op jit(solution)/shard_map/all_to_all | solution.py:69
  10.2 0.0 copy-start.2
  10.2 1.5 %multiply_reduce_fusion = f32[1024]{0:T(1024)S(1)} fusion(bf16[1024,512]{1,0:T(8,128)(2,1)} %src_ref.1), kind=kLoop, calls=%fused_computation | loop fusion | flops 1571840 | bytes 1052672 | tf_op jit(solution)/shard_map/reduce_sum | solution.py:64
  11.7 0.0 copy-done.1
  11.8 10.4 %all-to-all-done = bf16[32,8,640]{2,1,0:T(8,128)(2,1)S(1)} async-done(((bf16[32,8,640]{2,1,0:T(8,128)(2,1)}), bf16[32,8,640]{2,1,0:T(8,128)(2,1)S(1)}, u32[]{:S(2)}, u32[]{:S(2)}) %all-to-all-start) | async-done | bytes 327712 | tf_op jit(solution)/shard_map/all_to_all | solution.py:69
  22.2 0.0 copy-done
  22.2 1.6 %shard_map.68 = (f32[32,16]{1,0:T(8,128)S(1)}, f32[1,1024]{1,0:T(1,128)}) custom-call(bf16[1024,512]{1,0:T(8,128)(2,1)S(1)} %copy-done, bf16[256,640]{1,0:T(8,128)(2,1)S(1)} %bitcast.8, f32[2,1024]{1,0:T(2,128)S(1)} %pad_maximum_fusion.terms_ref), custom_call_target="tpu_custom_call" | custom-call | tf_op jit(solution)/shard_map/pallas_call | solution.py:75
  23.8 9.4 %all_to_all.17 = f32[32,1,16]{2,1,0:T(1,128)S(1)} all-to-all(f32[32,1,16]{2,1,0:T(1,128)S(1)} %bitcast.9), channel_id=1, replica_groups=mesh['group'=8,'blk'=4] {'group','blk'}, dimensions={0} | all-to-all | bytes 4096 | tf_op jit(solution)/shard_map/all_to_all | solution.py:87
  33.2 0.1 fusion
  33.3 0.0 copy-done.2
  33.3 0.5 %subtract_multiply_fusion = f32[8]{0:T(128)} fusion(f32[8]{0:T(128)S(1)} %copy-done.2, f32[8]{0:T(128)S(1)} %slice_reduce_fusion, f32[8]{0:T(128)S(1)} %fusion), kind=kLoop, calls=%fused_computation.8 | loop fusion | flops 24 | bytes 128 | tf_op jit(solution)/shard_map/mul | solution.py:92
  (4 shorter events, 0.0 us)
Async XLA Ops:
  0.6 11.1 %copy-start.1 = (f32[1024]{0:T(1024)S(1)}, f32[1024]{0:T(1024)}, u32[]{:S(2)}) copy-start(f32[1024]{0:T(1024)} %param.8) | copy-start | bytes 12292
  0.7 21.6 %copy-start = (bf16[1024,512]{1,0:T(8,128)(2,1)S(1)}, bf16[1024,512]{1,0:T(8,128)(2,1)}, u32[]{:S(2)}) copy-start(bf16[1024,512]{1,0:T(8,128)(2,1)} %src_ref.1) | copy-start | bytes 3145732
  2.9 19.3 %all-to-all-start = ((bf16[32,8,640]{2,1,0:T(8,128)(2,1)}), bf16[32,8,640]{2,1,0:T(8,128)(2,1)S(1)}, u32[]{:S(2)}, u32[]{:S(2)}) async-start(bf16[32,8,640]{2,1,0:T(8,128)(2,1)} %broadcast_select_fusion), calls=%async_computation | async-start | bytes 655360 | tf_op jit(solution)/shard_map/all_to_all | solution.py:69
  10.2 23.1 %copy-start.2 = (f32[8]{0:T(128)S(1)}, f32[8]{0:T(128)}, u32[]{:S(2)}) copy-start(f32[8]{0:T(128)} %param.9) | copy-start | bytes 100

commit v14 on v12

--- a/solution.py
+++ b/solution.py
@@ -16,7 +16,7 @@
     return lax.ppermute(x, AXES, route)
 
 
-def tail(features, factor, width, src_ref, rows_ref, terms_ref, col_ref, pot_ref):
+def tail(features, factor, width, src_ref, rows_ref, terms_ref, col_ref, dual_ref):
     block = rows_ref[...]
     rows = block[:, :features]
     pots = block[:, features:features + 1].astype(jnp.float32)
@@ -29,7 +29,7 @@
     row_max = jnp.max(logits, 0, keepdims=True)
     row_lse = row_max + jnp.log(jnp.sum(jnp.exp(logits - row_max), 0, keepdims=True))
     dual = terms_ref[1:2, :] - row_lse
-    pot_ref[...] = epsilon * dual + terms_ref[0:1, :]
+    dual_ref[...] = dual
     column = logits - pots / epsilon + dual
     col_max = jnp.max(column, 1, keepdims=True)
     col_sum = jnp.sum(jnp.exp(column - col_max), 1, keepdims=True)
@@ -74,7 +74,7 @@
 
     width = targets.shape[0]
     vmem = pl.BlockSpec(memory_space=pltpu.VMEM)
-    columns, source_potential = pl.pallas_call(
+    columns, source_dual = pl.pallas_call(
         functools.partial(tail, features, factor, width),
         out_shape=(
             jax.ShapeDtypeStruct((count, 2 * width), jnp.float32),
@@ -84,7 +84,7 @@
         out_specs=(vmem, vmem),
         compiler_params=pltpu.CompilerParams(vmem_limit_bytes=24 * 1024 * 1024),
     )(sources, everything, source_terms)
-    source_potential = source_potential.reshape(-1)
+    source_potential = epsilon * source_dual.reshape(-1) + source_terms[0]
 
     part = lax.all_to_all(columns, AXES, 0, 0, tiled=True)
     owned_max = jnp.max(part[:, :width], 0)

time: 33.4 us -> 33.9 us (1.015)
  blocking collectives: 9.37 us -> 0 us
  waiting for transfers between devices: 10.4 us -> 17 us
  starting transfers between devices: 7.3 us -> 9.86 us
  other arithmetic: 3.02 us -> 3.62 us
    all_to_all x1 -> x0, blocking collectives: 9.37 us -> none  [per_device(): part = lax.all_to_all(columns, AXES, 0, 0, tiled=True)]
    all_to_all x0 -> x1, waiting for transfers between devices: none -> 6.54 us  [per_device(): part = lax.all_to_all(columns, AXES, 0, 0, tiled=True)]
    all_to_all x0 -> x1, starting transfers between devices: none -> 2.57 us  [per_device(): part = lax.all_to_all(columns, AXES, 0, 0, tiled=True)]
    add x0 -> x1, other arithmetic: none -> 0.6 us  [per_device(): source_potential = epsilon * source_dual.reshape(-1) + source_terms[0]]
  transfers between devices with their start and end apart: 1 -> 2, of which waited for: 1 -> 2; matrix products, arithmetic and copies ran while one was open for 5% -> 6% of each run, Pallas kernels for 0% -> 0%
where the time goes in v14:
time: 33.9 us; the launch traced here: 33.6 us
  waiting for transfers between devices  17 us (50%)
  starting transfers between devices  9.86 us (29%)
  other arithmetic  3.62 us (11%)
  Pallas kernels  1.69 us (5%)
  local copies, waits for them, and re-layouts  0.75 us (2%)
  between operations  0.71 us (2%)
    all_to_all x1, waiting for transfers between devices, per_device(): lax.all_to_all(jnp.broadcast_to(held[None], (count,) + held.shape), AXES,...  10.4 us
    all_to_all x1, starting transfers between devices, per_device(): lax.all_to_all(jnp.broadcast_to(held[None], (count,) + held.shape), AXES,...  7.3 us
    all_to_all x1, waiting for transfers between devices, per_device(): part = lax.all_to_all(columns, AXES, 0, 0, tiled=True)  6.54 us
    all_to_all x1, starting transfers between devices, per_device(): part = lax.all_to_all(columns, AXES, 0, 0, tiled=True)  2.57 us
    pallas_call x1, Pallas kernels, per_device(): pl.pallas_call(functools.partial(tail, features, factor, width), out_shap...  1.69 us
    reduce_sum x1, other arithmetic, per_device(): jnp.sum(jnp.square(sources.astype(jnp.float32)), 1) / features  1.5 us
    select_n x1, other arithmetic, per_device(): jnp.where(lane < features, jnp.pad(targets, ((0, 0), (0, 128))), target_p...  0.86 us
    broadcast_in_dim x1, local copies, waits for them, and re-layouts, per_device(): jnp.broadcast_to(held[None], (count,) + held.shape)  0.74 us
  transfers between devices with their start and end apart: 2, of which 2 were waited for; matrix products, arithmetic and copies ran while one was open for 6% of the time, Pallas kernels for 0%

profile of v14, /device:TPU:0, one launch (start us, length us, event | category | flops | bytes accessed | tf_op | source)
XLA Modules:
  0.0 33.6 jit_solution(11086148306380514473)
XLA Ops:
  0.6 0.0 copy-start.1
  0.7 0.0 copy-start
  0.7 0.9 %pad_select_fusion = bf16[8,640]{1,0:T(8,128)(2,1)S(1)} fusion(bf16[8,512]{1,0:T(8,128)(2,1)} %param.6, pred[640]{0:T(1024)(128)(4,1)S(1)} %iota_compare_fusion, bf16[8]{0:T(256)(128)(2,1)} %param.7), kind=kLoop, calls=%fused_computation.4 | loop fusion | flops 5120 | bytes 19088 | tf_op jit(solution)/shard_map/jit(_where)/select_n | solution.py:57
  1.5 0.7 %broadcast_in_dim.11 = bf16[32,8,640]{2,1,0:T(8,128)(2,1)} broadcast(bf16[8,640]{1,0:T(8,128)(2,1)S(1)} %pad_select_fusion), dimensions={1,2} | broadcast | bytes 337920 | tf_op jit(solution)/shard_map/broadcast_in_dim | solution.py:72
  2.3 7.3 %all-to-all-start = ((bf16[32,8,640]{2,1,0:T(8,128)(2,1)}), bf16[32,8,640]{2,1,0:T(8,128)(2,1)S(1)}, u32[]{:S(2)}, u32[]{:S(2)}) async-start(bf16[32,8,640]{2,1,0:T(8,128)(2,1)} %broadcast_in_dim.11), calls=%async_computation | async-start | bytes 655360 | tf_op jit(solution)/shard_map/all_to_all | solution.py:71
  9.6 0.0 copy-start.2
  9.6 1.5 %multiply_reduce_fusion = f32[1024]{0:T(1024)S(1)} fusion(bf16[1024,512]{1,0:T(8,128)(2,1)} %src_ref.1), kind=kLoop, calls=%fused_computation | loop fusion | flops 1571840 | bytes 1052672 | tf_op jit(solution)/shard_map/reduce_sum | solution.py:66
  11.1 0.0 copy-done.1
  11.1 10.4 %all-to-all-done = bf16[32,8,640]{2,1,0:T(8,128)(2,1)S(1)} async-done(((bf16[32,8,640]{2,1,0:T(8,128)(2,1)}), bf16[32,8,640]{2,1,0:T(8,128)(2,1)S(1)}, u32[]{:S(2)}, u32[]{:S(2)}) %all-to-all-start) | async-done | bytes 327712 | tf_op jit(solution)/shard_map/all_to_all | solution.py:71
  21.6 0.0 copy-done
  21.6 1.7 %shard_map.68 = (f32[32,16]{1,0:T(8,128)}, f32[1,1024]{1,0:T(1,128)S(1)}) custom-call(bf16[1024,512]{1,0:T(8,128)(2,1)S(1)} %copy-done, bf16[256,640]{1,0:T(8,128)(2,1)S(1)} %bitcast.8, f32[2,1024]{1,0:T(2,128)S(1)} %pad_maximum_fusion.terms_ref), custom_call_target="tpu_custom_call" | custom-call | tf_op jit(solution)/shard_map/pallas_call | solution.py:77
  23.3 2.6 %all-to-all-start.1 = ((f32[32,1,16]{2,1,0:T(1,128)}), f32[32,1,16]{2,1,0:T(1,128)S(1)}, u32[]{:S(2)}, u32[]{:S(2)}) async-start(f32[32,1,16]{2,1,0:T(1,128)} %bitcast.5), calls=%async_computation.1 | async-start | bytes 32768 | tf_op jit(solution)/shard_map/all_to_all | solution.py:89
  25.8 0.6 %slice_add_fusion = f32[1,1024]{1,0:T(1,128)} fusion(f32[2,1024]{1,0:T(2,128)S(1)} %pad_maximum_fusion.terms_ref, f32[1,1024]{1,0:T(1,128)S(1)} %get-tuple-element.4), kind=kLoop, calls=%fused_computation.6 | loop fusion | flops 2048 | bytes 12288 | tf_op jit(solution)/shard_map/add | solution.py:87
  26.4 6.5 %all-to-all-done.1 = f32[32,1,16]{2,1,0:T(1,128)S(1)} async-done(((f32[32,1,16]{2,1,0:T(1,128)}), f32[32,1,16]{2,1,0:T(1,128)S(1)}, u32[]{:S(2)}, u32[]{:S(2)}) %all-to-all-start.1) | async-done | bytes 2080 | tf_op jit(solution)/shard_map/all_to_all | solution.py:89
  33.0 0.1 fusion
  33.1 0.0 copy-done.2
  33.1 0.5 %subtract_multiply_fusion = f32[8]{0:T(128)} fusion(f32[8]{0:T(128)S(1)} %copy-done.2, f32[8]{0:T(128)S(1)} %slice_reduce_fusion, f32[8]{0:T(128)S(1)} %fusion), kind=kLoop, calls=%fused_computation.9 | loop fusion | flops 24 | bytes 128 | tf_op jit(solution)/shard_map/mul | solution.py:94
  (4 shorter events, 0.0 us)
Async XLA Ops:
  0.6 10.5 %copy-start.1 = (f32[1024]{0:T(1024)S(1)}, f32[1024]{0:T(1024)}, u32[]{:S(2)}) copy-start(f32[1024]{0:T(1024)} %param.8) | copy-start | bytes 12292
  0.7 20.9 %copy-start = (bf16[1024,512]{1,0:T(8,128)(2,1)S(1)}, bf16[1024,512]{1,0:T(8,128)(2,1)}, u32[]{:S(2)}) copy-start(bf16[1024,512]{1,0:T(8,128)(2,1)} %src_ref.1) | copy-start | bytes 3145732
  2.3 19.3 %all-to-all-start = ((bf16[32,8,640]{2,1,0:T(8,128)(2,1)}), bf16[32,8,640]{2,1,0:T(8,128)(2,1)S(1)}, u32[]{:S(2)}, u32[]{:S(2)}) async-start(bf16[32,8,640]{2,1,0:T(8,128)(2,1)} %broadcast_in_dim.11), calls=%async_computation | async-start | bytes 655360 | tf_op jit(solution)/shard_map/all_to_all | solution.py:71
  9.6 23.5 %copy-start.2 = (f32[8]{0:T(128)S(1)}, f32[8]{0:T(128)}, u32[]{:S(2)}) copy-start(f32[8]{0:T(128)} %param.9) | copy-start | bytes 100
  23.3 9.7 %all-to-all-start.1 = ((f32[32,1,16]{2,1,0:T(1,128)}), f32[32,1,16]{2,1,0:T(1,128)S(1)}, u32[]{:S(2)}, u32[]{:S(2)}) async-start(f32[32,1,16]{2,1,0:T(1,128)} %bitcast.5), calls=%async_computation.1 | async-start | bytes 32768 | tf_op jit(solution)/shard_map/all_to_all | solution.py:89

commit v15 on v12

--- a/solution.py
+++ b/solution.py
@@ -9,11 +9,6 @@
 
 epsilon = 0.05
 AXES = ("group", "blk")
-
-
-def exchange(x, bit, count):
-    route = [(i, i ^ (1 << bit)) for i in range(count)]
-    return lax.ppermute(x, AXES, route)
 
 
 def tail(features, factor, width, src_ref, rows_ref, terms_ref, col_ref, pot_ref):
@@ -45,10 +40,6 @@
 
 def per_device(sources, targets, target_potential, log_source_mass, log_target_mass):
     count = lax.axis_size("group") * lax.axis_size("blk")
-    levels = count.bit_length() - 1
-    if (1 << levels) != count:
-        raise ValueError("count not pow2")
-    order = list(reversed(range(levels)))
     features = sources.shape[1]
     factor = 2.0 / (features * epsilon)
 

time: 33.4 us -> 33.4 us (level)
  no operation moved by 1% of the time
where the time goes in v15:
time: 33.4 us; the launch traced here: 33.1 us
  waiting for transfers between devices  10.4 us (31%)
  blocking collectives  9.37 us (28%)
  starting transfers between devices  7.3 us (22%)
  other arithmetic  3.02 us (9%)
  Pallas kernels  1.58 us (5%)
  local copies, waits for them, and re-layouts  0.75 us (2%)
  between operations  0.7 us (2%)
    all_to_all x1, waiting for transfers between devices, per_device(): lax.all_to_all(jnp.broadcast_to(held[None], (count,) + held.shape), AXES,...  10.4 us
    all_to_all x1, blocking collectives, per_device(): part = lax.all_to_all(columns, AXES, 0, 0, tiled=True)  9.37 us
    all_to_all x1, starting transfers between devices, per_device(): lax.all_to_all(jnp.broadcast_to(held[None], (count,) + held.shape), AXES,...  7.3 us
    pallas_call x1, Pallas kernels, per_device(): pl.pallas_call(functools.partial(tail, features, factor, width), out_shap...  1.58 us
    reduce_sum x1, other arithmetic, per_device(): jnp.sum(jnp.square(sources.astype(jnp.float32)), 1) / features  1.5 us
    select_n x1, other arithmetic, per_device(): jnp.where(lane < features, jnp.pad(targets, ((0, 0), (0, 128))), target_p...  0.86 us
    broadcast_in_dim x1, local copies, waits for them, and re-layouts, per_device(): jnp.broadcast_to(held[None], (count,) + held.shape)  0.74 us
  transfers between devices with their start and end apart: 1, of which 1 were waited for; matrix products, arithmetic and copies ran while one was open for 5% of the time, Pallas kernels for 0%

profile of v15, /device:TPU:0, one launch (start us, length us, event | category | flops | bytes accessed | tf_op | source)
XLA Modules:
  0.0 33.1 jit_solution(12109719929745963740)
XLA Ops:
  0.6 0.0 copy-start.1
  0.7 0.0 copy-start
  0.7 0.9 %pad_select_fusion = bf16[8,640]{1,0:T(8,128)(2,1)S(1)} fusion(bf16[8,512]{1,0:T(8,128)(2,1)} %param.6, pred[640]{0:T(1024)(128)(4,1)S(1)} %iota_compare_fusion, bf16[8]{0:T(256)(128)(2,1)} %param.7), kind=kLoop, calls=%fused_computation.4 | loop fusion | flops 5120 | bytes 19088 | tf_op jit(solution)/shard_map/jit(_where)/select_n | solution.py:48
  1.5 0.7 %broadcast_in_dim.11 = bf16[32,8,640]{2,1,0:T(8,128)(2,1)} broadcast(bf16[8,640]{1,0:T(8,128)(2,1)S(1)} %pad_select_fusion), dimensions={1,2} | broadcast | bytes 337920 | tf_op jit(solution)/shard_map/broadcast_in_dim | solution.py:63
  2.3 7.3 %all-to-all-start = ((bf16[32,8,640]{2,1,0:T(8,128)(2,1)}), bf16[32,8,640]{2,1,0:T(8,128)(2,1)S(1)}, u32[]{:S(2)}, u32[]{:S(2)}) async-start(bf16[32,8,640]{2,1,0:T(8,128)(2,1)} %broadcast_in_dim.11), calls=%async_computation | async-start | bytes 655360 | tf_op jit(solution)/shard_map/all_to_all | solution.py:62
  9.6 0.0 copy-start.2
  9.6 1.5 %multiply_reduce_fusion = f32[1024]{0:T(1024)S(1)} fusion(bf16[1024,512]{1,0:T(8,128)(2,1)} %src_ref.1), kind=kLoop, calls=%fused_computation | loop fusion | flops 1571840 | bytes 1052672 | tf_op jit(solution)/shard_map/reduce_sum | solution.py:57
  11.1 0.0 copy-done.1
  11.1 10.4 %all-to-all-done = bf16[32,8,640]{2,1,0:T(8,128)(2,1)S(1)} async-done(((bf16[32,8,640]{2,1,0:T(8,128)(2,1)}), bf16[32,8,640]{2,1,0:T(8,128)(2,1)S(1)}, u32[]{:S(2)}, u32[]{:S(2)}) %all-to-all-start) | async-done | bytes 327712 | tf_op jit(solution)/shard_map/all_to_all | solution.py:62
  21.6 0.0 copy-done
  21.6 1.6 %shard_map.68 = (f32[32,16]{1,0:T(8,128)S(1)}, f32[1,1024]{1,0:T(1,128)}) custom-call(bf16[1024,512]{1,0:T(8,128)(2,1)S(1)} %copy-done, bf16[256,640]{1,0:T(8,128)(2,1)S(1)} %bitcast.8, f32[2,1024]{1,0:T(2,128)S(1)} %pad_maximum_fusion.terms_ref), custom_call_target="tpu_custom_call" | custom-call | tf_op jit(solution)/shard_map/pallas_call | solution.py:68
  23.1 9.4 %all_to_all.17 = f32[32,1,16]{2,1,0:T(1,128)S(1)} all-to-all(f32[32,1,16]{2,1,0:T(1,128)S(1)} %bitcast.9), channel_id=1, replica_groups=mesh['group'=8,'blk'=4] {'group','blk'}, dimensions={0} | all-to-all | bytes 4096 | tf_op jit(solution)/shard_map/all_to_all | solution.py:80
  32.5 0.1 fusion
  32.6 0.0 copy-done.2
  32.6 0.5 %subtract_multiply_fusion = f32[8]{0:T(128)} fusion(f32[8]{0:T(128)S(1)} %copy-done.2, f32[8]{0:T(128)S(1)} %slice_reduce_fusion, f32[8]{0:T(128)S(1)} %fusion), kind=kLoop, calls=%fused_computation.8 | loop fusion | flops 24 | bytes 128 | tf_op jit(solution)/shard_map/mul | solution.py:85
  (4 shorter events, 0.0 us)
Async XLA Ops:
  0.6 10.5 %copy-start.1 = (f32[1024]{0:T(1024)S(1)}, f32[1024]{0:T(1024)}, u32[]{:S(2)}) copy-start(f32[1024]{0:T(1024)} %param.8) | copy-start | bytes 12292
  0.7 20.9 %copy-start = (bf16[1024,512]{1,0:T(8,128)(2,1)S(1)}, bf16[1024,512]{1,0:T(8,128)(2,1)}, u32[]{:S(2)}) copy-start(bf16[1024,512]{1,0:T(8,128)(2,1)} %src_ref.1) | copy-start | bytes 3145732
  2.3 19.3 %all-to-all-start = ((bf16[32,8,640]{2,1,0:T(8,128)(2,1)}), bf16[32,8,640]{2,1,0:T(8,128)(2,1)S(1)}, u32[]{:S(2)}, u32[]{:S(2)}) async-start(bf16[32,8,640]{2,1,0:T(8,128)(2,1)} %broadcast_in_dim.11), calls=%async_computation | async-start | bytes 655360 | tf_op jit(solution)/shard_map/all_to_all | solution.py:62
  9.6 23.1 %copy-start.2 = (f32[8]{0:T(128)S(1)}, f32[8]{0:T(128)}, u32[]{:S(2)}) copy-start(f32[8]{0:T(128)} %param.9) | copy-start | bytes 100

commit v16 on v15

--- a/solution.py
+++ b/solution.py
@@ -11,10 +11,9 @@
 AXES = ("group", "blk")
 
 
-def tail(features, factor, width, src_ref, rows_ref, terms_ref, col_ref, pot_ref):
-    block = rows_ref[...]
-    rows = block[:, :features]
-    pots = block[:, features:features + 1].astype(jnp.float32)
+def tail(features, factor, width, src_ref, rows_ref, pots_ref, terms_ref, col_ref, pot_ref):
+    block = rows = rows_ref[...]
+    pots = pots_ref[:, 0:1].astype(jnp.float32)
     offset = pots / epsilon - jnp.sum(jnp.square(rows.astype(jnp.float32)), 1, keepdims=True) / (
         features * epsilon
     )
@@ -43,14 +42,6 @@
     features = sources.shape[1]
     factor = 2.0 / (features * epsilon)
 
-    lane = lax.broadcasted_iota(jnp.int32, (targets.shape[0], features + 128), 1)
-    held = lax.optimization_barrier(
-        jnp.where(
-            lane < features,
-            jnp.pad(targets, ((0, 0), (0, 128))),
-            target_potential[:, None],
-        )
-    )
     source_terms = lax.optimization_barrier(
         jnp.stack(
             [
@@ -59,9 +50,13 @@
             ]
         )
     )
+    rows = targets.shape[0]
     everything = lax.all_to_all(
-        jnp.broadcast_to(held[None], (count,) + held.shape), AXES, 0, 0, tiled=True
-    ).reshape(count * held.shape[0], held.shape[1])
+        jnp.broadcast_to(targets[None], (count,) + targets.shape), AXES, 0, 0, tiled=True
+    ).reshape(count * rows, features)
+    pots = lax.all_to_all(
+        jnp.broadcast_to(target_potential[None, :, None], (count, rows, 128)), AXES, 0, 0, tiled=True
+    ).reshape(count * rows, 128)
 
     width = targets.shape[0]
     vmem = pl.BlockSpec(memory_space=pltpu.VMEM)
@@ -71,10 +66,10 @@
             jax.ShapeDtypeStruct((count, 2 * width), jnp.float32),
             jax.ShapeDtypeStruct((1, sources.shape[0]), jnp.float32),
         ),
-        in_specs=[vmem] * 3,
+        in_specs=[vmem] * 4,
         out_specs=(vmem, vmem),
         compiler_params=pltpu.CompilerParams(vmem_limit_bytes=24 * 1024 * 1024),
-    )(sources, everything, source_terms)
+    )(sources, everything, pots, source_terms)
     source_potential = source_potential.reshape(-1)
 
     part = lax.all_to_all(columns, AXES, 0, 0, tiled=True)

time: 33.4 us -> 42.4 us (1.27)
  blocking collectives: 9.37 us -> 23.8 us
  starting transfers between devices: 7.3 us -> 2.58 us
  local copies, waits for them, and re-layouts: 0.75 us -> 2.25 us
  waiting for transfers between devices: 10.4 us -> 9.04 us
  other arithmetic: 3.02 us -> 2.15 us
    all_to_all x0 -> x1, blocking collectives: none -> 14.5 us  [per_device(): lax.all_to_all(jnp.broadcast_to(target_potential[None, :, None], (count,...]
    all_to_all x1, starting transfers between devices: 7.3 us -> 2.58 us  [per_device(): lax.all_to_all(jnp.broadcast_to(targets[None], (count,) + targets.shape),...]
    broadcast_in_dim x1 -> x2, local copies, waits for them, and re-layouts: 0.74 us -> 2.23 us  [the longest x1 1.41 us: per_device(): jnp.broadcast_to(targets[None], (count,) + targets.shape)]
    all_to_all x1, waiting for transfers between devices: 10.4 us -> 9.04 us  [per_device(): lax.all_to_all(jnp.broadcast_to(targets[None], (count,) + targets.shape),...]
    select_n x1 -> x0, other arithmetic: 0.86 us -> none  [per_device(): jnp.where(lane < features, jnp.pad(targets, ((0, 0), (0, 128))), target_p...]
  transfers between devices with their start and end apart: 1 -> 1, of which waited for: 1 -> 1; matrix products, arithmetic and copies ran while one was open for 5% -> 4% of each run, Pallas kernels for 0% -> 0%
where the time goes in v16:
time: 42.4 us; the launch traced here: 42 us
  blocking collectives  23.8 us (56%)
  waiting for transfers between devices  9.04 us (21%)
  starting transfers between devices  2.58 us (6%)
  local copies, waits for them, and re-layouts  2.25 us (5%)
  other arithmetic  2.15 us (5%)
  Pallas kernels  1.58 us (4%)
  between operations  0.7 us (2%)
    all_to_all x1, blocking collectives, per_device(): lax.all_to_all(jnp.broadcast_to(target_potential[None, :, None], (count,...  14.5 us
    all_to_all x1, blocking collectives, per_device(): part = lax.all_to_all(columns, AXES, 0, 0, tiled=True)  9.25 us
    all_to_all x1, waiting for transfers between devices, per_device(): lax.all_to_all(jnp.broadcast_to(targets[None], (count,) + targets.shape),...  9.04 us
    all_to_all x1, starting transfers between devices, per_device(): lax.all_to_all(jnp.broadcast_to(targets[None], (count,) + targets.shape),...  2.58 us
    pallas_call x1, Pallas kernels, per_device(): pl.pallas_call(functools.partial(tail, features, factor, width), out_shap...  1.58 us
    reduce_sum x1, other arithmetic, per_device(): jnp.sum(jnp.square(sources.astype(jnp.float32)), 1) / features  1.5 us
    broadcast_in_dim x1, local copies, waits for them, and re-layouts, per_device(): jnp.broadcast_to(targets[None], (count,) + targets.shape)  1.41 us
  transfers between devices with their start and end apart: 1, of which 1 were waited for; matrix products, arithmetic and copies ran while one was open for 4% of the time, Pallas kernels for 0%

profile of v16, /device:TPU:0, one launch (start us, length us, event | category | flops | bytes accessed | tf_op | source)
XLA Modules:
  0.0 42.0 jit_solution(1159114819232531266)
XLA Ops:
  0.6 0.0 copy-start
  0.6 0.0 copy-start.1
  0.7 0.8 %broadcast_in_dim.5 = bf16[32,8,128]{2,1,0:T(8,128)(2,1)S(1)} broadcast(bf16[8]{0:T(256)(128)(2,1)} %param.7), dimensions={1} | broadcast | bytes 65552 | tf_op jit(solution)/shard_map/broadcast_in_dim | solution.py:58
  1.5 14.5 %all_to_all.22 = bf16[32,8,128]{2,1,0:T(8,128)(2,1)S(1)} all-to-all(bf16[32,8,128]{2,1,0:T(8,128)(2,1)S(1)} %broadcast_in_dim.5), channel_id=1, replica_groups=mesh['group'=8,'blk'=4] {'group','blk'}, dimensions={0} | all-to-all | bytes 131072 | tf_op jit(solution)/shard_map/all_to_all | solution.py:57
  16.0 1.4 %broadcast_in_dim.4 = bf16[32,8,512]{2,1,0:T(8,128)(2,1)} broadcast(bf16[8,512]{1,0:T(8,128)(2,1)} %param.6), dimensions={1,2} | broadcast | bytes 270336 | tf_op jit(solution)/shard_map/broadcast_in_dim | solution.py:55
  17.4 2.6 %all-to-all-start = ((bf16[32,8,512]{2,1,0:T(8,128)(2,1)}), bf16[32,8,512]{2,1,0:T(8,128)(2,1)S(1)}, u32[]{:S(2)}, u32[]{:S(2)}) async-start(bf16[32,8,512]{2,1,0:T(8,128)(2,1)} %broadcast_in_dim.4), calls=%async_computation | async-start | bytes 524288 | tf_op jit(solution)/shard_map/all_to_all | solution.py:54
  20.0 0.0 copy-start.2
  20.0 1.5 %multiply_reduce_fusion = f32[1024]{0:T(1024)S(1)} fusion(bf16[1024,512]{1,0:T(8,128)(2,1)} %src_ref.1), kind=kLoop, calls=%fused_computation | loop fusion | flops 1571840 | bytes 1052672 | tf_op jit(solution)/shard_map/reduce_sum | solution.py:48
  21.5 0.0 copy-done.1
  21.5 9.0 %all-to-all-done = bf16[32,8,512]{2,1,0:T(8,128)(2,1)S(1)} async-done(((bf16[32,8,512]{2,1,0:T(8,128)(2,1)}), bf16[32,8,512]{2,1,0:T(8,128)(2,1)S(1)}, u32[]{:S(2)}, u32[]{:S(2)}) %all-to-all-start) | async-done | bytes 262176 | tf_op jit(solution)/shard_map/all_to_all | solution.py:54
  30.6 0.0 copy-done
  30.6 1.6 %shard_map.68 = (f32[32,16]{1,0:T(8,128)S(1)}, f32[1,1024]{1,0:T(1,128)}) custom-call(bf16[1024,512]{1,0:T(8,128)(2,1)S(1)} %copy-done, bf16[256,512]{1,0:T(8,128)(2,1)S(1)} %bitcast.9, bf16[256,128]{1,0:T(8,128)(2,1)S(1)} %bitcast.10, f32[2,1024]{1,0:T(2,128)S(1)} %pad_maximum_fusion.terms_ref), custom_call_target="tpu_custom_call" | custom-call | tf_op jit(solution)/shard_map/pallas_call | solution.py:63
  32.2 9.3 %all_to_all.23 = f32[32,1,16]{2,1,0:T(1,128)S(1)} all-to-all(f32[32,1,16]{2,1,0:T(1,128)S(1)} %bitcast.11), channel_id=1, replica_groups=mesh['group'=8,'blk'=4] {'group','blk'}, dimensions={0} | all-to-all | bytes 4096 | tf_op jit(solution)/shard_map/all_to_all | solution.py:75
  41.4 0.1 fusion
  41.5 0.0 copy-done.2
  41.5 0.5 %subtract_multiply_fusion = f32[8]{0:T(128)} fusion(f32[8]{0:T(128)S(1)} %copy-done.2, f32[8]{0:T(128)S(1)} %slice_reduce_fusion, f32[8]{0:T(128)S(1)} %fusion), kind=kLoop, calls=%fused_computation.6 | loop fusion | flops 24 | bytes 128 | tf_op jit(solution)/shard_map/mul | solution.py:80
  (3 shorter events, 0.0 us)
Async XLA Ops:
  0.6 29.9 %copy-start = (bf16[1024,512]{1,0:T(8,128)(2,1)S(1)}, bf16[1024,512]{1,0:T(8,128)(2,1)}, u32[]{:S(2)}) copy-start(bf16[1024,512]{1,0:T(8,128)(2,1)} %src_ref.1) | copy-start | bytes 3145732
  0.6 20.9 %copy-start.1 = (f32[1024]{0:T(1024)S(1)}, f32[1024]{0:T(1024)}, u32[]{:S(2)}) copy-start(f32[1024]{0:T(1024)} %param.8) | copy-start | bytes 12292
  17.4 13.2 %all-to-all-start = ((bf16[32,8,512]{2,1,0:T(8,128)(2,1)}), bf16[32,8,512]{2,1,0:T(8,128)(2,1)S(1)}, u32[]{:S(2)}, u32[]{:S(2)}) async-start(bf16[32,8,512]{2,1,0:T(8,128)(2,1)} %broadcast_in_dim.4), calls=%async_computation | async-start | bytes 524288 | tf_op jit(solution)/shard_map/all_to_all | solution.py:54
  20.0 21.5 %copy-start.2 = (f32[8]{0:T(128)S(1)}, f32[8]{0:T(128)}, u32[]{:S(2)}) copy-start(f32[8]{0:T(128)} %param.9) | copy-start | bytes 100

commit v17 on v16

--- a/solution.py
+++ b/solution.py
@@ -13,7 +13,7 @@
 
 def tail(features, factor, width, src_ref, rows_ref, pots_ref, terms_ref, col_ref, pot_ref):
     block = rows = rows_ref[...]
-    pots = pots_ref[:, 0:1].astype(jnp.float32)
+    pots = pots_ref[...].astype(jnp.float32)
     offset = pots / epsilon - jnp.sum(jnp.square(rows.astype(jnp.float32)), 1, keepdims=True) / (
         features * epsilon
     )
@@ -51,12 +51,16 @@
         )
     )
     rows = targets.shape[0]
+    flat = rows * features
+    spare = -(flat + rows) % 128
+    chunk = jnp.concatenate(
+        [targets.reshape(flat), target_potential, jnp.zeros((spare,), targets.dtype)]
+    )
     everything = lax.all_to_all(
-        jnp.broadcast_to(targets[None], (count,) + targets.shape), AXES, 0, 0, tiled=True
-    ).reshape(count * rows, features)
-    pots = lax.all_to_all(
-        jnp.broadcast_to(target_potential[None, :, None], (count, rows, 128)), AXES, 0, 0, tiled=True
-    ).reshape(count * rows, 128)
+        jnp.broadcast_to(chunk[None], (count, chunk.shape[0])), AXES, 0, 0, tiled=True
+    )
+    pots = everything[:, flat:flat + rows].reshape(count * rows, 1)
+    everything = everything[:, :flat].reshape(count * rows, features)
 
     width = targets.shape[0]
     vmem = pl.BlockSpec(memory_space=pltpu.VMEM)

time: 42.4 us -> 36.8 us (0.87)
  blocking collectives: 23.8 us -> 9.21 us
  starting transfers between devices: 2.58 us -> 7.3 us
  waiting for transfers between devices: 9.04 us -> 10.8 us
  local copies, waits for them, and re-layouts: 2.25 us -> 3.76 us
  other arithmetic: 2.15 us -> 3.15 us
    all_to_all x1 -> x0, blocking collectives: 14.5 us -> none  [per_device(): lax.all_to_all(jnp.broadcast_to(target_potential[None, :, None], (count,...]
    all_to_all x1, starting transfers between devices: 2.58 us -> 7.3 us  [per_device(): lax.all_to_all(jnp.broadcast_to(chunk[None], (count, chunk.shape[0])), AX...]
    broadcast_in_dim x0 -> x1, other arithmetic: none -> 2.23 us  [per_device(): jnp.broadcast_to(chunk[None], (count, chunk.shape[0]))]
    unnamed x6 -> x10, local copies, waits for them, and re-layouts: 0.02 us -> 1.98 us
    all_to_all x1, waiting for transfers between devices: 9.04 us -> 10.8 us  [per_device(): lax.all_to_all(jnp.broadcast_to(chunk[None], (count, chunk.shape[0])), AX...]
    broadcast_in_dim x2 -> x3, local copies, waits for them, and re-layouts: 2.23 us -> 0.8 us  [the longest x2 0.79 us: per_device(): jnp.broadcast_to(chunk[None], (count, chunk.shape[0]))]
    reduce_sum x1, other arithmetic: 1.5 us -> 0.27 us  [per_device(): jnp.sum(jnp.square(sources.astype(jnp.float32)), 1) / features]
    concatenate x0 -> x1, local copies, waits for them, and re-layouts: none -> 0.74 us  [per_device(): jnp.concatenate([targets.reshape(flat), target_potential, jnp.zeros((spar...]
  transfers between devices with their start and end apart: 1 -> 1, of which waited for: 1 -> 1; matrix products, arithmetic and copies ran while one was open for 4% -> 1% of each run, Pallas kernels for 0% -> 0%
where the time goes in v17:
time: 36.8 us; the launch traced here: 36.5 us
  waiting for transfers between devices  10.8 us (29%)
  blocking collectives  9.21 us (25%)
  starting transfers between devices  7.3 us (20%)
  local copies, waits for them, and re-layouts  3.76 us (10%)
  other arithmetic  3.15 us (9%)
  Pallas kernels  1.58 us (4%)
  between operations  0.76 us (2%)
    all_to_all x1, waiting for transfers between devices, per_device(): lax.all_to_all(jnp.broadcast_to(chunk[None], (count, chunk.shape[0])), AX...  10.8 us
    all_to_all x1, blocking collectives, per_device(): part = lax.all_to_all(columns, AXES, 0, 0, tiled=True)  9.21 us
    all_to_all x1, starting transfers between devices, per_device(): lax.all_to_all(jnp.broadcast_to(chunk[None], (count, chunk.shape[0])), AX...  7.3 us
    broadcast_in_dim x1, other arithmetic, per_device(): jnp.broadcast_to(chunk[None], (count, chunk.shape[0]))  2.23 us
    unnamed x10, local copies, waits for them, and re-layouts  1.98 us
    pallas_call x1, Pallas kernels, per_device(): pl.pallas_call(functools.partial(tail, features, factor, width), out_shap...  1.58 us
    broadcast_in_dim x2, local copies, waits for them, and re-layouts, per_device(): jnp.broadcast_to(chunk[None], (count, chunk.shape[0]))  0.79 us
    concatenate x1, local copies, waits for them, and re-layouts, per_device(): jnp.concatenate([targets.reshape(flat), target_potential, jnp.zeros((spar...  0.74 us
  transfers between devices with their start and end apart: 1, of which 1 were waited for; matrix products, arithmetic and copies ran while one was open for 1% of the time, Pallas kernels for 0%

profile of v17, /device:TPU:0, one launch (start us, length us, event | category | flops | bytes accessed | tf_op | source)
XLA Modules:
  0.0 36.5 jit_solution(4206882310174849057)
XLA Ops:
  0.6 0.7 %copy.13 = bf16[1,4,8,128]{3,1,2,0:T(4,128)(2,1)S(1)} copy(bf16[1,4,8,128]{3,2,1,0:T(8,128)(2,1)} %bitcast.19) | data formatting | bytes 16384
  1.3 0.7 %concatenate.3 = bf16[4224]{0:T(1024)(128)(2,1)S(1)} concatenate(bf16[4096]{0:T(1024)(128)(2,1)S(1)} %bitcast.17, bf16[8]{0:T(256)(128)(2,1)} %param.7, bf16[120]{0:T(256)(128)(2,1)S(1)} %broadcast_in_dim.4), dimensions={0} | concatenate | bytes 16896 | tf_op jit(solution)/shard_map/concatenate | solution.py:56
  2.1 0.3 broadcast_in_dim.5
  2.4 0.0 copy-start
  2.4 0.5 %broadcast.19 = bf16[]{:T(256)} broadcast(bf16[]{:T(256)} %constant.16), dimensions={} | broadcast | bytes 4 | tf_op jit(solution)/shard_map/broadcast_in_dim | solution.py:60
  2.9 2.2 %reduce = bf16[32,4224]{1,0:T(8,128)(2,1)S(1)} reduce(bf16[32,1,4224]{2,1,0:T(2,128)(2,1)S(1)} %broadcast_in_dim.5, bf16[]{:T(256)} %broadcast.19), dimensions={1}, to_apply=%broadcast_in_dim.5.reduce_sub_computation | reduce | bytes 540674 | tf_op jit(solution)/shard_map/broadcast_in_dim | solution.py:60
  5.1 0.0 copy-start.1
  5.1 0.9 %reshape.39 = bf16[32,2,2112]{2,1,0:T(2,128)(2,1)} reshape(bf16[32,4224]{1,0:T(8,128)(2,1)S(1)} %reduce) | data formatting | bytes 540672
  6.1 7.3 %all-to-all-start = ((bf16[32,2,2112]{2,1,0:T(2,128)(2,1)}), bf16[32,2,2112]{2,1,0:T(2,128)(2,1)S(1)}, u32[]{:S(2)}, u32[]{:S(2)}) async-start(bf16[32,2,2112]{2,1,0:T(2,128)(2,1)} %reshape.39), calls=%async_computation | async-start | bytes 557056 | tf_op jit(solution)/shard_map/all_to_all | solution.py:59
  13.4 0.0 copy-done
  13.4 0.3 multiply_reduce_fusion
  13.7 0.0 copy-done.1
  13.7 10.8 %all-to-all-done = bf16[32,2,2112]{2,1,0:T(2,128)(2,1)S(1)} async-done(((bf16[32,2,2112]{2,1,0:T(2,128)(2,1)}), bf16[32,2,2112]{2,1,0:T(2,128)(2,1)S(1)}, u32[]{:S(2)}, u32[]{:S(2)}) %all-to-all-start) | async-done | bytes 270368 | tf_op jit(solution)/shard_map/all_to_all | solution.py:59
  24.5 0.3 reshape.40
  24.8 0.0 copy-start.2
  24.9 0.1 reshape.35.rows_ref
  25.0 0.1 reshape.38.pots_ref
  25.1 1.6 %shard_map.68 = (f32[32,16]{1,0:T(8,128)S(1)}, f32[1,1024]{1,0:T(1,128)}) custom-call(bf16[1024,512]{1,0:T(8,128)(2,1)S(1)} %copy-done, bf16[256,512]{1,0:T(8,128)(2,1)S(1)} %reshape.35.rows_ref, bf16[256,1]{1,0:T(8,128)(2,1)S(1)} %reshape.38.pots_ref, f32[2,1024]{1,0:T(2,128)S(1)} %pad_maximum_fusion.terms_ref), custom_call_target="tpu_custom_call" | custom-call | tf_op jit(solution)/shard_map/pallas_call | solution.py:67
  26.7 9.2 %all_to_all.21 = f32[32,1,16]{2,1,0:T(1,128)S(1)} all-to-all(f32[32,1,16]{2,1,0:T(1,128)S(1)} %bitcast.12), channel_id=1, replica_groups=mesh['group'=8,'blk'=4] {'group','blk'}, dimensions={0} | all-to-all | bytes 4096 | tf_op jit(solution)/shard_map/all_to_all | solution.py:79
  35.9 0.1 fusion
  36.0 0.0 copy-done.2
  36.0 0.5 %subtract_multiply_fusion = f32[8]{0:T(128)} fusion(f32[8]{0:T(128)S(1)} %copy-done.2, f32[8]{0:T(128)S(1)} %slice_reduce_fusion, f32[8]{0:T(128)S(1)} %fusion), kind=kLoop, calls=%fused_computation.7 | loop fusion | flops 24 | bytes 128 | tf_op jit(solution)/shard_map/mul | solution.py:84
  (7 shorter events, 0.1 us)
Async XLA Ops:
  2.4 11.0 %copy-start = (bf16[1024,512]{1,0:T(8,128)(2,1)S(1)}, bf16[1024,512]{1,0:T(8,128)(2,1)}, u32[]{:S(2)}) copy-start(bf16[1024,512]{1,0:T(8,128)(2,1)} %src_ref.1) | copy-start | bytes 3145732
  5.1 8.5 %copy-start.1 = (f32[1024]{0:T(1024)S(1)}, f32[1024]{0:T(1024)}, u32[]{:S(2)}) copy-start(f32[1024]{0:T(1024)} %param.8) | copy-start | bytes 12292
  6.1 18.4 %all-to-all-start = ((bf16[32,2,2112]{2,1,0:T(2,128)(2,1)}), bf16[32,2,2112]{2,1,0:T(2,128)(2,1)S(1)}, u32[]{:S(2)}, u32[]{:S(2)}) async-start(bf16[32,2,2112]{2,1,0:T(2,128)(2,1)} %reshape.39), calls=%async_computation | async-start | bytes 557056 | tf_op jit(solution)/shard_map/all_to_all | solution.py:59
  24.8 11.2 %copy-start.2 = (f32[8]{0:T(128)S(1)}, f32[8]{0:T(128)}, u32[]{:S(2)}) copy-start(f32[8]{0:T(128)} %param.9) | copy-start | bytes 100

commit v18 on v15

--- a/solution.py
+++ b/solution.py
@@ -28,15 +28,16 @@
     column = logits - pots / epsilon + dual
     col_max = jnp.max(column, 1, keepdims=True)
     col_sum = jnp.sum(jnp.exp(column - col_max), 1, keepdims=True)
-    diagonal = lax.broadcasted_iota(jnp.int32, (width, width), 0) == lax.broadcasted_iota(
-        jnp.int32, (width, width), 1
+    targets_all = block.shape[0]
+    r = lax.broadcasted_iota(jnp.int32, (targets_all, 2 * width), 0)
+    c = lax.broadcasted_iota(jnp.int32, (targets_all, 2 * width), 1)
+    spread = jnp.where(c == r % width, col_max, jnp.where(c == r % width + width, col_sum, 0.0))
+    owners = lax.broadcasted_iota(jnp.int32, (targets_all // width, targets_all), 0)
+    members = lax.broadcasted_iota(jnp.int32, (targets_all // width, targets_all), 1) // width
+    gather = (owners == members).astype(jnp.float32)
+    col_ref[...] = jnp.dot(
+        gather, spread, precision=lax.Precision.HIGHEST, preferred_element_type=jnp.float32
     )
-    for owner in range(block.shape[0] // width):
-        first = owner * width
-        for lanes, stat in ((0, col_max), (width, col_sum)):
-            piece = jnp.where(diagonal, stat[first:first + width], 0.0)
-            col_ref[owner:owner + 1, lanes:lanes + width] = jnp.sum(piece, 0, keepdims=True)
-
 
 def per_device(sources, targets, target_potential, log_source_mass, log_target_mass):
     count = lax.axis_size("group") * lax.axis_size("blk")

time: 33.4 us -> 33.2 us (level)
  no operation moved by 1% of the time
where the time goes in v18:
time: 33.2 us; the launch traced here: 32.9 us
  waiting for transfers between devices  10.4 us (31%)
  blocking collectives  9.37 us (28%)
  starting transfers between devices  7.3 us (22%)
  other arithmetic  3.02 us (9%)
  Pallas kernels  1.37 us (4%)
  local copies, waits for them, and re-layouts  0.75 us (2%)
  between operations  0.7 us (2%)
    all_to_all x1, waiting for transfers between devices, per_device(): lax.all_to_all(jnp.broadcast_to(held[None], (count,) + held.shape), AXES,...  10.4 us
    all_to_all x1, blocking collectives, per_device(): part = lax.all_to_all(columns, AXES, 0, 0, tiled=True)  9.37 us
    all_to_all x1, starting transfers between devices, per_device(): lax.all_to_all(jnp.broadcast_to(held[None], (count,) + held.shape), AXES,...  7.3 us
    reduce_sum x1, other arithmetic, per_device(): jnp.sum(jnp.square(sources.astype(jnp.float32)), 1) / features  1.5 us
    pallas_call x1, Pallas kernels, per_device(): pl.pallas_call(functools.partial(tail, features, factor, width), out_shap...  1.37 us
    select_n x1, other arithmetic, per_device(): jnp.where(lane < features, jnp.pad(targets, ((0, 0), (0, 128))), target_p...  0.86 us
    broadcast_in_dim x1, local copies, waits for them, and re-layouts, per_device(): jnp.broadcast_to(held[None], (count,) + held.shape)  0.74 us
  transfers between devices with their start and end apart: 1, of which 1 were waited for; matrix products, arithmetic and copies ran while one was open for 5% of the time, Pallas kernels for 0%

profile of v18, /device:TPU:0, one launch (start us, length us, event | category | flops | bytes accessed | tf_op | source)
XLA Modules:
  0.0 32.9 jit_solution(12965156419412152688)
XLA Ops:
  0.6 0.0 copy-start.1
  0.7 0.0 copy-start
  0.7 0.9 %pad_select_fusion = bf16[8,640]{1,0:T(8,128)(2,1)S(1)} fusion(bf16[8,512]{1,0:T(8,128)(2,1)} %param.6, pred[640]{0:T(1024)(128)(4,1)S(1)} %iota_compare_fusion, bf16[8]{0:T(256)(128)(2,1)} %param.7), kind=kLoop, calls=%fused_computation.4 | loop fusion | flops 5120 | bytes 19088 | tf_op jit(solution)/shard_map/jit(_where)/select_n | solution.py:49
  1.5 0.7 %broadcast_in_dim.11 = bf16[32,8,640]{2,1,0:T(8,128)(2,1)} broadcast(bf16[8,640]{1,0:T(8,128)(2,1)S(1)} %pad_select_fusion), dimensions={1,2} | broadcast | bytes 337920 | tf_op jit(solution)/shard_map/broadcast_in_dim | solution.py:64
  2.3 7.3 %all-to-all-start = ((bf16[32,8,640]{2,1,0:T(8,128)(2,1)}), bf16[32,8,640]{2,1,0:T(8,128)(2,1)S(1)}, u32[]{:S(2)}, u32[]{:S(2)}) async-start(bf16[32,8,640]{2,1,0:T(8,128)(2,1)} %broadcast_in_dim.11), calls=%async_computation | async-start | bytes 655360 | tf_op jit(solution)/shard_map/all_to_all | solution.py:63
  9.6 0.0 copy-start.2
  9.6 1.5 %multiply_reduce_fusion = f32[1024]{0:T(1024)S(1)} fusion(bf16[1024,512]{1,0:T(8,128)(2,1)} %src_ref.1), kind=kLoop, calls=%fused_computation | loop fusion | flops 1571840 | bytes 1052672 | tf_op jit(solution)/shard_map/reduce_sum | solution.py:58
  11.1 0.0 copy-done.1
  11.1 10.4 %all-to-all-done = bf16[32,8,640]{2,1,0:T(8,128)(2,1)S(1)} async-done(((bf16[32,8,640]{2,1,0:T(8,128)(2,1)}), bf16[32,8,640]{2,1,0:T(8,128)(2,1)S(1)}, u32[]{:S(2)}, u32[]{:S(2)}) %all-to-all-start) | async-done | bytes 327712 | tf_op jit(solution)/shard_map/all_to_all | solution.py:63
  21.6 0.0 copy-done
  21.6 1.4 %shard_map.68 = (f32[32,16]{1,0:T(8,128)S(1)}, f32[1,1024]{1,0:T(1,128)}) custom-call(bf16[1024,512]{1,0:T(8,128)(2,1)S(1)} %copy-done, bf16[256,640]{1,0:T(8,128)(2,1)S(1)} %bitcast.8, f32[2,1024]{1,0:T(2,128)S(1)} %pad_maximum_fusion.terms_ref), custom_call_target="tpu_custom_call" | custom-call | tf_op jit(solution)/shard_map/pallas_call | solution.py:69
  22.9 9.4 %all_to_all.17 = f32[32,1,16]{2,1,0:T(1,128)S(1)} all-to-all(f32[32,1,16]{2,1,0:T(1,128)S(1)} %bitcast.9), channel_id=1, replica_groups=mesh['group'=8,'blk'=4] {'group','blk'}, dimensions={0} | all-to-all | bytes 4096 | tf_op jit(solution)/shard_map/all_to_all | solution.py:81
  32.3 0.1 fusion
  32.4 0.0 copy-done.2
  32.4 0.5 %subtract_multiply_fusion = f32[8]{0:T(128)} fusion(f32[8]{0:T(128)S(1)} %copy-done.2, f32[8]{0:T(128)S(1)} %slice_reduce_fusion, f32[8]{0:T(128)S(1)} %fusion), kind=kLoop, calls=%fused_computation.8 | loop fusion | flops 24 | bytes 128 | tf_op jit(solution)/shard_map/mul | solution.py:86
  (4 shorter events, 0.0 us)
Async XLA Ops:
  0.6 10.5 %copy-start.1 = (f32[1024]{0:T(1024)S(1)}, f32[1024]{0:T(1024)}, u32[]{:S(2)}) copy-start(f32[1024]{0:T(1024)} %param.8) | copy-start | bytes 12292
  0.7 20.9 %copy-start = (bf16[1024,512]{1,0:T(8,128)(2,1)S(1)}, bf16[1024,512]{1,0:T(8,128)(2,1)}, u32[]{:S(2)}) copy-start(bf16[1024,512]{1,0:T(8,128)(2,1)} %src_ref.1) | copy-start | bytes 3145732
  2.3 19.3 %all-to-all-start = ((bf16[32,8,640]{2,1,0:T(8,128)(2,1)}), bf16[32,8,640]{2,1,0:T(8,128)(2,1)S(1)}, u32[]{:S(2)}, u32[]{:S(2)}) async-start(bf16[32,8,640]{2,1,0:T(8,128)(2,1)} %broadcast_in_dim.11), calls=%async_computation | async-start | bytes 655360 | tf_op jit(solution)/shard_map/all_to_all | solution.py:63
  9.6 22.8 %copy-start.2 = (f32[8]{0:T(128)S(1)}, f32[8]{0:T(128)}, u32[]{:S(2)}) copy-start(f32[8]{0:T(128)} %param.9) | copy-start | bytes 100

commit v19 on v18

--- a/solution.py
+++ b/solution.py
@@ -9,6 +9,20 @@
 
 epsilon = 0.05
 AXES = ("group", "blk")
+
+
+def spread_out(features, rows_ref, pots_ref, out_ref):
+    rows = rows_ref.shape[0]
+    diagonal = lax.broadcasted_iota(jnp.int32, (rows, rows), 0) == lax.broadcasted_iota(
+        jnp.int32, (rows, rows), 1
+    )
+    pots = pots_ref[...].astype(jnp.float32)
+    column = jnp.sum(jnp.where(diagonal, pots, 0.0), 1, keepdims=True)
+    lanes = jnp.broadcast_to(column, (rows, 128)).astype(out_ref.dtype)
+    block = rows_ref[...]
+    for k in range(out_ref.shape[0]):
+        out_ref[k, :, 0:features] = block
+        out_ref[k, :, features:features + 128] = lanes
 
 
 def tail(features, factor, width, src_ref, rows_ref, terms_ref, col_ref, pot_ref):
@@ -44,14 +58,6 @@
     features = sources.shape[1]
     factor = 2.0 / (features * epsilon)
 
-    lane = lax.broadcasted_iota(jnp.int32, (targets.shape[0], features + 128), 1)
-    held = lax.optimization_barrier(
-        jnp.where(
-            lane < features,
-            jnp.pad(targets, ((0, 0), (0, 128))),
-            target_potential[:, None],
-        )
-    )
     source_terms = lax.optimization_barrier(
         jnp.stack(
             [
@@ -60,12 +66,19 @@
             ]
         )
     )
-    everything = lax.all_to_all(
-        jnp.broadcast_to(held[None], (count,) + held.shape), AXES, 0, 0, tiled=True
-    ).reshape(count * held.shape[0], held.shape[1])
+    vmem = pl.BlockSpec(memory_space=pltpu.VMEM)
+    outgoing = pl.pallas_call(
+        functools.partial(spread_out, features),
+        out_shape=jax.ShapeDtypeStruct((count, targets.shape[0], features + 128), targets.dtype),
+        in_specs=[vmem] * 2,
+        out_specs=vmem,
+        compiler_params=pltpu.CompilerParams(vmem_limit_bytes=8 * 1024 * 1024),
+    )(targets, target_potential.reshape(1, -1))
+    everything = lax.all_to_all(outgoing, AXES, 0, 0, tiled=True).reshape(
+        count * targets.shape[0], features + 128
+    )
 
     width = targets.shape[0]
-    vmem = pl.BlockSpec(memory_space=pltpu.VMEM)
     columns, source_potential = pl.pallas_call(
         functools.partial(tail, features, factor, width),
         out_shape=(

time: 33.2 us -> 33.9 us (1.021)
  other arithmetic: 3.02 us -> 2.15 us
  Pallas kernels: 1.37 us -> 2.16 us
  local copies, waits for them, and re-layouts: 0.75 us -> 1.45 us
    unnamed x6 -> x10, local copies, waits for them, and re-layouts: 0.02 us -> 1.45 us
    select_n x1 -> x0, other arithmetic: 0.86 us -> none  [per_device(): jnp.where(lane < features, jnp.pad(targets, ((0, 0), (0, 128))), target_p...]
    pallas_call x0 -> x1, Pallas kernels: none -> 0.8 us  [per_device(): pl.pallas_call(functools.partial(spread_out, features), out_shape=jax.Sha...]
    broadcast_in_dim x1 -> x0, local copies, waits for them, and re-layouts: 0.74 us -> none  [per_device(): jnp.broadcast_to(held[None], (count,) + held.shape)]
where the time goes in v19:
time: 33.9 us; the launch traced here: 33.6 us
  waiting for transfers between devices  10.4 us (31%)
  blocking collectives  9.37 us (28%)
  starting transfers between devices  7.3 us (22%)
  Pallas kernels  2.16 us (6%)
  other arithmetic  2.15 us (6%)
  local copies, waits for them, and re-layouts  1.45 us (4%)
  between operations  0.7 us (2%)
    all_to_all x1, waiting for transfers between devices, per_device(): lax.all_to_all(outgoing, AXES, 0, 0, tiled=True)  10.4 us
    all_to_all x1, blocking collectives, per_device(): part = lax.all_to_all(columns, AXES, 0, 0, tiled=True)  9.37 us
    all_to_all x1, starting transfers between devices, per_device(): lax.all_to_all(outgoing, AXES, 0, 0, tiled=True)  7.3 us
    reduce_sum x1, other arithmetic, per_device(): jnp.sum(jnp.square(sources.astype(jnp.float32)), 1) / features  1.5 us
    unnamed x10, local copies, waits for them, and re-layouts  1.45 us
    pallas_call x1, Pallas kernels, per_device(): pl.pallas_call(functools.partial(tail, features, factor, width), out_shap...  1.37 us
    pallas_call x1, Pallas kernels, per_device(): pl.pallas_call(functools.partial(spread_out, features), out_shape=jax.Sha...  0.8 us
  transfers between devices with their start and end apart: 1, of which 1 were waited for; matrix products, arithmetic and copies ran while one was open for 5% of the time, Pallas kernels for 0%

profile of v19, /device:TPU:0, one launch (start us, length us, event | category | flops | bytes accessed | tf_op | source)
XLA Modules:
  0.0 33.6 jit_solution(7882348319211147718)
XLA Ops:
  0.6 0.0 copy-start
  0.6 0.0 copy-start.1
  0.7 0.8 %copy-done.1 = bf16[8,512]{1,0:T(8,128)(2,1)S(1)} copy-done((bf16[8,512]{1,0:T(8,128)(2,1)S(1)}, bf16[8,512]{1,0:T(8,128)(2,1)}, u32[]{:S(2)}) %copy-start.1) | copy-done | bytes 8216
  1.4 0.0 copy-start.2
  1.4 0.7 %copy-done.2 = bf16[8]{0:T(256)(128)(2,1)S(1)} copy-done((bf16[8]{0:T(256)(128)(2,1)S(1)}, bf16[8]{0:T(256)(128)(2,1)}, u32[]{:S(2)}) %copy-start.2) | copy-done | bytes 40
  2.1 0.0 copy-start.3
  2.1 0.8 %shard_map.68 = bf16[32,8,640]{2,1,0:T(8,128)(2,1)} custom-call(bf16[8,512]{1,0:T(8,128)(2,1)S(1)} %copy-done.1, bf16[1,8]{1,0:T(2,128)(2,1)S(1)} %bitcast.11), custom_call_target="tpu_custom_call" | custom-call | tf_op jit(solution)/shard_map/pallas_call | solution.py:70
  2.9 7.3 %all-to-all-start = ((bf16[32,8,640]{2,1,0:T(8,128)(2,1)}), bf16[32,8,640]{2,1,0:T(8,128)(2,1)S(1)}, u32[]{:S(2)}, u32[]{:S(2)}) async-start(bf16[32,8,640]{2,1,0:T(8,128)(2,1)} %shard_map.68), calls=%async_computation | async-start | bytes 655360 | tf_op jit(solution)/shard_map/all_to_all | solution.py:77
  10.2 0.0 copy-start.4
  10.2 1.5 %multiply_reduce_fusion = f32[1024]{0:T(1024)S(1)} fusion(bf16[1024,512]{1,0:T(8,128)(2,1)} %src_ref.1), kind=kLoop, calls=%fused_computation | loop fusion | flops 1571840 | bytes 1052672 | tf_op jit(solution)/shard_map/reduce_sum | solution.py:64
  11.7 0.0 copy-done.3
  11.7 10.4 %all-to-all-done = bf16[32,8,640]{2,1,0:T(8,128)(2,1)S(1)} async-done(((bf16[32,8,640]{2,1,0:T(8,128)(2,1)}), bf16[32,8,640]{2,1,0:T(8,128)(2,1)S(1)}, u32[]{:S(2)}, u32[]{:S(2)}) %all-to-all-start) | async-done | bytes 327712 | tf_op jit(solution)/shard_map/all_to_all | solution.py:77
  22.2 0.0 copy-done
  22.2 1.4 %shard_map.69 = (f32[32,16]{1,0:T(8,128)S(1)}, f32[1,1024]{1,0:T(1,128)}) custom-call(bf16[1024,512]{1,0:T(8,128)(2,1)S(1)} %copy-done, bf16[256,640]{1,0:T(8,128)(2,1)S(1)} %bitcast.9, f32[2,1024]{1,0:T(2,128)S(1)} %pad_maximum_fusion.terms_ref), custom_call_target="tpu_custom_call" | custom-call | tf_op jit(solution)/shard_map/pallas_call | solution.py:82
  23.6 9.4 %all_to_all.17 = f32[32,1,16]{2,1,0:T(1,128)S(1)} all-to-all(f32[32,1,16]{2,1,0:T(1,128)S(1)} %bitcast.10), channel_id=1, replica_groups=mesh['group'=8,'blk'=4] {'group','blk'}, dimensions={0} | all-to-all | bytes 4096 | tf_op jit(solution)/shard_map/all_to_all | solution.py:94
  32.9 0.1 fusion
  33.0 0.0 copy-done.4
  33.0 0.5 %subtract_multiply_fusion = f32[8]{0:T(128)} fusion(f32[8]{0:T(128)S(1)} %copy-done.4, f32[8]{0:T(128)S(1)} %slice_reduce_fusion, f32[8]{0:T(128)S(1)} %fusion), kind=kLoop, calls=%fused_computation.6 | loop fusion | flops 24 | bytes 128 | tf_op jit(solution)/shard_map/mul | solution.py:99
  (3 shorter events, 0.0 us)
Async XLA Ops:
  0.6 21.6 %copy-start = (bf16[1024,512]{1,0:T(8,128)(2,1)S(1)}, bf16[1024,512]{1,0:T(8,128)(2,1)}, u32[]{:S(2)}) copy-start(bf16[1024,512]{1,0:T(8,128)(2,1)} %src_ref.1) | copy-start | bytes 3145732
  0.6 0.8 %copy-start.1 = (bf16[8,512]{1,0:T(8,128)(2,1)S(1)}, bf16[8,512]{1,0:T(8,128)(2,1)}, u32[]{:S(2)}) copy-start(bf16[8,512]{1,0:T(8,128)(2,1)} %rows_ref.1) | copy-start | bytes 24580
  1.4 0.7 %copy-start.2 = (bf16[8]{0:T(256)(128)(2,1)S(1)}, bf16[8]{0:T(256)(128)(2,1)}, u32[]{:S(2)}) copy-start(bf16[8]{0:T(256)(128)(2,1)} %param.7) | copy-start | bytes 52
  2.1 9.6 %copy-start.3 = (f32[1024]{0:T(1024)S(1)}, f32[1024]{0:T(1024)}, u32[]{:S(2)}) copy-start(f32[1024]{0:T(1024)} %param.8) | copy-start | bytes 12292
  2.9 19.3 %all-to-all-start = ((bf16[32,8,640]{2,1,0:T(8,128)(2,1)}), bf16[32,8,640]{2,1,0:T(8,128)(2,1)S(1)}, u32[]{:S(2)}, u32[]{:S(2)}) async-start(bf16[32,8,640]{2,1,0:T(8,128)(2,1)} %shard_map.68), calls=%async_computation | async-start | bytes 655360 | tf_op jit(solution)/shard_map/all_to_all | solution.py:77
  10.2 22.8 %copy-start.4 = (f32[8]{0:T(128)S(1)}, f32[8]{0:T(128)}, u32[]{:S(2)}) copy-start(f32[8]{0:T(128)} %param.9) | copy-start | bytes 100

commit v20 on v18

--- a/solution.py
+++ b/solution.py
@@ -18,9 +18,7 @@
     offset = pots / epsilon - jnp.sum(jnp.square(rows.astype(jnp.float32)), 1, keepdims=True) / (
         features * epsilon
     )
-    logits = lax.dot_general(
-        rows, src_ref[...], (((1,), (1,)), ((), ())), preferred_element_type=jnp.float32
-    ) * factor + offset
+    logits = jnp.dot(rows, src_ref[...], preferred_element_type=jnp.float32) * factor + offset
     row_max = jnp.max(logits, 0, keepdims=True)
     row_lse = row_max + jnp.log(jnp.sum(jnp.exp(logits - row_max), 0, keepdims=True))
     dual = terms_ref[1:2, :] - row_lse
@@ -75,7 +73,7 @@
         in_specs=[vmem] * 3,
         out_specs=(vmem, vmem),
         compiler_params=pltpu.CompilerParams(vmem_limit_bytes=24 * 1024 * 1024),
-    )(sources, everything, source_terms)
+    )(sources.T, everything, source_terms)
     source_potential = source_potential.reshape(-1)
 
     part = lax.all_to_all(columns, AXES, 0, 0, tiled=True)

time: 33.2 us -> 33.2 us (level)
  local copies, waits for them, and re-layouts: 0.75 us -> 2.71 us
  other arithmetic: 3.02 us -> 1.7 us
  waiting for transfers between devices: 10.4 us -> 9.68 us
    unnamed x6 -> x7, local copies, waits for them, and re-layouts: 0.02 us -> 1.97 us
    reduce_sum x1, other arithmetic: 1.5 us -> 0.27 us  [per_device(): jnp.sum(jnp.square(sources.astype(jnp.float32)), 1) / features]
    all_to_all x1, waiting for transfers between devices: 10.4 us -> 9.68 us  [per_device(): lax.all_to_all(jnp.broadcast_to(held[None], (count,) + held.shape), AXES,...]
  transfers between devices with their start and end apart: 1 -> 1, of which waited for: 1 -> 1; matrix products, arithmetic and copies ran while one was open for 5% -> 6% of each run, Pallas kernels for 0% -> 0%
where the time goes in v20:
time: 33.2 us; the launch traced here: 32.8 us
  waiting for transfers between devices  9.68 us (29%)
  blocking collectives  9.37 us (28%)
  starting transfers between devices  7.3 us (22%)
  local copies, waits for them, and re-layouts  2.71 us (8%)
  other arithmetic  1.7 us (5%)
  Pallas kernels  1.33 us (4%)
  between operations  0.7 us (2%)
    all_to_all x1, waiting for transfers between devices, per_device(): lax.all_to_all(jnp.broadcast_to(held[None], (count,) + held.shape), AXES,...  9.68 us
    all_to_all x1, blocking collectives, per_device(): part = lax.all_to_all(columns, AXES, 0, 0, tiled=True)  9.37 us
    all_to_all x1, starting transfers between devices, per_device(): lax.all_to_all(jnp.broadcast_to(held[None], (count,) + held.shape), AXES,...  7.3 us
    unnamed x7, local copies, waits for them, and re-layouts  1.97 us
    pallas_call x1, Pallas kernels, per_device(): pl.pallas_call(functools.partial(tail, features, factor, width), out_shap...  1.33 us
    select_n x1, other arithmetic, per_device(): jnp.where(lane < features, jnp.pad(targets, ((0, 0), (0, 128))), target_p...  0.77 us
    broadcast_in_dim x1, local copies, waits for them, and re-layouts, per_device(): jnp.broadcast_to(held[None], (count,) + held.shape)  0.74 us
  transfers between devices with their start and end apart: 1, of which 1 were waited for; matrix products, arithmetic and copies ran while one was open for 6% of the time, Pallas kernels for 0%

profile of v20, /device:TPU:0, one launch (start us, length us, event | category | flops | bytes accessed | tf_op | source)
XLA Modules:
  0.0 32.8 jit_solution(3992486084485523148)
XLA Ops:
  0.6 0.8 %pad_select_fusion = bf16[8,640]{1,0:T(8,128)(2,1)S(1)} fusion(bf16[8,512]{1,0:T(8,128)(2,1)} %param.6, pred[640]{0:T(1024)(128)(4,1)S(1)} %iota_compare_fusion, bf16[8]{0:T(256)(128)(2,1)} %param.7), kind=kLoop, calls=%fused_computation.4 | loop fusion | flops 5120 | bytes 19088 | tf_op jit(solution)/shard_map/jit(_where)/select_n | solution.py:47
  1.4 0.7 %broadcast_in_dim.11 = bf16[32,8,640]{2,1,0:T(8,128)(2,1)} broadcast(bf16[8,640]{1,0:T(8,128)(2,1)S(1)} %pad_select_fusion), dimensions={1,2} | broadcast | bytes 337920 | tf_op jit(solution)/shard_map/broadcast_in_dim | solution.py:62
  2.2 7.3 %all-to-all-start = ((bf16[32,8,640]{2,1,0:T(8,128)(2,1)}), bf16[32,8,640]{2,1,0:T(8,128)(2,1)S(1)}, u32[]{:S(2)}, u32[]{:S(2)}) async-start(bf16[32,8,640]{2,1,0:T(8,128)(2,1)} %broadcast_in_dim.11), calls=%async_computation | async-start | bytes 655360 | tf_op jit(solution)/shard_map/all_to_all | solution.py:61
  9.5 0.0 copy-start
  9.5 1.6 %copy.8 = bf16[1024,512]{0,1:T(8,128)(2,1)S(1)} copy(bf16[1024,512]{1,0:T(8,128)(2,1)} %param.5) | data formatting | bytes 2097152 | tf_op args[0]
  11.1 0.0 copy-done
  11.1 0.0 copy-start.1
  11.1 0.0 copy-start.2
  11.1 0.3 multiply_reduce_fusion
  11.4 0.4 %copy-done.1 = f32[1024]{0:T(1024)S(1)} copy-done((f32[1024]{0:T(1024)S(1)}, f32[1024]{0:T(1024)}, u32[]{:S(2)}) %copy-start.1) | copy-done | bytes 4120
  11.8 9.7 %all-to-all-done = bf16[32,8,640]{2,1,0:T(8,128)(2,1)S(1)} async-done(((bf16[32,8,640]{2,1,0:T(8,128)(2,1)}), bf16[32,8,640]{2,1,0:T(8,128)(2,1)S(1)}, u32[]{:S(2)}, u32[]{:S(2)}) %all-to-all-start) | async-done | bytes 327712 | tf_op jit(solution)/shard_map/all_to_all | solution.py:61
  21.4 1.3 %shard_map.68 = (f32[32,16]{1,0:T(8,128)S(1)}, f32[1,1024]{1,0:T(1,128)}) custom-call(bf16[512,1024]{1,0:T(8,128)(2,1)S(1)} %bitcast.9, bf16[256,640]{1,0:T(8,128)(2,1)S(1)} %bitcast.10, f32[2,1024]{1,0:T(2,128)S(1)} %pad_maximum_fusion.terms_ref), custom_call_target="tpu_custom_call" | custom-call | tf_op jit(solution)/shard_map/pallas_call | solution.py:67
  22.8 9.4 %all_to_all.17 = f32[32,1,16]{2,1,0:T(1,128)S(1)} all-to-all(f32[32,1,16]{2,1,0:T(1,128)S(1)} %bitcast.11), channel_id=1, replica_groups=mesh['group'=8,'blk'=4] {'group','blk'}, dimensions={0} | all-to-all | bytes 4096 | tf_op jit(solution)/shard_map/all_to_all | solution.py:79
  32.2 0.1 fusion
  32.3 0.0 copy-done.2
  32.3 0.5 %subtract_multiply_fusion = f32[8]{0:T(128)} fusion(f32[8]{0:T(128)S(1)} %copy-done.2, f32[8]{0:T(128)S(1)} %slice_reduce_fusion, f32[8]{0:T(128)S(1)} %fusion), kind=kLoop, calls=%fused_computation.8 | loop fusion | flops 24 | bytes 128 | tf_op jit(solution)/shard_map/mul | solution.py:84
  (4 shorter events, 0.0 us)
Async XLA Ops:
  2.2 19.3 %all-to-all-start = ((bf16[32,8,640]{2,1,0:T(8,128)(2,1)}), bf16[32,8,640]{2,1,0:T(8,128)(2,1)S(1)}, u32[]{:S(2)}, u32[]{:S(2)}) async-start(bf16[32,8,640]{2,1,0:T(8,128)(2,1)} %broadcast_in_dim.11), calls=%async_computation | async-start | bytes 655360 | tf_op jit(solution)/shard_map/all_to_all | solution.py:61
  9.5 1.6 %copy-start = (bf16[1024,512]{1,0:T(8,128)(2,1)S(1)}, bf16[1024,512]{1,0:T(8,128)(2,1)}, u32[]{:S(2)}) copy-start(bf16[1024,512]{1,0:T(8,128)(2,1)} %param.5) | copy-start | bytes 3145732
  11.1 0.7 %copy-start.1 = (f32[1024]{0:T(1024)S(1)}, f32[1024]{0:T(1024)}, u32[]{:S(2)}) copy-start(f32[1024]{0:T(1024)} %param.8) | copy-start | bytes 12292
  11.1 21.2 %copy-start.2 = (f32[8]{0:T(128)S(1)}, f32[8]{0:T(128)}, u32[]{:S(2)}) copy-start(f32[8]{0:T(128)} %param.9) | copy-start | bytes 100

commit v21 on v20

--- a/solution.py
+++ b/solution.py
@@ -11,7 +11,7 @@
 AXES = ("group", "blk")
 
 
-def tail(features, factor, width, src_ref, rows_ref, terms_ref, col_ref, pot_ref):
+def tail(features, factor, width, src_ref, rows_ref, terms_ref, col_ref, dual_ref):
     block = rows_ref[...]
     rows = block[:, :features]
     pots = block[:, features:features + 1].astype(jnp.float32)
@@ -22,7 +22,7 @@
     row_max = jnp.max(logits, 0, keepdims=True)
     row_lse = row_max + jnp.log(jnp.sum(jnp.exp(logits - row_max), 0, keepdims=True))
     dual = terms_ref[1:2, :] - row_lse
-    pot_ref[...] = epsilon * dual + terms_ref[0:1, :]
+    dual_ref[...] = dual
     column = logits - pots / epsilon + dual
     col_max = jnp.max(column, 1, keepdims=True)
     col_sum = jnp.sum(jnp.exp(column - col_max), 1, keepdims=True)
@@ -64,7 +64,7 @@
 
     width = targets.shape[0]
     vmem = pl.BlockSpec(memory_space=pltpu.VMEM)
-    columns, source_potential = pl.pallas_call(
+    columns, source_dual = pl.pallas_call(
         functools.partial(tail, features, factor, width),
         out_shape=(
             jax.ShapeDtypeStruct((count, 2 * width), jnp.float32),
@@ -74,7 +74,7 @@
         out_specs=(vmem, vmem),
         compiler_params=pltpu.CompilerParams(vmem_limit_bytes=24 * 1024 * 1024),
     )(sources.T, everything, source_terms)
-    source_potential = source_potential.reshape(-1)
+    source_potential = epsilon * source_dual.reshape(-1) + source_terms[0]
 
     part = lax.all_to_all(columns, AXES, 0, 0, tiled=True)
     owned_max = jnp.max(part[:, :width], 0)

time: 33.2 us -> 33.9 us (1.021)
  blocking collectives: 9.37 us -> 0 us
  waiting for transfers between devices: 9.68 us -> 16.2 us
  starting transfers between devices: 7.3 us -> 9.86 us
  other arithmetic: 1.7 us -> 2.3 us
  Pallas kernels: 1.33 us -> 1.75 us
    all_to_all x1 -> x0, blocking collectives: 9.37 us -> none  [per_device(): part = lax.all_to_all(columns, AXES, 0, 0, tiled=True)]
    all_to_all x0 -> x1, waiting for transfers between devices: none -> 6.54 us  [per_device(): part = lax.all_to_all(columns, AXES, 0, 0, tiled=True)]
    all_to_all x0 -> x1, starting transfers between devices: none -> 2.57 us  [per_device(): part = lax.all_to_all(columns, AXES, 0, 0, tiled=True)]
    add x0 -> x1, other arithmetic: none -> 0.6 us  [per_device(): source_potential = epsilon * source_dual.reshape(-1) + source_terms[0]]
    pallas_call x1, Pallas kernels: 1.33 us -> 1.75 us  [per_device(): pl.pallas_call(functools.partial(tail, features, factor, width), out_shap...]
  transfers between devices with their start and end apart: 1 -> 2, of which waited for: 1 -> 2; matrix products, arithmetic and copies ran while one was open for 6% -> 7% of each run, Pallas kernels for 0% -> 0%
where the time goes in v21:
time: 33.9 us; the launch traced here: 33.6 us
  waiting for transfers between devices  16.2 us (48%)
  starting transfers between devices  9.86 us (29%)
  local copies, waits for them, and re-layouts  2.71 us (8%)
  other arithmetic  2.3 us (7%)
  Pallas kernels  1.75 us (5%)
  between operations  0.71 us (2%)
    all_to_all x1, waiting for transfers between devices, per_device(): lax.all_to_all(jnp.broadcast_to(held[None], (count,) + held.shape), AXES,...  9.68 us
    all_to_all x1, starting transfers between devices, per_device(): lax.all_to_all(jnp.broadcast_to(held[None], (count,) + held.shape), AXES,...  7.3 us
    all_to_all x1, waiting for transfers between devices, per_device(): part = lax.all_to_all(columns, AXES, 0, 0, tiled=True)  6.54 us
    all_to_all x1, starting transfers between devices, per_device(): part = lax.all_to_all(columns, AXES, 0, 0, tiled=True)  2.57 us
    unnamed x7, local copies, waits for them, and re-layouts  1.97 us
    pallas_call x1, Pallas kernels, per_device(): pl.pallas_call(functools.partial(tail, features, factor, width), out_shap...  1.75 us
    select_n x1, other arithmetic, per_device(): jnp.where(lane < features, jnp.pad(targets, ((0, 0), (0, 128))), target_p...  0.77 us
    broadcast_in_dim x1, local copies, waits for them, and re-layouts, per_device(): jnp.broadcast_to(held[None], (count,) + held.shape)  0.74 us
  transfers between devices with their start and end apart: 2, of which 2 were waited for; matrix products, arithmetic and copies ran while one was open for 7% of the time, Pallas kernels for 0%

profile of v21, /device:TPU:0, one launch (start us, length us, event | category | flops | bytes accessed | tf_op | source)
XLA Modules:
  0.0 33.6 jit_solution(8663691610871541354)
XLA Ops:
  0.6 0.8 %pad_select_fusion = bf16[8,640]{1,0:T(8,128)(2,1)S(1)} fusion(bf16[8,512]{1,0:T(8,128)(2,1)} %param.6, pred[640]{0:T(1024)(128)(4,1)S(1)} %iota_compare_fusion, bf16[8]{0:T(256)(128)(2,1)} %param.7), kind=kLoop, calls=%fused_computation.4 | loop fusion | flops 5120 | bytes 19088 | tf_op jit(solution)/shard_map/jit(_where)/select_n | solution.py:47
  1.4 0.7 %broadcast_in_dim.11 = bf16[32,8,640]{2,1,0:T(8,128)(2,1)} broadcast(bf16[8,640]{1,0:T(8,128)(2,1)S(1)} %pad_select_fusion), dimensions={1,2} | broadcast | bytes 337920 | tf_op jit(solution)/shard_map/broadcast_in_dim | solution.py:62
  2.2 7.3 %all-to-all-start = ((bf16[32,8,640]{2,1,0:T(8,128)(2,1)}), bf16[32,8,640]{2,1,0:T(8,128)(2,1)S(1)}, u32[]{:S(2)}, u32[]{:S(2)}) async-start(bf16[32,8,640]{2,1,0:T(8,128)(2,1)} %broadcast_in_dim.11), calls=%async_computation | async-start | bytes 655360 | tf_op jit(solution)/shard_map/all_to_all | solution.py:61
  9.5 0.0 copy-start
  9.5 1.6 %copy.8 = bf16[1024,512]{0,1:T(8,128)(2,1)S(1)} copy(bf16[1024,512]{1,0:T(8,128)(2,1)} %param.5) | data formatting | bytes 2097152 | tf_op args[0]
  11.1 0.0 copy-done
  11.1 0.0 copy-start.1
  11.1 0.0 copy-start.2
  11.1 0.3 multiply_reduce_fusion
  11.4 0.4 %copy-done.1 = f32[1024]{0:T(1024)S(1)} copy-done((f32[1024]{0:T(1024)S(1)}, f32[1024]{0:T(1024)}, u32[]{:S(2)}) %copy-start.1) | copy-done | bytes 4120
  11.8 9.7 %all-to-all-done = bf16[32,8,640]{2,1,0:T(8,128)(2,1)S(1)} async-done(((bf16[32,8,640]{2,1,0:T(8,128)(2,1)}), bf16[32,8,640]{2,1,0:T(8,128)(2,1)S(1)}, u32[]{:S(2)}, u32[]{:S(2)}) %all-to-all-start) | async-done | bytes 327712 | tf_op jit(solution)/shard_map/all_to_all | solution.py:61
  21.4 1.8 %shard_map.68 = (f32[32,16]{1,0:T(8,128)}, f32[1,1024]{1,0:T(1,128)S(1)}) custom-call(bf16[512,1024]{1,0:T(8,128)(2,1)S(1)} %bitcast.9, bf16[256,640]{1,0:T(8,128)(2,1)S(1)} %bitcast.10, f32[2,1024]{1,0:T(2,128)S(1)} %pad_maximum_fusion.terms_ref), custom_call_target="tpu_custom_call" | custom-call | tf_op jit(solution)/shard_map/pallas_call | solution.py:67
  23.2 2.6 %all-to-all-start.1 = ((f32[32,1,16]{2,1,0:T(1,128)}), f32[32,1,16]{2,1,0:T(1,128)S(1)}, u32[]{:S(2)}, u32[]{:S(2)}) async-start(f32[32,1,16]{2,1,0:T(1,128)} %bitcast.6), calls=%async_computation.1 | async-start | bytes 32768 | tf_op jit(solution)/shard_map/all_to_all | solution.py:79
  25.8 0.6 %slice_add_fusion = f32[1,1024]{1,0:T(1,128)} fusion(f32[2,1024]{1,0:T(2,128)S(1)} %pad_maximum_fusion.terms_ref, f32[1,1024]{1,0:T(1,128)S(1)} %get-tuple-element.4), kind=kLoop, calls=%fused_computation.6 | loop fusion | flops 2048 | bytes 12288 | tf_op jit(solution)/shard_map/add | solution.py:77
  26.4 6.5 %all-to-all-done.1 = f32[32,1,16]{2,1,0:T(1,128)S(1)} async-done(((f32[32,1,16]{2,1,0:T(1,128)}), f32[32,1,16]{2,1,0:T(1,128)S(1)}, u32[]{:S(2)}, u32[]{:S(2)}) %all-to-all-start.1) | async-done | bytes 2080 | tf_op jit(solution)/shard_map/all_to_all | solution.py:79
  32.9 0.1 fusion
  33.0 0.0 copy-done.2
  33.0 0.5 %subtract_multiply_fusion = f32[8]{0:T(128)} fusion(f32[8]{0:T(128)S(1)} %copy-done.2, f32[8]{0:T(128)S(1)} %slice_reduce_fusion, f32[8]{0:T(128)S(1)} %fusion), kind=kLoop, calls=%fused_computation.9 | loop fusion | flops 24 | bytes 128 | tf_op jit(solution)/shard_map/mul | solution.py:84
  (4 shorter events, 0.0 us)
Async XLA Ops:
  2.2 19.3 %all-to-all-start = ((bf16[32,8,640]{2,1,0:T(8,128)(2,1)}), bf16[32,8,640]{2,1,0:T(8,128)(2,1)S(1)}, u32[]{:S(2)}, u32[]{:S(2)}) async-start(bf16[32,8,640]{2,1,0:T(8,128)(2,1)} %broadcast_in_dim.11), calls=%async_computation | async-start | bytes 655360 | tf_op jit(solution)/shard_map/all_to_all | solution.py:61
  9.5 1.6 %copy-start = (bf16[1024,512]{1,0:T(8,128)(2,1)S(1)}, bf16[1024,512]{1,0:T(8,128)(2,1)}, u32[]{:S(2)}) copy-start(bf16[1024,512]{1,0:T(8,128)(2,1)} %param.5) | copy-start | bytes 3145732
  11.1 0.7 %copy-start.1 = (f32[1024]{0:T(1024)S(1)}, f32[1024]{0:T(1024)}, u32[]{:S(2)}) copy-start(f32[1024]{0:T(1024)} %param.8) | copy-start | bytes 12292
  11.1 22.0 %copy-start.2 = (f32[8]{0:T(128)S(1)}, f32[8]{0:T(128)}, u32[]{:S(2)}) copy-start(f32[8]{0:T(128)} %param.9) | copy-start | bytes 100
  23.2 9.7 %all-to-all-start.1 = ((f32[32,1,16]{2,1,0:T(1,128)}), f32[32,1,16]{2,1,0:T(1,128)S(1)}, u32[]{:S(2)}, u32[]{:S(2)}) async-start(f32[32,1,16]{2,1,0:T(1,128)} %bitcast.6), calls=%async_computation.1 | async-start | bytes 32768 | tf_op jit(solution)/shard_map/all_to_all | solution.py:79

commit v22 on v20

--- a/solution.py
+++ b/solution.py
@@ -59,7 +59,7 @@
         )
     )
     everything = lax.all_to_all(
-        jnp.broadcast_to(held[None], (count,) + held.shape), AXES, 0, 0, tiled=True
+        jnp.broadcast_to(held[None], (count,) + held.shape), AXES[::-1], 0, 0, tiled=True
     ).reshape(count * held.shape[0], held.shape[1])
 
     width = targets.shape[0]
@@ -76,7 +76,7 @@
     )(sources.T, everything, source_terms)
     source_potential = source_potential.reshape(-1)
 
-    part = lax.all_to_all(columns, AXES, 0, 0, tiled=True)
+    part = lax.all_to_all(columns, AXES[::-1], 0, 0, tiled=True)
     owned_max = jnp.max(part[:, :width], 0)
     owned_sum = jnp.sum(part[:, width:] * jnp.exp(part[:, :width] - owned_max[None, :]), 0)
     part = (owned_max, owned_sum)

time: 33.2 us -> 33.1 us (level)
  no operation moved by 1% of the time
where the time goes in v22:
time: 33.1 us; the launch traced here: 32.8 us
  waiting for transfers between devices  9.83 us (30%)
  blocking collectives  9.18 us (28%)
  starting transfers between devices  7.3 us (22%)
  local copies, waits for them, and re-layouts  2.71 us (8%)
  other arithmetic  1.7 us (5%)
  Pallas kernels  1.33 us (4%)
  between operations  0.7 us (2%)
    all_to_all x1, waiting for transfers between devices, per_device(): lax.all_to_all(jnp.broadcast_to(held[None], (count,) + held.shape), AXES[...  9.83 us
    all_to_all x1, blocking collectives, per_device(): part = lax.all_to_all(columns, AXES[::-1], 0, 0, tiled=True)  9.18 us
    all_to_all x1, starting transfers between devices, per_device(): lax.all_to_all(jnp.broadcast_to(held[None], (count,) + held.shape), AXES[...  7.3 us
    unnamed x7, local copies, waits for them, and re-layouts  1.97 us
    pallas_call x1, Pallas kernels, per_device(): pl.pallas_call(functools.partial(tail, features, factor, width), out_shap...  1.33 us
    select_n x1, other arithmetic, per_device(): jnp.where(lane < features, jnp.pad(targets, ((0, 0), (0, 128))), target_p...  0.77 us
    broadcast_in_dim x1, local copies, waits for them, and re-layouts, per_device(): jnp.broadcast_to(held[None], (count,) + held.shape)  0.74 us
  transfers between devices with their start and end apart: 1, of which 1 were waited for; matrix products, arithmetic and copies ran while one was open for 6% of the time, Pallas kernels for 0%

profile of v22, /device:TPU:0, one launch (start us, length us, event | category | flops | bytes accessed | tf_op | source)
XLA Modules:
  0.0 32.8 jit_solution(11490987897028384211)
XLA Ops:
  0.6 0.8 %pad_select_fusion = bf16[8,640]{1,0:T(8,128)(2,1)S(1)} fusion(bf16[8,512]{1,0:T(8,128)(2,1)} %param.6, pred[640]{0:T(1024)(128)(4,1)S(1)} %iota_compare_fusion, bf16[8]{0:T(256)(128)(2,1)} %param.7), kind=kLoop, calls=%fused_computation.4 | loop fusion | flops 5120 | bytes 19088 | tf_op jit(solution)/shard_map/jit(_where)/select_n | solution.py:47
  1.4 0.7 %broadcast_in_dim.11 = bf16[32,8,640]{2,1,0:T(8,128)(2,1)} broadcast(bf16[8,640]{1,0:T(8,128)(2,1)S(1)} %pad_select_fusion), dimensions={1,2} | broadcast | bytes 337920 | tf_op jit(solution)/shard_map/broadcast_in_dim | solution.py:62
  2.2 7.3 %all-to-all-start = ((bf16[32,8,640]{2,1,0:T(8,128)(2,1)}), bf16[32,8,640]{2,1,0:T(8,128)(2,1)S(1)}, u32[]{:S(2)}, u32[]{:S(2)}) async-start(bf16[32,8,640]{2,1,0:T(8,128)(2,1)} %broadcast_in_dim.11), calls=%async_computation | async-start | bytes 655360 | tf_op jit(solution)/shard_map/all_to_all | solution.py:61
  9.5 0.0 copy-start
  9.5 1.6 %copy.8 = bf16[1024,512]{0,1:T(8,128)(2,1)S(1)} copy(bf16[1024,512]{1,0:T(8,128)(2,1)} %param.5) | data formatting | bytes 2097152 | tf_op args[0]
  11.1 0.0 copy-done
  11.1 0.0 copy-start.1
  11.1 0.0 copy-start.2
  11.1 0.3 multiply_reduce_fusion
  11.4 0.4 %copy-done.1 = f32[1024]{0:T(1024)S(1)} copy-done((f32[1024]{0:T(1024)S(1)}, f32[1024]{0:T(1024)}, u32[]{:S(2)}) %copy-start.1) | copy-done | bytes 4120
  11.8 9.8 %all-to-all-done = bf16[32,8,640]{2,1,0:T(8,128)(2,1)S(1)} async-done(((bf16[32,8,640]{2,1,0:T(8,128)(2,1)}), bf16[32,8,640]{2,1,0:T(8,128)(2,1)S(1)}, u32[]{:S(2)}, u32[]{:S(2)}) %all-to-all-start) | async-done | bytes 327712 | tf_op jit(solution)/shard_map/all_to_all | solution.py:61
  21.6 1.3 %shard_map.68 = (f32[32,16]{1,0:T(8,128)S(1)}, f32[1,1024]{1,0:T(1,128)}) custom-call(bf16[512,1024]{1,0:T(8,128)(2,1)S(1)} %bitcast.9, bf16[256,640]{1,0:T(8,128)(2,1)S(1)} %bitcast.10, f32[2,1024]{1,0:T(2,128)S(1)} %pad_maximum_fusion.terms_ref), custom_call_target="tpu_custom_call" | custom-call | tf_op jit(solution)/shard_map/pallas_call | solution.py:67
  22.9 9.2 %all_to_all.17 = f32[32,1,16]{2,1,0:T(1,128)S(1)} all-to-all(f32[32,1,16]{2,1,0:T(1,128)S(1)} %bitcast.11), channel_id=1, replica_groups=mesh['group'=8,'blk'=4] {'blk','group'}, dimensions={0} | all-to-all | bytes 4096 | tf_op jit(solution)/shard_map/all_to_all | solution.py:79
  32.1 0.1 fusion
  32.2 0.0 copy-done.2
  32.2 0.5 %subtract_multiply_fusion = f32[8]{0:T(128)} fusion(f32[8]{0:T(128)S(1)} %copy-done.2, f32[8]{0:T(128)S(1)} %slice_reduce_fusion, f32[8]{0:T(128)S(1)} %fusion), kind=kLoop, calls=%fused_computation.8 | loop fusion | flops 24 | bytes 128 | tf_op jit(solution)/shard_map/mul | solution.py:84
  (4 shorter events, 0.0 us)
Async XLA Ops:
  2.2 19.4 %all-to-all-start = ((bf16[32,8,640]{2,1,0:T(8,128)(2,1)}), bf16[32,8,640]{2,1,0:T(8,128)(2,1)S(1)}, u32[]{:S(2)}, u32[]{:S(2)}) async-start(bf16[32,8,640]{2,1,0:T(8,128)(2,1)} %broadcast_in_dim.11), calls=%async_computation | async-start | bytes 655360 | tf_op jit(solution)/shard_map/all_to_all | solution.py:61
  9.5 1.6 %copy-start = (bf16[1024,512]{1,0:T(8,128)(2,1)S(1)}, bf16[1024,512]{1,0:T(8,128)(2,1)}, u32[]{:S(2)}) copy-start(bf16[1024,512]{1,0:T(8,128)(2,1)} %param.5) | copy-start | bytes 3145732
  11.1 0.7 %copy-start.1 = (f32[1024]{0:T(1024)S(1)}, f32[1024]{0:T(1024)}, u32[]{:S(2)}) copy-start(f32[1024]{0:T(1024)} %param.8) | copy-start | bytes 12292
  11.1 21.2 %copy-start.2 = (f32[8]{0:T(128)S(1)}, f32[8]{0:T(128)}, u32[]{:S(2)}) copy-start(f32[8]{0:T(128)} %param.9) | copy-start | bytes 100

commit v23 on v20

--- a/solution.py
+++ b/solution.py
@@ -25,7 +25,11 @@
     pot_ref[...] = epsilon * dual + terms_ref[0:1, :]
     column = logits - pots / epsilon + dual
     col_max = jnp.max(column, 1, keepdims=True)
-    col_sum = jnp.sum(jnp.exp(column - col_max), 1, keepdims=True)
+    ones = jnp.ones((column.shape[1], 128), jnp.float32)
+    col_sum = jnp.dot(
+        jnp.exp(column - col_max), ones, precision=lax.Precision.HIGHEST,
+        preferred_element_type=jnp.float32,
+    )[:, 0:1]
     targets_all = block.shape[0]
     r = lax.broadcasted_iota(jnp.int32, (targets_all, 2 * width), 0)
     c = lax.broadcasted_iota(jnp.int32, (targets_all, 2 * width), 1)

time: 33.2 us -> 34.4 us (1.036)
  Pallas kernels: 1.33 us -> 2.51 us
    pallas_call x1, Pallas kernels: 1.33 us -> 2.51 us  [per_device(): pl.pallas_call(functools.partial(tail, features, factor, width), out_shap...]
  transfers between devices with their start and end apart: 1 -> 1, of which waited for: 1 -> 1; matrix products, arithmetic and copies ran while one was open for 6% -> 5% of each run, Pallas kernels for 0% -> 0%
where the time goes in v23:
time: 34.4 us; the launch traced here: 34 us
  waiting for transfers between devices  9.68 us (28%)
  blocking collectives  9.38 us (27%)
  starting transfers between devices  7.3 us (21%)
  local copies, waits for them, and re-layouts  2.71 us (8%)
  Pallas kernels  2.51 us (7%)
  other arithmetic  1.7 us (5%)
  between operations  0.71 us (2%)
    all_to_all x1, waiting for transfers between devices, per_device(): lax.all_to_all(jnp.broadcast_to(held[None], (count,) + held.shape), AXES,...  9.68 us
    all_to_all x1, blocking collectives, per_device(): part = lax.all_to_all(columns, AXES, 0, 0, tiled=True)  9.38 us
    all_to_all x1, starting transfers between devices, per_device(): lax.all_to_all(jnp.broadcast_to(held[None], (count,) + held.shape), AXES,...  7.3 us
    pallas_call x1, Pallas kernels, per_device(): pl.pallas_call(functools.partial(tail, features, factor, width), out_shap...  2.51 us
    unnamed x7, local copies, waits for them, and re-layouts  1.97 us
    select_n x1, other arithmetic, per_device(): jnp.where(lane < features, jnp.pad(targets, ((0, 0), (0, 128))), target_p...  0.77 us
    broadcast_in_dim x1, local copies, waits for them, and re-layouts, per_device(): jnp.broadcast_to(held[None], (count,) + held.shape)  0.74 us
  transfers between devices with their start and end apart: 1, of which 1 were waited for; matrix products, arithmetic and copies ran while one was open for 5% of the time, Pallas kernels for 0%

profile of v23, /device:TPU:0, one launch (start us, length us, event | category | flops | bytes accessed | tf_op | source)
XLA Modules:
  0.0 34.0 jit_solution(13631256190601871634)
XLA Ops:
  0.6 0.8 %pad_select_fusion = bf16[8,640]{1,0:T(8,128)(2,1)S(1)} fusion(bf16[8,512]{1,0:T(8,128)(2,1)} %param.6, pred[640]{0:T(1024)(128)(4,1)S(1)} %iota_compare_fusion, bf16[8]{0:T(256)(128)(2,1)} %param.7), kind=kLoop, calls=%fused_computation.4 | loop fusion | flops 5120 | bytes 19088 | tf_op jit(solution)/shard_map/jit(_where)/select_n | solution.py:51
  1.4 0.7 %broadcast_in_dim.11 = bf16[32,8,640]{2,1,0:T(8,128)(2,1)} broadcast(bf16[8,640]{1,0:T(8,128)(2,1)S(1)} %pad_select_fusion), dimensions={1,2} | broadcast | bytes 337920 | tf_op jit(solution)/shard_map/broadcast_in_dim | solution.py:66
  2.2 7.3 %all-to-all-start = ((bf16[32,8,640]{2,1,0:T(8,128)(2,1)}), bf16[32,8,640]{2,1,0:T(8,128)(2,1)S(1)}, u32[]{:S(2)}, u32[]{:S(2)}) async-start(bf16[32,8,640]{2,1,0:T(8,128)(2,1)} %broadcast_in_dim.11), calls=%async_computation | async-start | bytes 655360 | tf_op jit(solution)/shard_map/all_to_all | solution.py:65
  9.5 0.0 copy-start
  9.5 1.6 %copy.8 = bf16[1024,512]{0,1:T(8,128)(2,1)S(1)} copy(bf16[1024,512]{1,0:T(8,128)(2,1)} %param.5) | data formatting | bytes 2097152 | tf_op args[0]
  11.1 0.0 copy-done
  11.1 0.0 copy-start.1
  11.1 0.0 copy-start.2
  11.1 0.3 multiply_reduce_fusion
  11.4 0.4 %copy-done.1 = f32[1024]{0:T(1024)S(1)} copy-done((f32[1024]{0:T(1024)S(1)}, f32[1024]{0:T(1024)}, u32[]{:S(2)}) %copy-start.1) | copy-done | bytes 4120
  11.8 9.7 %all-to-all-done = bf16[32,8,640]{2,1,0:T(8,128)(2,1)S(1)} async-done(((bf16[32,8,640]{2,1,0:T(8,128)(2,1)}), bf16[32,8,640]{2,1,0:T(8,128)(2,1)S(1)}, u32[]{:S(2)}, u32[]{:S(2)}) %all-to-all-start) | async-done | bytes 327712 | tf_op jit(solution)/shard_map/all_to_all | solution.py:65
  21.4 2.5 %shard_map.68 = (f32[32,16]{1,0:T(8,128)S(1)}, f32[1,1024]{1,0:T(1,128)}) custom-call(bf16[512,1024]{1,0:T(8,128)(2,1)S(1)} %bitcast.9, bf16[256,640]{1,0:T(8,128)(2,1)S(1)} %bitcast.10, f32[2,1024]{1,0:T(2,128)S(1)} %pad_maximum_fusion.terms_ref), custom_call_target="tpu_custom_call" | custom-call | tf_op jit(solution)/shard_map/pallas_call | solution.py:71
  24.0 9.4 %all_to_all.17 = f32[32,1,16]{2,1,0:T(1,128)S(1)} all-to-all(f32[32,1,16]{2,1,0:T(1,128)S(1)} %bitcast.11), channel_id=1, replica_groups=mesh['group'=8,'blk'=4] {'group','blk'}, dimensions={0} | all-to-all | bytes 4096 | tf_op jit(solution)/shard_map/all_to_all | solution.py:83
  33.4 0.1 fusion
  33.5 0.0 copy-done.2
  33.5 0.5 %subtract_multiply_fusion = f32[8]{0:T(128)} fusion(f32[8]{0:T(128)S(1)} %copy-done.2, f32[8]{0:T(128)S(1)} %slice_reduce_fusion, f32[8]{0:T(128)S(1)} %fusion), kind=kLoop, calls=%fused_computation.8 | loop fusion | flops 24 | bytes 128 | tf_op jit(solution)/shard_map/mul | solution.py:88
  (4 shorter events, 0.0 us)
Async XLA Ops:
  2.2 19.3 %all-to-all-start = ((bf16[32,8,640]{2,1,0:T(8,128)(2,1)}), bf16[32,8,640]{2,1,0:T(8,128)(2,1)S(1)}, u32[]{:S(2)}, u32[]{:S(2)}) async-start(bf16[32,8,640]{2,1,0:T(8,128)(2,1)} %broadcast_in_dim.11), calls=%async_computation | async-start | bytes 655360 | tf_op jit(solution)/shard_map/all_to_all | solution.py:65
  9.5 1.6 %copy-start = (bf16[1024,512]{1,0:T(8,128)(2,1)S(1)}, bf16[1024,512]{1,0:T(8,128)(2,1)}, u32[]{:S(2)}) copy-start(bf16[1024,512]{1,0:T(8,128)(2,1)} %param.5) | copy-start | bytes 3145732
  11.1 0.7 %copy-start.1 = (f32[1024]{0:T(1024)S(1)}, f32[1024]{0:T(1024)}, u32[]{:S(2)}) copy-start(f32[1024]{0:T(1024)} %param.8) | copy-start | bytes 12292
  11.1 22.4 %copy-start.2 = (f32[8]{0:T(128)S(1)}, f32[8]{0:T(128)}, u32[]{:S(2)}) copy-start(f32[8]{0:T(128)} %param.9) | copy-start | bytes 100

commit v24 on v20

--- a/solution.py
+++ b/solution.py
@@ -34,7 +34,7 @@
     members = lax.broadcasted_iota(jnp.int32, (targets_all // width, targets_all), 1) // width
     gather = (owners == members).astype(jnp.float32)
     col_ref[...] = jnp.dot(
-        gather, spread, precision=lax.Precision.HIGHEST, preferred_element_type=jnp.float32
+        gather, spread, precision=lax.Precision.HIGH, preferred_element_type=jnp.float32
     )
 
 def per_device(sources, targets, target_potential, log_source_mass, log_target_mass):

time: 33.2 us -> 33.2 us (level)
  no operation moved by 1% of the time
where the time goes in v24:
time: 33.2 us; the launch traced here: 32.8 us
  waiting for transfers between devices  9.68 us (29%)
  blocking collectives  9.37 us (28%)
  starting transfers between devices  7.3 us (22%)
  local copies, waits for them, and re-layouts  2.71 us (8%)
  other arithmetic  1.7 us (5%)
  Pallas kernels  1.33 us (4%)
  between operations  0.7 us (2%)
    all_to_all x1, waiting for transfers between devices, per_device(): lax.all_to_all(jnp.broadcast_to(held[None], (count,) + held.shape), AXES,...  9.68 us
    all_to_all x1, blocking collectives, per_device(): part = lax.all_to_all(columns, AXES, 0, 0, tiled=True)  9.37 us
    all_to_all x1, starting transfers between devices, per_device(): lax.all_to_all(jnp.broadcast_to(held[None], (count,) + held.shape), AXES,...  7.3 us
    unnamed x7, local copies, waits for them, and re-layouts  1.97 us
    pallas_call x1, Pallas kernels, per_device(): pl.pallas_call(functools.partial(tail, features, factor, width), out_shap...  1.33 us
    select_n x1, other arithmetic, per_device(): jnp.where(lane < features, jnp.pad(targets, ((0, 0), (0, 128))), target_p...  0.77 us
    broadcast_in_dim x1, local copies, waits for them, and re-layouts, per_device(): jnp.broadcast_to(held[None], (count,) + held.shape)  0.74 us
  transfers between devices with their start and end apart: 1, of which 1 were waited for; matrix products, arithmetic and copies ran while one was open for 6% of the time, Pallas kernels for 0%

profile of v24, /device:TPU:0, one launch (start us, length us, event | category | flops | bytes accessed | tf_op | source)
XLA Modules:
  0.0 32.8 jit_solution(12115251916303716039)
XLA Ops:
  0.6 0.8 %pad_select_fusion = bf16[8,640]{1,0:T(8,128)(2,1)S(1)} fusion(bf16[8,512]{1,0:T(8,128)(2,1)} %param.6, pred[640]{0:T(1024)(128)(4,1)S(1)} %iota_compare_fusion, bf16[8]{0:T(256)(128)(2,1)} %param.7), kind=kLoop, calls=%fused_computation.4 | loop fusion | flops 5120 | bytes 19088 | tf_op jit(solution)/shard_map/jit(_where)/select_n | solution.py:47
  1.4 0.7 %broadcast_in_dim.11 = bf16[32,8,640]{2,1,0:T(8,128)(2,1)} broadcast(bf16[8,640]{1,0:T(8,128)(2,1)S(1)} %pad_select_fusion), dimensions={1,2} | broadcast | bytes 337920 | tf_op jit(solution)/shard_map/broadcast_in_dim | solution.py:62
  2.2 7.3 %all-to-all-start = ((bf16[32,8,640]{2,1,0:T(8,128)(2,1)}), bf16[32,8,640]{2,1,0:T(8,128)(2,1)S(1)}, u32[]{:S(2)}, u32[]{:S(2)}) async-start(bf16[32,8,640]{2,1,0:T(8,128)(2,1)} %broadcast_in_dim.11), calls=%async_computation | async-start | bytes 655360 | tf_op jit(solution)/shard_map/all_to_all | solution.py:61
  9.5 0.0 copy-start
  9.5 1.6 %copy.8 = bf16[1024,512]{0,1:T(8,128)(2,1)S(1)} copy(bf16[1024,512]{1,0:T(8,128)(2,1)} %param.5) | data formatting | bytes 2097152 | tf_op args[0]
  11.1 0.0 copy-done
  11.1 0.0 copy-start.1
  11.1 0.0 copy-start.2
  11.1 0.3 multiply_reduce_fusion
  11.4 0.4 %copy-done.1 = f32[1024]{0:T(1024)S(1)} copy-done((f32[1024]{0:T(1024)S(1)}, f32[1024]{0:T(1024)}, u32[]{:S(2)}) %copy-start.1) | copy-done | bytes 4120
  11.8 9.7 %all-to-all-done = bf16[32,8,640]{2,1,0:T(8,128)(2,1)S(1)} async-done(((bf16[32,8,640]{2,1,0:T(8,128)(2,1)}), bf16[32,8,640]{2,1,0:T(8,128)(2,1)S(1)}, u32[]{:S(2)}, u32[]{:S(2)}) %all-to-all-start) | async-done | bytes 327712 | tf_op jit(solution)/shard_map/all_to_all | solution.py:61
  21.4 1.3 %shard_map.68 = (f32[32,16]{1,0:T(8,128)S(1)}, f32[1,1024]{1,0:T(1,128)}) custom-call(bf16[512,1024]{1,0:T(8,128)(2,1)S(1)} %bitcast.9, bf16[256,640]{1,0:T(8,128)(2,1)S(1)} %bitcast.10, f32[2,1024]{1,0:T(2,128)S(1)} %pad_maximum_fusion.terms_ref), custom_call_target="tpu_custom_call" | custom-call | tf_op jit(solution)/shard_map/pallas_call | solution.py:67
  22.8 9.4 %all_to_all.17 = f32[32,1,16]{2,1,0:T(1,128)S(1)} all-to-all(f32[32,1,16]{2,1,0:T(1,128)S(1)} %bitcast.11), channel_id=1, replica_groups=mesh['group'=8,'blk'=4] {'group','blk'}, dimensions={0} | all-to-all | bytes 4096 | tf_op jit(solution)/shard_map/all_to_all | solution.py:79
  32.2 0.1 fusion
  32.3 0.0 copy-done.2
  32.3 0.5 %subtract_multiply_fusion = f32[8]{0:T(128)} fusion(f32[8]{0:T(128)S(1)} %copy-done.2, f32[8]{0:T(128)S(1)} %slice_reduce_fusion, f32[8]{0:T(128)S(1)} %fusion), kind=kLoop, calls=%fused_computation.8 | loop fusion | flops 24 | bytes 128 | tf_op jit(solution)/shard_map/mul | solution.py:84
  (4 shorter events, 0.0 us)
Async XLA Ops:
  2.2 19.3 %all-to-all-start = ((bf16[32,8,640]{2,1,0:T(8,128)(2,1)}), bf16[32,8,640]{2,1,0:T(8,128)(2,1)S(1)}, u32[]{:S(2)}, u32[]{:S(2)}) async-start(bf16[32,8,640]{2,1,0:T(8,128)(2,1)} %broadcast_in_dim.11), calls=%async_computation | async-start | bytes 655360 | tf_op jit(solution)/shard_map/all_to_all | solution.py:61
  9.5 1.6 %copy-start = (bf16[1024,512]{1,0:T(8,128)(2,1)S(1)}, bf16[1024,512]{1,0:T(8,128)(2,1)}, u32[]{:S(2)}) copy-start(bf16[1024,512]{1,0:T(8,128)(2,1)} %param.5) | copy-start | bytes 3145732
  11.1 0.7 %copy-start.1 = (f32[1024]{0:T(1024)S(1)}, f32[1024]{0:T(1024)}, u32[]{:S(2)}) copy-start(f32[1024]{0:T(1024)} %param.8) | copy-start | bytes 12292
  11.1 21.2 %copy-start.2 = (f32[8]{0:T(128)S(1)}, f32[8]{0:T(128)}, u32[]{:S(2)}) copy-start(f32[8]{0:T(128)} %param.9) | copy-start | bytes 100
